TPU v7x, 32 devices: a whole 2x2x4 slice. The times are simulated.
32 devices in a mesh: dp: 4 (over y, core), fsdp: 8 (over z, x).
Axes of the slice: x: 2, y: 2, z: 4, core: 2. Of those that a mesh axis runs over, the one named last changes fastest.
Arguments:
- tokens: bfloat16 [32, 1024, 1024], P(('dp', 'fsdp')), may hold values from -6 to 6
- lengths: int32 [32], P(('dp', 'fsdp')), may hold values from 256 to 1024, as said below
- attend_weight: bfloat16 [1024, 3072], P(('dp', 'fsdp')), may hold values from -0.1875 to 0.1875
- project_weight: bfloat16 [1024, 1024], P(('dp', 'fsdp')), may hold values from -0.75 to 0.75
- expand_weight: bfloat16 [1024, 4096], P(('dp', 'fsdp')), may hold values from -0.1875 to 0.1875
- contract_weight: bfloat16 [4096, 1024], P(('dp', 'fsdp')), may hold values from -0.09375 to 0.09375
- inner_bias: bfloat16 [4096], P(('dp', 'fsdp')), may hold values from -3 to 3
- outer_bias: bfloat16 [1024], P(('dp', 'fsdp')), may hold values from -3 to 3
- norm_gain: bfloat16 [1024], P(('dp', 'fsdp')), may hold values from 0.25 to 1.75
- norm_shift: bfloat16 [1024], P(('dp', 'fsdp')), may hold values from -2 to 2
- cotangent: bfloat16 [32, 1024, 1024], P(('dp', 'fsdp')), may hold values from -6 to 6
Outputs:
- output: bfloat16 [32, 1024, 1024], P(('dp', 'fsdp'))
- grad_tokens: bfloat16 [32, 1024, 1024], P(('dp', 'fsdp'))
- grad_attend: float32 [1024, 3072], P(('dp', 'fsdp'))
- grad_project: float32 [1024, 1024], P(('dp', 'fsdp'))
- grad_expand: float32 [1024, 4096], P(('dp', 'fsdp'))
- grad_contract: float32 [4096, 1024], P(('dp', 'fsdp'))
- grad_inner: float32 [4096], P(('dp', 'fsdp'))
- grad_outer: float32 [1024], P(('dp', 'fsdp'))
- grad_gain: float32 [1024], P(('dp', 'fsdp'))
- grad_shift: float32 [1024], P(('dp', 'fsdp'))
Inputs may be any that keep to these rules, and one draw needn't show every extreme that they name: rows 2i and 2i+1 have equal lengths; positions at or past a row's length are padding.
All inputs are finite; a program needn't handle non-finite values.
Results may differ from a plain program's by a relative error of at most 0.0085.
Values may be sent and summed in bfloat16 or wider, within the bound.
No kernel may reach another device: no remote copies, remote signals or barrier semaphores. Data moves between devices by JAX's collectives and lax.ppermute only.
A program may use at most 320 MiB of HBM per device.

v0:
```python
import math

import jax
import jax.numpy as jnp
from jax import lax
from jax.sharding import PartitionSpec as P

HEADS = 16
HEAD_DIM = 64
ROT = 32


epsilon = 1e-05


def layer_norm(rows, gain, shift):
    center = jnp.mean(rows, axis=-1, keepdims=True)
    spread = rows - center
    variance = jnp.mean(spread * spread, axis=-1, keepdims=True)
    return spread * lax.rsqrt(variance + epsilon) * gain + shift


def rotary_tables(length):
    position = jnp.arange(length).astype(jnp.float32)[:, None]
    ladder = jnp.arange(ROT // 2).astype(jnp.float32) * (-2.0 * math.log(10000.0) / ROT)
    angle = position * jnp.exp(ladder)[None, :]
    return (jnp.cos(angle)[:, None, :], jnp.sin(angle)[:, None, :])


def rotate(field, cosine, sine):
    paired = field[..., :ROT].reshape(field.shape[:-1] + (ROT // 2, 2))
    first = paired[..., 0]
    second = paired[..., 1]
    turned = jnp.stack([first * cosine - second * sine, second * cosine + first * sine], axis=-1)
    return jnp.concatenate([turned.reshape(field.shape[:-1] + (ROT,)), field[..., ROT:]], axis=-1)


def allowed_keys(first, count, length, seq_len):
    query_place = first + jnp.arange(count)[:, None]
    key_place = jnp.arange(seq_len)[None, :]
    return (key_place <= query_place) & (key_place < length)


def attend_forward(item):
    query, keys, values, length = item
    seq_len = keys.shape[0]
    block = min(512, seq_len)
    results = []
    logsums = []
    for first in range(0, seq_len, block):
        scores = jnp.einsum(
            "qhd,khd->hqk", query[first : first + block], keys, preferred_element_type=jnp.float32
        ) * HEAD_DIM ** (-0.5)
        masked = jnp.where(allowed_keys(first, block, length, seq_len)[None], scores, -1000000000.0)
        top = jnp.max(masked, axis=-1, keepdims=True)
        weights = jnp.exp(masked - top)
        total = jnp.sum(weights, axis=-1, keepdims=True)
        probs = (weights / total).astype(jnp.bfloat16)
        results.append(
            jnp.einsum("hqk,khd->qhd", probs, values, preferred_element_type=jnp.float32)
        )
        logsums.append(top + jnp.log(total))
    return (jnp.concatenate(results, axis=0).astype(jnp.bfloat16), jnp.concatenate(logsums, axis=1))


def attend_backward(item):
    query, keys, values, upstream, logsum, length = item
    seq_len = keys.shape[0]
    block = min(512, seq_len)
    scale = HEAD_DIM ** (-0.5)
    query_parts = []
    key_grad = jnp.zeros(keys.shape, jnp.float32)
    value_grad = jnp.zeros(values.shape, jnp.float32)
    for first in range(0, seq_len, block):
        query_rows = query[first : first + block]
        upstream_rows = upstream[first : first + block]
        scores = (
            jnp.einsum("qhd,khd->hqk", query_rows, keys, preferred_element_type=jnp.float32) * scale
        )
        masked = jnp.where(allowed_keys(first, block, length, seq_len)[None], scores, -1000000000.0)
        probs = jnp.exp(masked - logsum[:, first : first + block])
        upward = jnp.einsum(
            "qhd,khd->hqk", upstream_rows, values, preferred_element_type=jnp.float32
        )
        inner = jnp.sum(probs * upward, axis=-1, keepdims=True)
        score_grad = (probs * (upward - inner)).astype(jnp.bfloat16)
        query_parts.append(
            jnp.einsum("hqk,khd->qhd", score_grad, keys, preferred_element_type=jnp.float32) * scale
        )
        key_grad = (
            key_grad
            + jnp.einsum("hqk,qhd->khd", score_grad, query_rows, preferred_element_type=jnp.float32)
            * scale
        )
        value_grad = value_grad + jnp.einsum(
            "hqk,qhd->khd",
            probs.astype(jnp.bfloat16),
            upstream_rows,
            preferred_element_type=jnp.float32,
        )
    return (jnp.concatenate(query_parts, axis=0), key_grad, value_grad)


def gelu_tanh(inner):
    return jax.nn.gelu(inner, approximate=True)


def body(
    tokens,
    lengths,
    attend_weight,
    project_weight,
    expand_weight,
    contract_weight,
    inner_bias,
    outer_bias,
    norm_gain,
    norm_shift,
    cotangent,
):
    seq_dev, seq_len, width = tokens.shape
    count = seq_dev * seq_len
    (
        attend_full,
        project_full,
        expand_full,
        contract_full,
        inner_full,
        outer_full,
        gain_full,
        shift_full,
    ) = (
        lax.all_gather(attend_weight, ("dp", "fsdp"), axis=0, tiled=True),
        lax.all_gather(project_weight, ("dp", "fsdp"), axis=0, tiled=True),
        lax.all_gather(expand_weight, ("dp", "fsdp"), axis=0, tiled=True),
        lax.all_gather(contract_weight, ("dp", "fsdp"), axis=0, tiled=True),
        lax.all_gather(inner_bias, ("dp", "fsdp"), axis=0, tiled=True),
        lax.all_gather(outer_bias, ("dp", "fsdp"), axis=0, tiled=True),
        lax.all_gather(norm_gain, ("dp", "fsdp"), axis=0, tiled=True),
        lax.all_gather(norm_shift, ("dp", "fsdp"), axis=0, tiled=True),
    )
    rows = tokens.reshape(count, width).astype(jnp.float32)
    normed, norm_pull = jax.vjp(
        layer_norm, rows, gain_full.astype(jnp.float32), shift_full.astype(jnp.float32)
    )
    normed_low = normed.astype(jnp.bfloat16)
    triple = jnp.dot(normed_low, attend_full, preferred_element_type=jnp.float32).reshape(
        seq_dev, seq_len, 3, HEADS, HEAD_DIM
    )
    cosine, sine = rotary_tables(seq_len)

    def turn(query, keys):
        return (rotate(query, cosine, sine), rotate(keys, cosine, sine))

    (query, keys), turn_pull = jax.vjp(turn, triple[:, :, 0], triple[:, :, 1])
    query_low = query.astype(jnp.bfloat16)
    keys_low = keys.astype(jnp.bfloat16)
    values_low = triple[:, :, 2].astype(jnp.bfloat16)
    attended, logsums = lax.map(attend_forward, (query_low, keys_low, values_low, lengths))
    mixed_low = attended.reshape(count, width)
    hidden = jnp.dot(
        normed_low, expand_full, preferred_element_type=jnp.float32
    ) + inner_full.astype(jnp.float32)
    active, gelu_pull = jax.vjp(gelu_tanh, hidden)
    active_low = active.astype(jnp.bfloat16)
    result = rows + jnp.dot(mixed_low, project_full, preferred_element_type=jnp.float32)
    result = (
        result
        + jnp.dot(active_low, contract_full, preferred_element_type=jnp.float32)
        + outer_full.astype(jnp.float32)
    )
    output = result.astype(jnp.bfloat16).reshape(tokens.shape)
    attend_back, project_back, expand_back, contract_back = (
        lax.all_gather(attend_weight, ("dp", "fsdp"), axis=0, tiled=True),
        lax.all_gather(project_weight, ("dp", "fsdp"), axis=0, tiled=True),
        lax.all_gather(expand_weight, ("dp", "fsdp"), axis=0, tiled=True),
        lax.all_gather(contract_weight, ("dp", "fsdp"), axis=0, tiled=True),
    )
    upstream = cotangent.reshape(count, width)
    outer_grad = jnp.sum(upstream, axis=0, dtype=jnp.float32)
    contract_grad = jnp.einsum(
        "tf,td->fd", active_low, upstream, preferred_element_type=jnp.float32
    )
    project_grad = jnp.einsum("te,td->ed", mixed_low, upstream, preferred_element_type=jnp.float32)
    active_grad = jnp.einsum(
        "td,fd->tf", upstream, contract_back, preferred_element_type=jnp.float32
    )
    hidden_grad = gelu_pull(active_grad)[0].astype(jnp.bfloat16)
    expand_grad = jnp.einsum(
        "te,tf->ef", normed_low, hidden_grad, preferred_element_type=jnp.float32
    )
    inner_grad = jnp.sum(hidden_grad, axis=0, dtype=jnp.float32)
    normed_grad = jnp.einsum(
        "tf,ef->te", hidden_grad, expand_back, preferred_element_type=jnp.float32
    )
    mixed_grad = jnp.einsum("td,ed->te", upstream, project_back, preferred_element_type=jnp.float32)
    mixed_grad = mixed_grad.astype(jnp.bfloat16).reshape(seq_dev, seq_len, HEADS, HEAD_DIM)
    query_grad, key_grad, value_grad = lax.map(
        attend_backward, (query_low, keys_low, values_low, mixed_grad, logsums, lengths)
    )
    query_turned, key_turned = turn_pull((query_grad, key_grad))
    triple_grad = (
        jnp.stack([query_turned, key_turned, value_grad], axis=2)
        .reshape(count, 3 * width)
        .astype(jnp.bfloat16)
    )
    attend_grad = jnp.einsum(
        "te,tc->ec", normed_low, triple_grad, preferred_element_type=jnp.float32
    )
    normed_grad = normed_grad + jnp.einsum(
        "tc,ec->te", triple_grad, attend_back, preferred_element_type=jnp.float32
    )
    rows_grad, gain_grad, shift_grad = norm_pull(normed_grad)
    token_grad = (
        (upstream.astype(jnp.float32) + rows_grad).astype(jnp.bfloat16).reshape(tokens.shape)
    )
    (
        attend_part,
        project_part,
        expand_part,
        contract_part,
        inner_part,
        outer_part,
        gain_part,
        shift_part,
    ) = (
        lax.psum_scatter(attend_grad, ("dp", "fsdp"), scatter_dimension=0, tiled=True),
        lax.psum_scatter(project_grad, ("dp", "fsdp"), scatter_dimension=0, tiled=True),
        lax.psum_scatter(expand_grad, ("dp", "fsdp"), scatter_dimension=0, tiled=True),
        lax.psum_scatter(contract_grad, ("dp", "fsdp"), scatter_dimension=0, tiled=True),
        lax.psum_scatter(inner_grad, ("dp", "fsdp"), scatter_dimension=0, tiled=True),
        lax.psum_scatter(outer_grad, ("dp", "fsdp"), scatter_dimension=0, tiled=True),
        lax.psum_scatter(gain_grad, ("dp", "fsdp"), scatter_dimension=0, tiled=True),
        lax.psum_scatter(shift_grad, ("dp", "fsdp"), scatter_dimension=0, tiled=True),
    )
    return (
        output,
        token_grad,
        attend_part,
        project_part,
        expand_part,
        contract_part,
        inner_part,
        outer_part,
        gain_part,
        shift_part,
    )


def solution(mesh):
    return jax.shard_map(
        body,
        mesh=mesh,
        in_specs=(
            P(("dp", "fsdp"), None, None),
            P(("dp", "fsdp")),
            P(("dp", "fsdp"), None),
            P(("dp", "fsdp"), None),
            P(("dp", "fsdp"), None),
            P(("dp", "fsdp"), None),
            P(("dp", "fsdp")),
            P(("dp", "fsdp")),
            P(("dp", "fsdp")),
            P(("dp", "fsdp")),
            P(("dp", "fsdp"), None, None),
        ),
        out_specs=(
            P(("dp", "fsdp"), None, None),
            P(("dp", "fsdp"), None, None),
            P(("dp", "fsdp"), None),
            P(("dp", "fsdp"), None),
            P(("dp", "fsdp"), None),
            P(("dp", "fsdp"), None),
            P(("dp", "fsdp")),
            P(("dp", "fsdp")),
            P(("dp", "fsdp")),
            P(("dp", "fsdp")),
        ),
        check_vma=False,
    )
```

profile of v0, /device:TPU:0, one launch (start us, length us, event | category | flops | bytes accessed | tf_op | source)
XLA Modules:
  0.0 1461.5 jit_solution(16712139840498762564)
XLA Ops:
  13.3 42.2 %all-reduce.16 = (bf16[1024]{0:T(1024)(128)(2,1)S(1)}, bf16[1024]{0:T(1024)(128)(2,1)S(1)}, bf16[1024]{0:T(1024)(128)(2,1)}) all-reduce(bf16[1024]{0:T(1024)(128)(2,1)S(1)} %dynamic-update-slice.1, bf16[1024]{0:T(1024)(128)(2,1)S(1)} %dynamic-update-slice, ...), channel_id=1, replica_groups=mesh['dp'=4,'fsdp'=8] {'dp','fsdp'}, use_global_device_ids=true, to_apply=%add.9 | all-reduce | flops 3072 | bytes 12288
  76.4 65.0 %all-gather.6.cloned.1.call-done = bf16[1024,3072]{1,0:T(8,128)(2,1)} async-done(((bf16[32,3072]{1,0:T(8,128)(2,1)}), bf16[1024,3072]{1,0:T(8,128)(2,1)}) %all-gather.6.cloned.1.call-update) | async-done | bytes 6291472 | tf_op jit(solution)/shard_map/all_gather | solution.py:133
  193.4 15.3 %fusion.91 = (f32[16,512]{1,0:T(8,128)S(1)}, f32[16,512,1024]{2,1,0:T(8,128)}) fusion(bf16[1024,16,32]{0,2,1:T(8,128)(2,1)S(1)} %fusion.68, bf16[1024,16,32]{0,2,1:T(8,128)(2,1)} %concatenate.49, bf16[1,1024,16,32]{1,3,2,0:T(8,128)(2,1)S(1)} %slice.135, bf16[1,1024,16,32]{1,3,2,0:T(8,128)(2,1)S(1)} %concatenate.47, pred[512,1024]{1,0:T(8,128)(4,1)} %get-tuple-element.97), kind=kOutput, calls=%fused_computation.143 | convolution fusion | flops 1105190912 | bytes 38305792 | tf_op jit(solution)/shard_map/while/body/eval_jaxpr/qhd,khd->hqk/dot_general | solution.py:51
  208.7 14.7 %fusion.1 = f32[16,512]{1,0:T(8,128)S(1)} fusion(f32[16,512,1024]{2,1,0:T(8,128)} %get-tuple-element.99, f32[16,512]{1,0:T(8,128)S(1)} %get-tuple-element.98), kind=kLoop, calls=%fused_computation.13 | loop fusion | flops 16769024 | bytes 33619968 | tf_op jit(solution)/shard_map/while/body/eval_jaxpr/reduce_sum | solution.py:57
  223.5 13.9 fusion.92
  237.5 16.4 %fusion = f32[16,512]{1,0:T(8,128)S(1)} fusion(f32[16,512,1024]{2,1,0:T(8,128)} %get-tuple-element.101, f32[16,512]{1,0:T(8,128)S(1)} %get-tuple-element.100), kind=kLoop, calls=%fused_computation.12 | loop fusion | flops 16769024 | bytes 33619968 | tf_op jit(solution)/shard_map/while/body/eval_jaxpr/reduce_sum | solution.py:57
  254.0 24.8 %multiply_reduce_fusion.1 = (f32[16,512]{1,0:T(8,128)S(1)}, f32[16,512,1024]{2,1,0:T(8,128)}) fusion(f32[16,512,1024]{2,1,0:T(8,128)} %get-tuple-element.101, f32[16,512]{1,0:T(8,128)S(1)} %log_add_fusion.1, bf16[512,16,64]{0,2,1:T(8,128)(2,1)} %bitcast.179, f32[1,1024,3,16,64]{1,4,3,2,0:T(8,128)S(1)} %bitcast.178), kind=kOutput, calls=%fused_computation.4 | convolution fusion | flops 1098899456 | bytes 70320128 | tf_op jit(solution)/shard_map/while/body/eval_jaxpr/qhd,khd->hqk/dot_general | solution.py:82
  278.9 28.4 %multiply_convert_fusion.1 = bf16[16,512,1024]{2,1,0:T(8,128)(2,1)} fusion(f32[16,512,1024]{2,1,0:T(8,128)} %get-tuple-element.105, f32[16,512,1024]{2,1,0:T(8,128)} %get-tuple-element.101, f32[16,512]{1,0:T(8,128)S(1)} %get-tuple-element.104, f32[16,512]{1,0:T(8,128)S(1)} %log_add_fusion.1), kind=kLoop, calls=%fused_computation.3 | loop fusion | flops 33554432 | bytes 83951616 | tf_op jit(solution)/shard_map/while/body/eval_jaxpr/convert_element_type | solution.py:86
  307.3 24.0 %multiply_reduce_fusion = (f32[16,512]{1,0:T(8,128)S(1)}, f32[16,512,1024]{2,1,0:T(8,128)}) fusion(f32[16,512,1024]{2,1,0:T(8,128)} %get-tuple-element.99, f32[16,512]{1,0:T(8,128)S(1)} %log_add_fusion, bf16[512,16,64]{0,2,1:T(8,128)(2,1)S(1)} %bitcast.181, f32[1,1024,3,16,64]{1,4,3,2,0:T(8,128)} %copy-done), kind=kOutput, calls=%fused_computation.1 | convolution fusion | flops 1098899456 | bytes 70320128 | tf_op jit(solution)/shard_map/while/body/eval_jaxpr/qhd,khd->hqk/dot_general | solution.py:82
  342.1 27.9 %multiply_convert_fusion = bf16[16,512,1024]{2,1,0:T(8,128)(2,1)} fusion(f32[16,512,1024]{2,1,0:T(8,128)} %get-tuple-element.103, f32[16,512,1024]{2,1,0:T(8,128)} %get-tuple-element.99, f32[16,512]{1,0:T(8,128)S(1)} %get-tuple-element.102, f32[16,512]{1,0:T(8,128)S(1)} %log_add_fusion), kind=kLoop, calls=%fused_computation | loop fusion | flops 33554432 | bytes 83951616 | tf_op jit(solution)/shard_map/while/body/eval_jaxpr/convert_element_type | solution.py:86
  384.0 14.3 fusion.63
  398.4 14.8 %fusion.64 = bf16[16,64,512]{2,1,0:T(8,128)(2,1)S(1)} fusion(f32[16,512,1024]{2,1,0:T(8,128)} %get-tuple-element.101, f32[16,512]{1,0:T(8,128)S(1)} %copy-done.36, f32[16,512]{1,0:T(8,128)S(1)} %copy-done.34, f32[1,1024,3,16,64]{1,4,3,2,0:T(8,128)} %copy-done), kind=kOutput, calls=%fused_computation.101 | convolution fusion | flops 1099431936 | bytes 36765696 | tf_op jit(solution)/shard_map/while/body/eval_jaxpr/hqk,khd->qhd/dot_general | solution.py:60
  478.1 15.6 %fusion.11 = f32[16,64,1024]{2,1,0:T(8,128)} fusion(bf16[512,16,64]{0,2,1:T(8,128)(2,1)S(1)} %bitcast.182, f32[16,512,1024]{2,1,0:T(8,128)} %get-tuple-element.99, f32[16,512]{1,0:T(8,128)S(1)} %copy-done.21), kind=kOutput, calls=%fused_computation.25 | convolution fusion | flops 1090519040 | bytes 38830080 | tf_op jit(solution)/shard_map/while/body/eval_jaxpr/hqk,qhd->khd/dot_general | solution.py:95
  493.7 16.8 %add_bitcast_fusion = bf16[1,1024,1,16,64]{1,4,3,2,0:T(8,128)(2,1)} fusion(f32[16,64,1024]{2,1,0:T(8,128)} %fusion.11, bf16[512,16,64]{0,2,1:T(8,128)(2,1)S(1)} %bitcast.180, f32[16,512,1024]{2,1,0:T(8,128)} %get-tuple-element.101, f32[16,512]{1,0:T(8,128)S(1)} %copy-done.23), kind=kOutput, calls=%fused_computation.66 | convolution fusion | flops 1092616192 | bytes 40927232 | tf_op jit(solution)/shard_map/while/body/eval_jaxpr/hqk,qhd->khd/dot_general | solution.py:95
  527.9 66.2 %all-gather = bf16[32,1,128]{2,1,0:T(2,128)(2,1)S(1)} all-gather(bf16[1,1,128]{2,1,0:T(2,128)(2,1)S(1)} %bitcast.190), channel_id=1, replica_groups=mesh['dp'=4,'fsdp'=8] {'dp','fsdp'}, dimensions={0}, use_global_device_ids=true | all-gather | bytes 8448 | tf_op jit(solution)/shard_map/all_gather | solution.py:137
  594.2 15.3 %fusion.84 = f32[1024,4096]{1,0:T(8,128)} fusion(bf16[1024,4096]{1,0:T(8,128)(2,1)} %all-gather.10.cloned.1.call-done, bf16[1,1024,1024]{2,1,0:T(8,128)(2,1)S(1)} %copy-done.2, f32[1024]{0:T(1024)S(1)} %copy-done.46, f32[1024]{0:T(1024)S(1)} %copy-done.40, f32[1024]{0:T(1024)S(1)} %copy-done.42, f32[1024]{0:T(1024)S(1)} %copy-done.38), kind=kOutput, calls=%fused_computation.137 | convolution fusion | flops 8596226048 | bytes 27279360 | tf_op jit(solution)/shard_map/dot_general | solution.py:161
  609.5 26.6 %convert_reduce_fusion = (f32[4096]{0:T(1024)S(1)}, bf16[1024,4096]{1,0:T(8,128)(2,1)}) fusion(f32[1024,4096]{1,0:T(8,128)} %fusion.84, f32[4096]{0:T(1024)S(1)} %bitcast.187, bf16[4096,1024]{1,0:T(8,128)(2,1)} %all-gather.12.cloned.1.call-done, bf16[1,1024,1024]{2,1,0:T(8,128)(2,1)} %param.21), kind=kOutput, calls=%fused_computation.27 | convolution fusion | flops 8686399488 | bytes 35684352 | tf_op jit(solution)/shard_map/td,fd->tf/dot_general | solution.py:185
  636.2 15.3 %fusion.82 = f32[1024,4096]{1,0:T(8,128)} fusion(bf16[1024,4096]{1,0:T(8,128)(2,1)} %get-tuple-element.108, bf16[1,1024,1024]{2,1,0:T(8,128)(2,1)S(1)} %copy-done.2, f32[1024]{0:T(1024)S(1)} %copy-done.46, f32[1024]{0:T(1024)S(1)} %copy-done.40, f32[1024]{0:T(1024)S(1)} %copy-done.42, f32[1024]{0:T(1024)S(1)} %copy-done.38), kind=kOutput, calls=%fused_computation.136 | convolution fusion | flops 8596226048 | bytes 27279360 | tf_op jit(solution)/shard_map/te,tf->ef/dot_general | solution.py:189
  651.6 20.3 %fusion.44 = f32[4096,1024]{1,0:T(8,128)} fusion(bf16[1,1024,1024]{2,1,0:T(8,128)(2,1)} %param.21, f32[1024,4096]{1,0:T(8,128)} %fusion.84, f32[4096]{0:T(1024)S(1)} %bitcast.188), kind=kOutput, calls=%fused_computation.80 | convolution fusion | flops 8631877632 | bytes 35667968 | tf_op jit(solution)/shard_map/tf,td->fd/dot_general | solution.py:181
  690.4 14.8 %fusion.87 = (f32[1024]{0:T(1024)S(1)}, f32[1024]{0:T(1024)S(1)}, f32[1024,1024]{1,0:T(8,128)S(1)}) fusion(f32[1024]{0:T(1024)S(1)} %copy-done.40, f32[1024]{0:T(1024)S(1)} %copy-done.38, bf16[1,1024,1024]{2,1,0:T(8,128)(2,1)S(1)} %copy-done.2, f32[1024,1024]{1,0:T(8,128)S(1)} %fusion.97, bf16[1024,4096]{1,0:T(8,128)(2,1)} %get-tuple-element.108, ...), kind=kOutput, calls=%fused_computation.139 | convolution fusion | flops 8597272576 | bytes 27279360 | tf_op jit(solution)/shard_map/tf,ef->te/dot_general | solution.py:193
  710.8 43.4 %all-reduce.15 = (f32[4096]{0:T(1024)S(1)}, f32[1024]{0:T(1024)S(1)}, f32[1024]{0:T(1024)S(1)}, f32[1024]{0:T(1024)S(1)}) all-reduce(f32[4096]{0:T(1024)S(1)} %get-tuple-element.107, f32[1024]{0:T(1024)S(1)} %get-tuple-element.86, f32[1024]{0:T(1024)S(1)} %get-tuple-element.51, ...), channel_id=6, replica_groups=mesh['dp'=4,'fsdp'=8] {'dp','fsdp'}, use_global_device_ids=true, to_apply=%region_15.16.clone | all-reduce | flops 7168 | bytes 57344
  756.5 18.4 %fusion.41 = bf16[1,1024,1024]{2,1,0:T(8,128)(2,1)} fusion(f32[1024,1024]{1,0:T(8,128)} %fusion.65, bf16[1,1024,1024]{2,1,0:T(8,128)(2,1)S(1)} %copy-done.2, f32[1024]{0:T(1024)S(1)} %convert_element_type.202, bf16[4096,1024]{1,0:T(8,128)(2,1)} %all-gather.12.cloned.1.call-done, f32[1024,4096]{1,0:T(8,128)} %fusion.84, f32[4096]{0:T(1024)S(1)} %bitcast.189), kind=kOutput, calls=%fused_computation.71 | convolution fusion | flops 8637120512 | bytes 33574912 | tf_op jit(solution)/shard_map/dot_general | solution.py:169
  775.0 319.2 %reduce-scatter.9.cloned.1.call-done = f32[32,4096]{1,0:T(8,128)} async-done(((f32[1024,4096]{1,0:T(8,128)}), f32[32,4096]{1,0:T(8,128)}) %reduce-scatter.9.cloned.1.call-update) | async-done | bytes 524304 | tf_op jit(solution)/shard_map/reduce_scatter | solution.py:229
  1094.2 360.3 %reduce-scatter.11.cloned.1.call-done = f32[128,1024]{1,0:T(8,128)} async-done(((f32[4096,1024]{1,0:T(8,128)}), f32[128,1024]{1,0:T(8,128)}) %reduce-scatter.11.cloned.1.call-update) | async-done | bytes 524304 | tf_op jit(solution)/shard_map/reduce_scatter | solution.py:230
  (198 shorter events, 211.6 us)
Async XLA Ops:
  7.2 50.2 %copy-start.1 = (bf16[1,1024,1024]{2,1,0:T(8,128)(2,1)S(1)}, bf16[1,1024,1024]{2,1,0:T(8,128)(2,1)}, u32[]{:S(2)}) copy-start(bf16[1,1024,1024]{2,1,0:T(8,128)(2,1)} %param.11) | copy-start | bytes 6291460
  7.2 63.1 %all-gather.8.cloned.1.call-start = ((), (), s32[]{:S(2)}) async-start(), calls=%async_computation.5 | async-start | bytes 2162688 | tf_op jit(solution)/shard_map/all_gather | solution.py:134
  7.9 133.5 %all-gather.6.cloned.1.call-start = ((), (), s32[]{:S(2)}) async-start(), calls=%async_computation.4 | async-start | bytes 6488064 | tf_op jit(solution)/shard_map/all_gather | solution.py:133
  8.7 585.5 %all-gather.10.cloned.1.call-start = ((), (), s32[]{:S(2)}) async-start(), calls=%async_computation.6 | async-start | bytes 8650752 | tf_op jit(solution)/shard_map/all_gather | solution.py:135
  9.4 600.1 %all-gather.12.cloned.1.call-start = ((), (), s32[]{:S(2)}) async-start(), calls=%async_computation.7 | async-start | bytes 8650752 | tf_op jit(solution)/shard_map/all_gather | solution.py:136
  10.0 765.0 %reduce-scatter.7.cloned.1.call-start = ((), (), s32[]{:S(2)}) async-start(), calls=%async_computation.9 | async-start | bytes 4325376 | tf_op jit(solution)/shard_map/reduce_scatter | solution.py:228
  55.4 94.6 %copy-start.45 = (f32[1024]{0:T(1024)}, f32[1024]{0:T(1024)S(1)}, u32[]{:S(2)}) copy-start(f32[1024]{0:T(1024)S(1)} %convert_element_type.192) | copy-start | bytes 12292
  55.4 94.6 %copy-start.39 = (f32[1024]{0:T(1024)}, f32[1024]{0:T(1024)S(1)}, u32[]{:S(2)}) copy-start(f32[1024]{0:T(1024)S(1)} %convert_element_type.191) | copy-start | bytes 12292
  57.4 92.7 %copy-start.37 = (f32[1024]{0:T(1024)}, f32[1024]{0:T(1024)S(1)}, u32[]{:S(2)}) copy-start(f32[1024]{0:T(1024)S(1)} %broadcast_multiply_fusion) | copy-start | bytes 12292
  58.7 91.4 %copy-start.41 = (f32[1024]{0:T(1024)}, f32[1024]{0:T(1024)S(1)}, u32[]{:S(2)}) copy-start(f32[1024]{0:T(1024)S(1)} %fusion.72) | copy-start | bytes 12292
  59.0 117.0 %copy-start.24 = (f32[1024,16]{0,1:T(8,128)}, f32[1024,16]{0,1:T(8,128)S(1)}, u32[]{:S(2)}) copy-start(f32[1024,16]{0,1:T(8,128)S(1)} %get-tuple-element.94) | copy-start | bytes 196612
  59.0 117.0 %copy-start.26 = (f32[1024,16]{0,1:T(8,128)}, f32[1024,16]{0,1:T(8,128)S(1)}, u32[]{:S(2)}) copy-start(f32[1024,16]{0,1:T(8,128)S(1)} %get-tuple-element.95) | copy-start | bytes 196612
  165.8 57.7 %copy-start.7 = (bf16[1024,16,32]{0,2,1:T(8,128)(2,1)}, bf16[1024,16,32]{0,2,1:T(8,128)(2,1)S(1)}, u32[]{:S(2)}) copy-start(bf16[1024,16,32]{0,2,1:T(8,128)(2,1)S(1)} %fusion.68) | copy-start | bytes 3145732
  167.5 56.0 %copy-start.3 = (bf16[1,1024,16,32]{1,3,2,0:T(8,128)(2,1)}, bf16[1,1024,16,32]{1,3,2,0:T(8,128)(2,1)S(1)}, u32[]{:S(2)}) copy-start(bf16[1,1024,16,32]{1,3,2,0:T(8,128)(2,1)S(1)} %slice.135) | copy-start | bytes 3145732
  190.8 32.8 %copy-start.5 = (bf16[1,1024,16,32]{1,3,2,0:T(8,128)(2,1)}, bf16[1,1024,16,32]{1,3,2,0:T(8,128)(2,1)S(1)}, u32[]{:S(2)}) copy-start(bf16[1,1024,16,32]{1,3,2,0:T(8,128)(2,1)S(1)} %concatenate.47) | copy-start | bytes 3145732
  223.5 118.6 %copy-start.20 = (f32[16,512]{1,0:T(8,128)}, f32[16,512]{1,0:T(8,128)S(1)}, u32[]{:S(2)}) copy-start(f32[16,512]{1,0:T(8,128)S(1)} %log_add_fusion) | copy-start | bytes 98308
  253.9 24.9 %copy-start.35 = (f32[16,512]{1,0:T(8,128)}, f32[16,512]{1,0:T(8,128)S(1)}, u32[]{:S(2)}) copy-start(f32[16,512]{1,0:T(8,128)S(1)} %fusion) | copy-start | bytes 98308
  254.0 24.9 %copy-start.22 = (f32[16,512]{1,0:T(8,128)}, f32[16,512]{1,0:T(8,128)S(1)}, u32[]{:S(2)}) copy-start(f32[16,512]{1,0:T(8,128)S(1)} %log_add_fusion.1) | copy-start | bytes 98308
  278.9 28.4 %copy-start.12 = (bf16[512,1024]{0,1:T(8,128)(2,1)S(1)}, bf16[512,1024]{0,1:T(8,128)(2,1)}, u32[]{:S(2)}) copy-start(bf16[512,1024]{0,1:T(8,128)(2,1)} %get-tuple-element.89) | copy-start | bytes 3145732
  307.3 24.0 %copy-start.4 = (bf16[1,1024,16,32]{1,3,2,0:T(8,128)(2,1)S(1)}, bf16[1,1024,16,32]{1,3,2,0:T(8,128)(2,1)}, u32[]{:S(2)}) copy-start(bf16[1,1024,16,32]{1,3,2,0:T(8,128)(2,1)} %copy-done.3) | copy-start | bytes 3145732
  307.3 24.0 %copy-start.6 = (bf16[1,1024,16,32]{1,3,2,0:T(8,128)(2,1)S(1)}, bf16[1,1024,16,32]{1,3,2,0:T(8,128)(2,1)}, u32[]{:S(2)}) copy-start(bf16[1,1024,16,32]{1,3,2,0:T(8,128)(2,1)} %copy-done.5) | copy-start | bytes 3145732
  430.8 344.1 %reduce-scatter.5.cloned.1.call-start = ((), (), s32[]{:S(2)}) async-start(), calls=%async_computation.8 | async-start | bytes 12976128 | tf_op jit(solution)/shard_map/reduce_scatter | solution.py:227
  527.3 566.9 %reduce-scatter.9.cloned.1.call-start = ((), (), s32[]{:S(2)}) async-start(), calls=%async_computation.10 | async-start | bytes 17301504 | tf_op jit(solution)/shard_map/reduce_scatter | solution.py:229
  651.5 802.9 %reduce-scatter.11.cloned.1.call-start = ((), (), s32[]{:S(2)}) async-start(), calls=%async_computation.11 | async-start | bytes 17301504 | tf_op jit(solution)/shard_map/reduce_scatter | solution.py:230
  (39 other events, 310.4 us)
Sparse Core Ops, SparseCore 0:
  11.0 59.2 all-gather.7
  73.3 68.1 all-gather.5
  144.4 75.6 all-gather.9
  222.9 75.7 all-gather.11
  430.9 143.8 reduce-scatter.6
  581.3 152.2 reduce-scatter.4
  736.5 357.6 reduce-scatter.8
  1097.1 357.3 reduce-scatter.10
where the time goes:
time: 1470 us; the launch traced here: 1460 us
  waiting for transfers between devices  757 us (51%)
  matrix products  343 us (23%)
  blocking collectives  152 us (10%)
  other arithmetic  136 us (9%)
  local copies, waits for them, and re-layouts  57.5 us (4%)
  between operations  15.7 us (1%)
    reduce_scatter x1, waiting for transfers between devices, body(): lax.psum_scatter(contract_grad, ('dp', 'fsdp'), scatter_dimension=0, tile...  360 us
    reduce_scatter x1, waiting for transfers between devices, body(): lax.psum_scatter(expand_grad, ('dp', 'fsdp'), scatter_dimension=0, tiled=...  319 us
    unnamed x2, blocking collectives  85.5 us
    all_gather x1, blocking collectives, body(): lax.all_gather(inner_bias, ('dp', 'fsdp'), axis=0, tiled=True)  66.2 us
    all_gather x1, waiting for transfers between devices, body(): lax.all_gather(attend_weight, ('dp', 'fsdp'), axis=0, tiled=True)  65 us
    convert_element_type x2, other arithmetic, attend_backward(): score_grad = (probs * (upward - inner)).astype(jnp.bfloat16)  56.3 us
    dot_general x2, matrix products, attend_backward(): jnp.einsum('qhd,khd->hqk', upstream_rows, values, preferred_element_type=...  48.8 us
    dot_general x2, matrix products, attend_backward(): jnp.einsum('hqk,qhd->khd', probs.astype(jnp.bfloat16), upstream_rows, pre...  32.4 us
  transfers between devices with their start and end apart: 8, of which 4 were waited for; matrix products, arithmetic and copies ran while one was open for 36% of the time, Pallas kernels for 0%

commit v1 on v0

--- a/solution.py
+++ b/solution.py
@@ -1,3 +1,4 @@
+import functools
 import math
 
 import jax
@@ -105,6 +106,61 @@
     return jax.nn.gelu(inner, approximate=True)
 
 
+ALL = ("dp", "fsdp")
+
+
+PACK = 6144
+
+
+def padded(flat, axis):
+    size = sum(item.shape[axis] for item in flat)
+    extra = -size % PACK
+    if extra:
+        shape = list(flat[0].shape)
+        shape[axis] = extra
+        flat = flat + [jnp.zeros(shape, flat[0].dtype)]
+    return jnp.concatenate(flat, axis=axis)
+
+
+def gather_packed(parts):
+    flat = [part.reshape(-1) for part in parts]
+    packed = padded(flat, 0)
+    full = lax.all_gather(packed, ALL, axis=0, tiled=False)
+    pieces = []
+    offset = 0
+    for part, item in zip(parts, flat):
+        size = item.shape[0]
+        piece = full[:, offset : offset + size]
+        pieces.append(piece.reshape((full.shape[0] * part.shape[0],) + part.shape[1:]))
+        offset += size
+    return pieces
+
+
+SCATTER_ROWS = 8
+SCATTER_COLUMNS = 768
+
+
+def pack_for_scatter(parts, count):
+    flat = [part.astype(jnp.bfloat16).reshape(count, -1) for part in parts]
+    size = sum(item.shape[1] for item in flat)
+    extra = -size % (SCATTER_ROWS * SCATTER_COLUMNS)
+    if extra:
+        flat = flat + [jnp.zeros((count, extra), jnp.bfloat16)]
+    return jnp.concatenate(flat, axis=1).reshape(count * SCATTER_ROWS, -1)
+
+
+def scatter_packed(packed, parts, count):
+    summed = lax.psum_scatter(packed, ALL, scatter_dimension=0, tiled=True).reshape(-1)
+    pieces = []
+    offset = 0
+    for part in parts:
+        size = part.size // count
+        piece = summed[offset : offset + size].astype(jnp.float32)
+        pieces.append(piece.reshape((part.shape[0] // count,) + part.shape[1:]))
+        offset += size
+    return pieces
+
+
 def body(
     tokens,
     lengths,
@@ -117,29 +173,18 @@
     norm_gain,
     norm_shift,
     cotangent,
+    *,
+    count,
 ):
     seq_dev, seq_len, width = tokens.shape
-    count = seq_dev * seq_len
-    (
-        attend_full,
-        project_full,
-        expand_full,
-        contract_full,
-        inner_full,
-        outer_full,
-        gain_full,
-        shift_full,
-    ) = (
-        lax.all_gather(attend_weight, ("dp", "fsdp"), axis=0, tiled=True),
-        lax.all_gather(project_weight, ("dp", "fsdp"), axis=0, tiled=True),
-        lax.all_gather(expand_weight, ("dp", "fsdp"), axis=0, tiled=True),
-        lax.all_gather(contract_weight, ("dp", "fsdp"), axis=0, tiled=True),
-        lax.all_gather(inner_bias, ("dp", "fsdp"), axis=0, tiled=True),
-        lax.all_gather(outer_bias, ("dp", "fsdp"), axis=0, tiled=True),
-        lax.all_gather(norm_gain, ("dp", "fsdp"), axis=0, tiled=True),
-        lax.all_gather(norm_shift, ("dp", "fsdp"), axis=0, tiled=True),
-    )
-    rows = tokens.reshape(count, width).astype(jnp.float32)
+    positions = seq_dev * seq_len
+    attend_full, gain_full, shift_full, inner_full, outer_full = gather_packed(
+        [attend_weight, norm_gain, norm_shift, inner_bias, outer_bias]
+    )
+    expand_full, project_full, contract_full = gather_packed(
+        [expand_weight, project_weight, contract_weight]
+    )
+    rows = tokens.reshape(positions, width).astype(jnp.float32)
     normed, norm_pull = jax.vjp(
         layer_norm, rows, gain_full.astype(jnp.float32), shift_full.astype(jnp.float32)
     )
@@ -157,7 +202,7 @@
     keys_low = keys.astype(jnp.bfloat16)
     values_low = triple[:, :, 2].astype(jnp.bfloat16)
     attended, logsums = lax.map(attend_forward, (query_low, keys_low, values_low, lengths))
-    mixed_low = attended.reshape(count, width)
+    mixed_low = attended.reshape(positions, width)
     hidden = jnp.dot(
         normed_low, expand_full, preferred_element_type=jnp.float32
     ) + inner_full.astype(jnp.float32)
@@ -170,69 +215,52 @@
         + outer_full.astype(jnp.float32)
     )
     output = result.astype(jnp.bfloat16).reshape(tokens.shape)
-    attend_back, project_back, expand_back, contract_back = (
-        lax.all_gather(attend_weight, ("dp", "fsdp"), axis=0, tiled=True),
-        lax.all_gather(project_weight, ("dp", "fsdp"), axis=0, tiled=True),
-        lax.all_gather(expand_weight, ("dp", "fsdp"), axis=0, tiled=True),
-        lax.all_gather(contract_weight, ("dp", "fsdp"), axis=0, tiled=True),
-    )
-    upstream = cotangent.reshape(count, width)
+    upstream = cotangent.reshape(positions, width)
     outer_grad = jnp.sum(upstream, axis=0, dtype=jnp.float32)
     contract_grad = jnp.einsum(
         "tf,td->fd", active_low, upstream, preferred_element_type=jnp.float32
     )
     project_grad = jnp.einsum("te,td->ed", mixed_low, upstream, preferred_element_type=jnp.float32)
     active_grad = jnp.einsum(
-        "td,fd->tf", upstream, contract_back, preferred_element_type=jnp.float32
+        "td,fd->tf", upstream, contract_full, preferred_element_type=jnp.float32
     )
     hidden_grad = gelu_pull(active_grad)[0].astype(jnp.bfloat16)
     expand_grad = jnp.einsum(
         "te,tf->ef", normed_low, hidden_grad, preferred_element_type=jnp.float32
     )
     inner_grad = jnp.sum(hidden_grad, axis=0, dtype=jnp.float32)
+    early = [contract_grad, project_grad, expand_grad, inner_grad, outer_grad]
+    early_packed = pack_for_scatter(early, count)
     normed_grad = jnp.einsum(
-        "tf,ef->te", hidden_grad, expand_back, preferred_element_type=jnp.float32
-    )
-    mixed_grad = jnp.einsum("td,ed->te", upstream, project_back, preferred_element_type=jnp.float32)
+        "tf,ef->te", hidden_grad, expand_full, preferred_element_type=jnp.float32
+    )
+    mixed_grad = jnp.einsum("td,ed->te", upstream, project_full, preferred_element_type=jnp.float32)
     mixed_grad = mixed_grad.astype(jnp.bfloat16).reshape(seq_dev, seq_len, HEADS, HEAD_DIM)
+    early_packed, mixed_grad = lax.optimization_barrier((early_packed, mixed_grad))
+    contract_part, project_part, expand_part, inner_part, outer_part = scatter_packed(
+        early_packed, early, count
+    )
     query_grad, key_grad, value_grad = lax.map(
         attend_backward, (query_low, keys_low, values_low, mixed_grad, logsums, lengths)
     )
     query_turned, key_turned = turn_pull((query_grad, key_grad))
     triple_grad = (
         jnp.stack([query_turned, key_turned, value_grad], axis=2)
-        .reshape(count, 3 * width)
+        .reshape(positions, 3 * width)
         .astype(jnp.bfloat16)
     )
     attend_grad = jnp.einsum(
         "te,tc->ec", normed_low, triple_grad, preferred_element_type=jnp.float32
     )
     normed_grad = normed_grad + jnp.einsum(
-        "tc,ec->te", triple_grad, attend_back, preferred_element_type=jnp.float32
+        "tc,ec->te", triple_grad, attend_full, preferred_element_type=jnp.float32
     )
     rows_grad, gain_grad, shift_grad = norm_pull(normed_grad)
     token_grad = (
         (upstream.astype(jnp.float32) + rows_grad).astype(jnp.bfloat16).reshape(tokens.shape)
     )
-    (
-        attend_part,
-        project_part,
-        expand_part,
-        contract_part,
-        inner_part,
-        outer_part,
-        gain_part,
-        shift_part,
-    ) = (
-        lax.psum_scatter(attend_grad, ("dp", "fsdp"), scatter_dimension=0, tiled=True),
-        lax.psum_scatter(project_grad, ("dp", "fsdp"), scatter_dimension=0, tiled=True),
-        lax.psum_scatter(expand_grad, ("dp", "fsdp"), scatter_dimension=0, tiled=True),
-        lax.psum_scatter(contract_grad, ("dp", "fsdp"), scatter_dimension=0, tiled=True),
-        lax.psum_scatter(inner_grad, ("dp", "fsdp"), scatter_dimension=0, tiled=True),
-        lax.psum_scatter(outer_grad, ("dp", "fsdp"), scatter_dimension=0, tiled=True),
-        lax.psum_scatter(gain_grad, ("dp", "fsdp"), scatter_dimension=0, tiled=True),
-        lax.psum_scatter(shift_grad, ("dp", "fsdp"), scatter_dimension=0, tiled=True),
-    )
+    late = [attend_grad, gain_grad, shift_grad]
+    attend_part, gain_part, shift_part = scatter_packed(pack_for_scatter(late, count), late, count)
     return (
         output,
         token_grad,
@@ -248,8 +276,9 @@
 
 
 def solution(mesh):
+    count = mesh.shape["dp"] * mesh.shape["fsdp"]
     return jax.shard_map(
-        body,
+        functools.partial(body, count=count),
         mesh=mesh,
         in_specs=(
             P(("dp", "fsdp"), None, None),

time: 1470 us -> 1110 us (0.76)
  waiting for transfers between devices: 757 us -> 364 us
  local copies, waits for them, and re-layouts: 57.5 us -> 250 us
  blocking collectives: 152 us -> 0 us
    reduce_scatter x4 -> x2, waiting for transfers between devices: 680 us -> 300 us  [scatter_packed(): lax.psum_scatter(packed, ALL, scatter_dimension=0, tiled=True).reshape(-1)]
    reshape x0 -> x13, local copies, waits for them, and re-layouts: none -> 93.7 us  [the longest x2 34.7 us: pack_for_scatter(): return jnp.concatenate(flat, axis=1).reshape(count * SCATTER_ROWS, -1)]
    unnamed x2 -> x0, blocking collectives: 85.5 us -> none
    all_gather x1 -> x0, blocking collectives: 66.2 us -> none  [body(): lax.all_gather(inner_bias, ('dp', 'fsdp'), axis=0, tiled=True)]
    all_gather x0 -> x2, local copies, waits for them, and re-layouts: none -> 33.5 us  [gather_packed(): full = lax.all_gather(packed, ALL, axis=0, tiled=False)]
    unnamed x120 -> x136, local copies, waits for them, and re-layouts: 14.7 us -> 40.8 us
    slice x1 -> x6, local copies, waits for them, and re-layouts: 1.53 us -> 20.9 us  [the longest x4 17.7 us: gather_packed(): piece = full[:, offset:offset + size]]
    all_gather x4 -> x2, waiting for transfers between devices: 74.8 us -> 63.4 us  [gather_packed(): full = lax.all_gather(packed, ALL, axis=0, tiled=False)]
  transfers between devices with their start and end apart: 8 -> 4, of which waited for: 4 -> 3; matrix products, arithmetic and copies ran while one was open for 36% -> 19% of each run, Pallas kernels for 0% -> 0%
where the time goes in v1:
time: 1110 us
  waiting for transfers between devices  364 us (33%)
  matrix products  340 us (31%)
  local copies, waits for them, and re-layouts  250 us (23%)
  other arithmetic  136 us (12%)
  between operations  15.6 us (1%)
    reduce_scatter x2, waiting for transfers between devices, scatter_packed(): lax.psum_scatter(packed, ALL, scatter_dimension=0, tiled=True).reshape(-1)  300 us
    all_gather x2, waiting for transfers between devices, gather_packed(): full = lax.all_gather(packed, ALL, axis=0, tiled=False)  63.4 us
    convert_element_type x2, other arithmetic, attend_backward(): score_grad = (probs * (upward - inner)).astype(jnp.bfloat16)  56.2 us
    dot_general x2, matrix products, attend_backward(): jnp.einsum('qhd,khd->hqk', upstream_rows, values, preferred_element_type=...  49 us
    unnamed x136, local copies, waits for them, and re-layouts  40.8 us
    reshape x2, local copies, waits for them, and re-layouts, pack_for_scatter(): return jnp.concatenate(flat, axis=1).reshape(count * SCATTER_ROWS, -1)  34.7 us
    all_gather x2, local copies, waits for them, and re-layouts, gather_packed(): full = lax.all_gather(packed, ALL, axis=0, tiled=False)  33.5 us
    dot_general x2, matrix products, attend_backward(): jnp.einsum('hqk,qhd->khd', probs.astype(jnp.bfloat16), upstream_rows, pre...  32.5 us
  transfers between devices with their start and end apart: 4, of which 3 were waited for; matrix products, arithmetic and copies ran while one was open for 19% of the time, Pallas kernels for 0%

profile of v1, /device:TPU:0, one launch (start us, length us, event | category | flops | bytes accessed | tf_op | source)
XLA Modules:
  0.0 1106.7 jit_solution(12804325806021193374)
XLA Ops:
  26.2 63.4 %all-gather.5.cloned.1.call-done = bf16[3342336]{0:T(1024)(128)(2,1)} async-done(((bf16[104448]{0:T(1024)(128)(2,1)}), bf16[3342336]{0:T(1024)(128)(2,1)}) %all-gather.5.cloned.1.call-update) | async-done | bytes 6684688 | tf_op jit(solution)/shard_map/all_gather | solution.py:128
  167.7 15.4 %fusion.109 = (f32[16,512]{1,0:T(8,128)S(1)}, f32[16,512,1024]{2,1,0:T(8,128)}) fusion(bf16[1024,16,32]{0,2,1:T(8,128)(2,1)S(1)} %fusion.78, bf16[1024,16,32]{0,2,1:T(8,128)(2,1)S(1)} %concatenate.63, bf16[1,1024,16,32]{1,3,2,0:T(8,128)(2,1)S(1)} %slice.252, bf16[1,1024,16,32]{1,3,2,0:T(8,128)(2,1)S(1)} %concatenate.61, ...), kind=kOutput, calls=%fused_computation.182 | convolution fusion | flops 1105190912 | bytes 38305792 | tf_op jit(solution)/shard_map/while/body/eval_jaxpr/qhd,khd->hqk/dot_general | solution.py:52
  183.1 14.3 %fusion.110 = (f32[16,512]{1,0:T(8,128)S(1)}, f32[16,512,1024]{2,1,0:T(8,128)}) fusion(bf16[1024,16,32]{0,2,1:T(8,128)(2,1)S(1)} %fusion.78, bf16[1024,16,32]{0,2,1:T(8,128)(2,1)S(1)} %concatenate.63, bf16[1,1024,16,32]{1,3,2,0:T(8,128)(2,1)S(1)} %concatenate.61, bf16[1,1024,16,32]{1,3,2,0:T(8,128)(2,1)S(1)} %slice.252, pred[512,1024]{1,0:T(8,128)(4,1)S(1)} %copy-done.32), kind=kOutput, calls=%fused_computation.183 | convolution fusion | flops 1105190912 | bytes 38305792 | tf_op jit(solution)/shard_map/while/body/eval_jaxpr/qhd,khd->hqk/dot_general | solution.py:52
  197.4 15.6 %fusion.1 = f32[16,512]{1,0:T(8,128)S(1)} fusion(f32[16,512,1024]{2,1,0:T(8,128)} %get-tuple-element.99, f32[16,512]{1,0:T(8,128)S(1)} %get-tuple-element.98), kind=kLoop, calls=%fused_computation.13 | loop fusion | flops 16769024 | bytes 33619968 | tf_op jit(solution)/shard_map/while/body/eval_jaxpr/reduce_sum | solution.py:58
  226.5 17.2 %fusion.73 = bf16[16,64,512]{2,1,0:T(8,128)(2,1)} fusion(f32[16,512,1024]{2,1,0:T(8,128)} %get-tuple-element.99, f32[16,512]{1,0:T(8,128)S(1)} %fusion.1, f32[16,512]{1,0:T(8,128)S(1)} %get-tuple-element.98, f32[1,1024,3,16,64]{1,4,3,2,0:T(8,128)} %copy-done.1), kind=kOutput, calls=%fused_computation.112 | convolution fusion | flops 1099431936 | bytes 36765696 | tf_op jit(solution)/shard_map/while/body/eval_jaxpr/hqk,khd->qhd/dot_general | solution.py:61
  243.7 13.9 %fusion.74 = bf16[16,64,512]{2,1,0:T(8,128)(2,1)} fusion(f32[16,512,1024]{2,1,0:T(8,128)} %get-tuple-element.101, f32[16,512]{1,0:T(8,128)S(1)} %fusion, f32[16,512]{1,0:T(8,128)S(1)} %get-tuple-element.100, f32[1,1024,3,16,64]{1,4,3,2,0:T(8,128)S(1)} %bitcast.215), kind=kOutput, calls=%fused_computation.113 | convolution fusion | flops 1099431936 | bytes 36765696 | tf_op jit(solution)/shard_map/while/body/eval_jaxpr/hqk,khd->qhd/dot_general | solution.py:61
  266.0 25.8 %reshape.648 = bf16[32,294912]{1,0:T(8,128)(2,1)} reshape(bf16[9437184]{0:T(1024)(128)(2,1)} %all-gather.7.cloned.1.call-done) | data formatting | bytes 37748736 | tf_op jit(solution)/shard_map/all_gather | solution.py:128
  329.0 15.2 %fusion.56 = f32[1024,4096]{1,0:T(8,128)} fusion(bf16[1024,4096]{1,0:T(8,128)(2,1)} %reshape.622, bf16[1,1024,1024]{2,1,0:T(8,128)(2,1)S(1)} %copy-done.3, f32[1024]{0:T(1024)S(1)} %copy-done.49, f32[1024]{0:T(1024)S(1)} %copy-done.38, f32[1024]{0:T(1024)S(1)} %copy-done.41, f32[1024]{0:T(1024)S(1)} %copy-done.34), kind=kOutput, calls=%fused_computation.94 | convolution fusion | flops 8596226048 | bytes 27279360 | tf_op jit(solution)/shard_map/dot_general | solution.py:206
  344.2 18.4 %convolution_convert_fusion.1 = bf16[4096,1024]{1,0:T(8,128)(2,1)} fusion(bf16[1,1024,1024]{2,1,0:T(8,128)(2,1)S(1)} %copy-done.16, f32[1024,4096]{1,0:T(8,128)} %fusion.56, f32[4096]{0:T(1024)S(1)} %fusion.92), kind=kOutput, calls=%fused_computation.38 | convolution fusion | flops 8636071936 | bytes 27279360 | tf_op jit(solution)/shard_map/tf,td->fd/dot_general | solution.py:220
  371.5 26.0 %fusion.111 = (bf16[4096]{0:T(1024)(128)(2,1)S(1)}, bf16[1024,4096]{1,0:T(8,128)(2,1)}) fusion(f32[1024,4096]{1,0:T(8,128)} %fusion.56, f32[4096]{0:T(1024)S(1)} %fusion.92, bf16[4096,1024]{1,0:T(8,128)(2,1)} %reshape.623, bf16[1,1024,1024]{2,1,0:T(8,128)(2,1)} %param.21), kind=kOutput, calls=%fused_computation.184 | convolution fusion | flops 8682205184 | bytes 35676160 | tf_op jit(solution)/shard_map/td,fd->tf/dot_general | solution.py:224
  397.6 15.4 %convolution_convert_fusion = bf16[1024,4096]{1,0:T(8,128)(2,1)} fusion(bf16[1024,4096]{1,0:T(8,128)(2,1)} %get-tuple-element.103, bf16[1,1024,1024]{2,1,0:T(8,128)(2,1)S(1)} %copy-done.3, f32[1024]{0:T(1024)S(1)} %copy-done.49, f32[1024]{0:T(1024)S(1)} %copy-done.38, f32[1024]{0:T(1024)S(1)} %copy-done.41, f32[1024]{0:T(1024)S(1)} %copy-done.34), kind=kOutput, calls=%fused_computation.37 | convolution fusion | flops 8600420352 | bytes 18890752 | tf_op jit(solution)/shard_map/te,tf->ef/dot_general | solution.py:228
  443.1 26.9 %reshape.631 = bf16[256,37632]{1,0:T(8,128)(2,1)} reshape(bf16[32,301056]{1,0:T(8,128)(2,1)} %dynamic-update-slice.9) | data formatting | bytes 38535168 | tf_op jit(solution)/shard_map/reshape | solution.py:149
  470.1 16.0 %fusion.11 = f32[16,64,1024]{2,1,0:T(8,128)} fusion(f32[16,512,1024]{2,1,0:T(8,128)} %get-tuple-element.99, f32[16,512]{1,0:T(8,128)S(1)} %copy-done.26, bf16[1,1024,16,64]{1,3,2,0:T(8,128)(2,1)} %bitcast.221), kind=kOutput, calls=%fused_computation.25 | convolution fusion | flops 1090519040 | bytes 38830080 | tf_op jit(solution)/shard_map/while/body/eval_jaxpr/hqk,qhd->khd/dot_general | solution.py:96
  486.1 25.0 %multiply_reduce_fusion = (f32[16,512]{1,0:T(8,128)S(1)}, f32[16,512,1024]{2,1,0:T(8,128)}) fusion(f32[16,512,1024]{2,1,0:T(8,128)} %get-tuple-element.99, f32[16,512]{1,0:T(8,128)S(1)} %copy-done.26, bf16[1,1024,16,64]{1,3,2,0:T(8,128)(2,1)} %bitcast.222, f32[1,1024,3,16,64]{1,4,3,2,0:T(8,128)} %copy-done.1), kind=kOutput, calls=%fused_computation.1 | convolution fusion | flops 1098899456 | bytes 70320128 | tf_op jit(solution)/shard_map/while/body/eval_jaxpr/qhd,khd->hqk/dot_general | solution.py:83
  511.1 24.0 %multiply_reduce_fusion.1 = (f32[16,512]{1,0:T(8,128)S(1)}, f32[16,512,1024]{2,1,0:T(8,128)}) fusion(f32[16,512,1024]{2,1,0:T(8,128)} %get-tuple-element.101, f32[16,512]{1,0:T(8,128)S(1)} %copy-done.27, bf16[1,1024,16,64]{1,3,2,0:T(8,128)(2,1)} %bitcast.223, f32[1,1024,3,16,64]{1,4,3,2,0:T(8,128)S(1)} %bitcast.217), kind=kOutput, calls=%fused_computation.4 | convolution fusion | flops 1098899456 | bytes 70320128 | tf_op jit(solution)/shard_map/while/body/eval_jaxpr/qhd,khd->hqk/dot_general | solution.py:83
  535.1 28.0 %multiply_convert_fusion.1 = bf16[16,512,1024]{2,1,0:T(8,128)(2,1)} fusion(f32[16,512,1024]{2,1,0:T(8,128)} %get-tuple-element.107, f32[16,512,1024]{2,1,0:T(8,128)} %get-tuple-element.101, f32[16,512]{1,0:T(8,128)S(1)} %get-tuple-element.106, f32[16,512]{1,0:T(8,128)S(1)} %copy-done.27), kind=kLoop, calls=%fused_computation.3 | loop fusion | flops 33554432 | bytes 83951616 | tf_op jit(solution)/shard_map/while/body/eval_jaxpr/convert_element_type | solution.py:87
  563.2 12.8 %multiply_bitcast_fusion.2 = f32[512,16,64]{0,2,1:T(8,128)} fusion(bf16[16,512,1024]{2,1,0:T(8,128)(2,1)} %multiply_convert_fusion.1, bf16[1024,16,32]{0,2,1:T(8,128)(2,1)} %copy-done.11, bf16[1024,16,32]{0,2,1:T(8,128)(2,1)S(1)} %copy-done.10), kind=kOutput, calls=%fused_computation.100 | convolution fusion | flops 1078460416 | bytes 20971520 | tf_op jit(solution)/shard_map/while/body/eval_jaxpr/hqk,khd->qhd/dot_general | solution.py:89
  586.8 16.6 %fusion.44 = bf16[1,1024,1,16,64]{1,4,3,2,0:T(8,128)(2,1)} fusion(f32[16,64,1024]{2,1,0:T(8,128)} %fusion.11, f32[16,512,1024]{2,1,0:T(8,128)} %get-tuple-element.101, f32[16,512]{1,0:T(8,128)S(1)} %copy-done.27, bf16[1,1024,16,64]{1,3,2,0:T(8,128)(2,1)} %bitcast.224), kind=kOutput, calls=%fused_computation.77 | convolution fusion | flops 1092616192 | bytes 40927232 | tf_op jit(solution)/shard_map/while/body/eval_jaxpr/hqk,qhd->khd/dot_general | solution.py:96
  603.3 28.1 %multiply_convert_fusion = bf16[16,512,1024]{2,1,0:T(8,128)(2,1)} fusion(f32[16,512,1024]{2,1,0:T(8,128)} %get-tuple-element.105, f32[16,512,1024]{2,1,0:T(8,128)} %get-tuple-element.99, f32[16,512]{1,0:T(8,128)S(1)} %get-tuple-element.104, f32[16,512]{1,0:T(8,128)S(1)} %copy-done.26), kind=kLoop, calls=%fused_computation | loop fusion | flops 33554432 | bytes 83951616 | tf_op jit(solution)/shard_map/while/body/eval_jaxpr/convert_element_type | solution.py:87
  631.4 12.6 %multiply_bitcast_fusion.1 = f32[512,16,64]{0,2,1:T(8,128)} fusion(bf16[16,512,1024]{2,1,0:T(8,128)(2,1)} %multiply_convert_fusion, bf16[1024,16,32]{0,2,1:T(8,128)(2,1)} %copy-done.11, bf16[1024,16,32]{0,2,1:T(8,128)(2,1)S(1)} %copy-done.10), kind=kOutput, calls=%fused_computation.99 | convolution fusion | flops 1078460416 | bytes 20971520 | tf_op jit(solution)/shard_map/while/body/eval_jaxpr/hqk,khd->qhd/dot_general | solution.py:89
  717.2 13.1 %fusion.105 = (bf16[1024]{0:T(1024)(128)(2,1)S(1)}, f32[1024]{0:T(1024)S(1)}, f32[1024,1024]{1,0:T(8,128)}) fusion(f32[1024]{0:T(1024)S(1)} %copy-done.39, f32[1024]{0:T(1024)S(1)} %copy-done.35, bf16[1,1024,1024]{2,1,0:T(8,128)(2,1)S(1)} %copy-done.4, f32[1024,1024]{1,0:T(8,128)S(1)} %copy-done.51, bf16[1024,4096]{1,0:T(8,128)(2,1)} %get-tuple-element.103, ...), kind=kOutput, calls=%fused_computation.178 | convolution fusion | flops 8597272576 | bytes 27277312 | tf_op jit(solution)/shard_map/tf,ef->te/dot_general | solution.py:234
  769.7 18.3 %fusion.47 = bf16[1,1024,1024]{2,1,0:T(8,128)(2,1)} fusion(f32[1024,1024]{1,0:T(8,128)S(1)} %fusion.75, bf16[1,1024,1024]{2,1,0:T(8,128)(2,1)S(1)} %copy-done.4, f32[1024]{0:T(1024)S(1)} %reshape.645, bf16[4096,1024]{1,0:T(8,128)(2,1)} %reshape.623, f32[1024,4096]{1,0:T(8,128)} %fusion.56, f32[4096]{0:T(1024)S(1)} %copy-done.47), kind=kOutput, calls=%fused_computation.80 | convolution fusion | flops 8637120512 | bytes 33574912 | tf_op jit(solution)/shard_map/dot_general | solution.py:214
  787.9 89.9 %reduce-scatter.3.cloned.1.call-done = bf16[8,13056]{1,0:T(8,128)(2,1)} async-done(((bf16[256,13056]{1,0:T(8,128)(2,1)}), bf16[8,13056]{1,0:T(8,128)(2,1)}) %reduce-scatter.3.cloned.1.call-update) | async-done | bytes 208912 | tf_op jit(solution)/shard_map/reduce_scatter | solution.py:153
  881.7 210.6 %reduce-scatter.5.cloned.1.call-done = bf16[8,37632]{1,0:T(8,128)(2,1)} async-done(((bf16[256,37632]{1,0:T(8,128)(2,1)}), bf16[8,37632]{1,0:T(8,128)(2,1)}) %reduce-scatter.5.cloned.1.call-update) | async-done | bytes 602128 | tf_op jit(solution)/shard_map/reduce_scatter | solution.py:153
  (241 shorter events, 328.6 us)
Async XLA Ops:
  7.2 82.4 %all-gather.5.cloned.1.call-start = ((), (), s32[]{:S(2)}) async-start(), calls=%async_computation.4 | async-start | bytes 6893568 | tf_op jit(solution)/shard_map/all_gather | solution.py:128
  16.2 249.8 %all-gather.7.cloned.1.call-start = ((), (), s32[]{:S(2)}) async-start(), calls=%async_computation.5 | async-start | bytes 19464192 | tf_op jit(solution)/shard_map/all_gather | solution.py:128
  19.9 857.9 %reduce-scatter.3.cloned.1.call-start = ((), (), s32[]{:S(2)}) async-start(), calls=%async_computation.2 | async-start | bytes 6893568 | tf_op jit(solution)/shard_map/reduce_scatter | solution.py:153
  23.7 97.4 %copy-start.33 = (f32[1024]{0:T(1024)}, f32[1024]{0:T(1024)S(1)}, u32[]{:S(2)}) copy-start(f32[1024]{0:T(1024)S(1)} %broadcast_multiply_fusion) | copy-start | bytes 12292
  24.4 72.9 %copy-start.43 = (f32[1024]{0:T(1024)}, f32[1024]{0:T(1024)S(1)}, u32[]{:S(2)}) copy-start(f32[1024]{0:T(1024)S(1)} %fusion.33) | copy-start | bytes 12292
  24.4 96.7 %copy-start.40 = (f32[1024]{0:T(1024)}, f32[1024]{0:T(1024)S(1)}, u32[]{:S(2)}) copy-start(f32[1024]{0:T(1024)S(1)} %fusion.93) | copy-start | bytes 12292
  24.7 125.3 %copy-start.28 = (f32[1024,16]{0,1:T(8,128)}, f32[1024,16]{0,1:T(8,128)S(1)}, u32[]{:S(2)}) copy-start(f32[1024,16]{0,1:T(8,128)S(1)} %get-tuple-element.94) | copy-start | bytes 196612
  24.7 125.3 %copy-start.30 = (f32[1024,16]{0,1:T(8,128)}, f32[1024,16]{0,1:T(8,128)S(1)}, u32[]{:S(2)}) copy-start(f32[1024,16]{0,1:T(8,128)S(1)} %get-tuple-element.95) | copy-start | bytes 196612
  140.7 42.4 %copy-start.5 = (bf16[1,1024,16,32]{1,3,2,0:T(8,128)(2,1)}, bf16[1,1024,16,32]{1,3,2,0:T(8,128)(2,1)S(1)}, u32[]{:S(2)}) copy-start(bf16[1,1024,16,32]{1,3,2,0:T(8,128)(2,1)S(1)} %slice.252) | copy-start | bytes 3145732
  163.6 19.4 %copy-start.7 = (bf16[1,1024,16,32]{1,3,2,0:T(8,128)(2,1)}, bf16[1,1024,16,32]{1,3,2,0:T(8,128)(2,1)S(1)}, u32[]{:S(2)}) copy-start(bf16[1,1024,16,32]{1,3,2,0:T(8,128)(2,1)S(1)} %concatenate.61) | copy-start | bytes 3145732
  165.5 17.6 %copy-start.9 = (bf16[1024,16,32]{0,2,1:T(8,128)(2,1)}, bf16[1024,16,32]{0,2,1:T(8,128)(2,1)S(1)}, u32[]{:S(2)}) copy-start(bf16[1024,16,32]{0,2,1:T(8,128)(2,1)S(1)} %concatenate.63) | copy-start | bytes 3145732
  197.4 21.5 %copy-start = (f32[16,512,1024]{2,1,0:T(8,128)S(1)}, f32[16,512,1024]{2,1,0:T(8,128)}, u32[]{:S(2)}) copy-start(f32[16,512,1024]{2,1,0:T(8,128)} %get-tuple-element.101) | copy-start | bytes 100663296
  218.8 24.8 %slice-start.1 = ((s8[12582912]{0:T(1024)(128)(4,1)}), s8[4194304]{0:T(1024)(128)(4,1)S(1)}, s32[]{:S(2)}) async-start(s8[12582912]{0:T(1024)(128)(4,1)} %bitcast.214), calls=%async_computation.7 | async-start | bytes 8388608
  226.5 17.2 %slice-start.2 = ((s8[12582912]{0:T(1024)(128)(4,1)}), s8[4194304]{0:T(1024)(128)(4,1)S(1)}, s32[]{:S(2)}) async-start(s8[12582912]{0:T(1024)(128)(4,1)} %bitcast.214), calls=%async_computation.8 | async-start | bytes 8388608
  264.7 106.8 %copy-start.46 = (f32[4096]{0:T(1024)}, f32[4096]{0:T(1024)S(1)}, u32[]{:S(2)}) copy-start(f32[4096]{0:T(1024)S(1)} %fusion.92) | copy-start | bytes 49156
  443.1 27.0 %copy-start.26 = (f32[16,512]{1,0:T(8,128)S(1)}, f32[16,512]{1,0:T(8,128)}, u32[]{:S(2)}) copy-start(f32[16,512]{1,0:T(8,128)} %log_add_fusion) | copy-start | bytes 98308
  470.1 41.0 %slice-start.4 = ((s8[12582912]{0:T(1024)(128)(4,1)}), s8[4194304]{0:T(1024)(128)(4,1)S(1)}, s32[]{:S(2)}) async-start(s8[12582912]{0:T(1024)(128)(4,1)} %bitcast.216), calls=%async_computation.10 | async-start | bytes 8388608
  486.1 25.1 %slice-start.5 = ((s8[12582912]{0:T(1024)(128)(4,1)}), s8[4194304]{0:T(1024)(128)(4,1)S(1)}, s32[]{:S(2)}) async-start(s8[12582912]{0:T(1024)(128)(4,1)} %bitcast.216), calls=%async_computation.11 | async-start | bytes 8388608
  486.1 25.1 %slice-start.6 = ((s8[12582912]{0:T(1024)(128)(4,1)}), s8[4194304]{0:T(1024)(128)(4,1)S(1)}, s32[]{:S(2)}) async-start(s8[12582912]{0:T(1024)(128)(4,1)} %bitcast.216), calls=%async_computation.12 | async-start | bytes 8388608
  486.1 25.1 %copy-start.27 = (f32[16,512]{1,0:T(8,128)S(1)}, f32[16,512]{1,0:T(8,128)}, u32[]{:S(2)}) copy-start(f32[16,512]{1,0:T(8,128)} %log_add_fusion.1) | copy-start | bytes 98308
  535.1 28.1 %copy-start.10 = (bf16[1024,16,32]{0,2,1:T(8,128)(2,1)S(1)}, bf16[1024,16,32]{0,2,1:T(8,128)(2,1)}, u32[]{:S(2)}) copy-start(bf16[1024,16,32]{0,2,1:T(8,128)(2,1)} %copy-done.9) | copy-start | bytes 3145732
  692.5 24.7 %slice-start.9 = ((s8[8388608]{0:T(1024)(128)(4,1)}), s8[4194304]{0:T(1024)(128)(4,1)S(1)}, s32[]{:S(2)}) async-start(s8[8388608]{0:T(1024)(128)(4,1)} %bitcast.225), calls=%async_computation.15 | async-start | bytes 8388608
  696.4 20.8 %slice-start.10 = ((s8[8388608]{0:T(1024)(128)(4,1)}), s8[4194304]{0:T(1024)(128)(4,1)S(1)}, s32[]{:S(2)}) async-start(s8[8388608]{0:T(1024)(128)(4,1)} %bitcast.225), calls=%async_computation.16 | async-start | bytes 8388608
  761.3 330.9 %reduce-scatter.5.cloned.1.call-start = ((), (), s32[]{:S(2)}) async-start(), calls=%async_computation.3 | async-start | bytes 19869696 | tf_op jit(solution)/shard_map/reduce_scatter | solution.py:153
  (43 other events, 376.7 us)
Sparse Core Ops, SparseCore 0:
  16.3 73.2 all-gather.4
  92.6 122.4 all-gather.6
  761.4 116.3 reduce-scatter.2
  884.1 208.0 reduce-scatter.4

commit v2 on v1

--- a/solution.py
+++ b/solution.py
@@ -1,10 +1,10 @@
-import functools
 import math
 
 import jax
 import jax.numpy as jnp
 from jax import lax
 from jax.sharding import PartitionSpec as P
+
 
 HEADS = 16
 HEAD_DIM = 64
@@ -150,7 +150,8 @@
 
 
 def scatter_packed(packed, parts, count):
-    summed = lax.psum_scatter(packed, ALL, scatter_dimension=0, tiled=True).reshape(-1)
+    summed = lax.psum_scatter(packed, ALL, scatter_dimension=0, tiled=True)
+    summed = summed.reshape(-1)
     pieces = []
     offset = 0
     for part in parts:
@@ -277,8 +278,12 @@
 
 def solution(mesh):
     count = mesh.shape["dp"] * mesh.shape["fsdp"]
+
+    def layer_body(*args):
+        return body(*args, count=count)
+
     return jax.shard_map(
-        functools.partial(body, count=count),
+        layer_body,
         mesh=mesh,
         in_specs=(
             P(("dp", "fsdp"), None, None),

time: 1110 us -> 1110 us (level)
  no operation moved by 1% of the time
where the time goes in v2:
time: 1110 us
  waiting for transfers between devices  364 us (33%)
  matrix products  340 us (31%)
  local copies, waits for them, and re-layouts  250 us (23%)
  other arithmetic  136 us (12%)
  between operations  15.6 us (1%)
    reduce_scatter x2, waiting for transfers between devices, scatter_packed(): summed = lax.psum_scatter(packed, ALL, scatter_dimension=0, tiled=True)  300 us
    all_gather x2, waiting for transfers between devices, gather_packed(): full = lax.all_gather(packed, ALL, axis=0, tiled=False)  63.4 us
    convert_element_type x2, other arithmetic, attend_backward(): score_grad = (probs * (upward - inner)).astype(jnp.bfloat16)  56.2 us
    dot_general x2, matrix products, attend_backward(): jnp.einsum('qhd,khd->hqk', upstream_rows, values, preferred_element_type=...  49 us
    unnamed x136, local copies, waits for them, and re-layouts  40.8 us
    reshape x2, local copies, waits for them, and re-layouts, pack_for_scatter(): return jnp.concatenate(flat, axis=1).reshape(count * SCATTER_ROWS, -1)  34.7 us
    all_gather x2, local copies, waits for them, and re-layouts, gather_packed(): full = lax.all_gather(packed, ALL, axis=0, tiled=False)  33.5 us
    dot_general x2, matrix products, attend_backward(): jnp.einsum('hqk,qhd->khd', probs.astype(jnp.bfloat16), upstream_rows, pre...  32.5 us
  transfers between devices with their start and end apart: 4, of which 3 were waited for; matrix products, arithmetic and copies ran while one was open for 19% of the time, Pallas kernels for 0%

profile of v2, /device:TPU:0, one launch (start us, length us, event | category | flops | bytes accessed | tf_op | source)
XLA Modules:
  0.0 1106.7 jit_solution(12804325806021193374)
XLA Ops:
  26.2 63.4 %all-gather.5.cloned.1.call-done = bf16[3342336]{0:T(1024)(128)(2,1)} async-done(((bf16[104448]{0:T(1024)(128)(2,1)}), bf16[3342336]{0:T(1024)(128)(2,1)}) %all-gather.5.cloned.1.call-update) | async-done | bytes 6684688 | tf_op jit(solution)/shard_map/all_gather | solution.py:128
  167.7 15.4 %fusion.109 = (f32[16,512]{1,0:T(8,128)S(1)}, f32[16,512,1024]{2,1,0:T(8,128)}) fusion(bf16[1024,16,32]{0,2,1:T(8,128)(2,1)S(1)} %fusion.78, bf16[1024,16,32]{0,2,1:T(8,128)(2,1)S(1)} %concatenate.63, bf16[1,1024,16,32]{1,3,2,0:T(8,128)(2,1)S(1)} %slice.252, bf16[1,1024,16,32]{1,3,2,0:T(8,128)(2,1)S(1)} %concatenate.61, ...), kind=kOutput, calls=%fused_computation.182 | convolution fusion | flops 1105190912 | bytes 38305792 | tf_op jit(solution)/shard_map/while/body/eval_jaxpr/qhd,khd->hqk/dot_general | solution.py:52
  183.1 14.3 %fusion.110 = (f32[16,512]{1,0:T(8,128)S(1)}, f32[16,512,1024]{2,1,0:T(8,128)}) fusion(bf16[1024,16,32]{0,2,1:T(8,128)(2,1)S(1)} %fusion.78, bf16[1024,16,32]{0,2,1:T(8,128)(2,1)S(1)} %concatenate.63, bf16[1,1024,16,32]{1,3,2,0:T(8,128)(2,1)S(1)} %concatenate.61, bf16[1,1024,16,32]{1,3,2,0:T(8,128)(2,1)S(1)} %slice.252, pred[512,1024]{1,0:T(8,128)(4,1)S(1)} %copy-done.32), kind=kOutput, calls=%fused_computation.183 | convolution fusion | flops 1105190912 | bytes 38305792 | tf_op jit(solution)/shard_map/while/body/eval_jaxpr/qhd,khd->hqk/dot_general | solution.py:52
  197.4 15.6 %fusion.1 = f32[16,512]{1,0:T(8,128)S(1)} fusion(f32[16,512,1024]{2,1,0:T(8,128)} %get-tuple-element.99, f32[16,512]{1,0:T(8,128)S(1)} %get-tuple-element.98), kind=kLoop, calls=%fused_computation.13 | loop fusion | flops 16769024 | bytes 33619968 | tf_op jit(solution)/shard_map/while/body/eval_jaxpr/reduce_sum | solution.py:58
  226.5 17.2 %fusion.73 = bf16[16,64,512]{2,1,0:T(8,128)(2,1)} fusion(f32[16,512,1024]{2,1,0:T(8,128)} %get-tuple-element.99, f32[16,512]{1,0:T(8,128)S(1)} %fusion.1, f32[16,512]{1,0:T(8,128)S(1)} %get-tuple-element.98, f32[1,1024,3,16,64]{1,4,3,2,0:T(8,128)} %copy-done.1), kind=kOutput, calls=%fused_computation.112 | convolution fusion | flops 1099431936 | bytes 36765696 | tf_op jit(solution)/shard_map/while/body/eval_jaxpr/hqk,khd->qhd/dot_general | solution.py:61
  243.7 13.9 %fusion.74 = bf16[16,64,512]{2,1,0:T(8,128)(2,1)} fusion(f32[16,512,1024]{2,1,0:T(8,128)} %get-tuple-element.101, f32[16,512]{1,0:T(8,128)S(1)} %fusion, f32[16,512]{1,0:T(8,128)S(1)} %get-tuple-element.100, f32[1,1024,3,16,64]{1,4,3,2,0:T(8,128)S(1)} %bitcast.215), kind=kOutput, calls=%fused_computation.113 | convolution fusion | flops 1099431936 | bytes 36765696 | tf_op jit(solution)/shard_map/while/body/eval_jaxpr/hqk,khd->qhd/dot_general | solution.py:61
  266.0 25.8 %reshape.648 = bf16[32,294912]{1,0:T(8,128)(2,1)} reshape(bf16[9437184]{0:T(1024)(128)(2,1)} %all-gather.7.cloned.1.call-done) | data formatting | bytes 37748736 | tf_op jit(solution)/shard_map/all_gather | solution.py:128
  329.0 15.2 %fusion.56 = f32[1024,4096]{1,0:T(8,128)} fusion(bf16[1024,4096]{1,0:T(8,128)(2,1)} %reshape.622, bf16[1,1024,1024]{2,1,0:T(8,128)(2,1)S(1)} %copy-done.3, f32[1024]{0:T(1024)S(1)} %copy-done.49, f32[1024]{0:T(1024)S(1)} %copy-done.38, f32[1024]{0:T(1024)S(1)} %copy-done.41, f32[1024]{0:T(1024)S(1)} %copy-done.34), kind=kOutput, calls=%fused_computation.94 | convolution fusion | flops 8596226048 | bytes 27279360 | tf_op jit(solution)/shard_map/dot_general | solution.py:207
  344.2 18.4 %convolution_convert_fusion.1 = bf16[4096,1024]{1,0:T(8,128)(2,1)} fusion(bf16[1,1024,1024]{2,1,0:T(8,128)(2,1)S(1)} %copy-done.16, f32[1024,4096]{1,0:T(8,128)} %fusion.56, f32[4096]{0:T(1024)S(1)} %fusion.92), kind=kOutput, calls=%fused_computation.38 | convolution fusion | flops 8636071936 | bytes 27279360 | tf_op jit(solution)/shard_map/tf,td->fd/dot_general | solution.py:221
  371.5 26.0 %fusion.111 = (bf16[4096]{0:T(1024)(128)(2,1)S(1)}, bf16[1024,4096]{1,0:T(8,128)(2,1)}) fusion(f32[1024,4096]{1,0:T(8,128)} %fusion.56, f32[4096]{0:T(1024)S(1)} %fusion.92, bf16[4096,1024]{1,0:T(8,128)(2,1)} %reshape.623, bf16[1,1024,1024]{2,1,0:T(8,128)(2,1)} %param.21), kind=kOutput, calls=%fused_computation.184 | convolution fusion | flops 8682205184 | bytes 35676160 | tf_op jit(solution)/shard_map/td,fd->tf/dot_general | solution.py:225
  397.6 15.4 %convolution_convert_fusion = bf16[1024,4096]{1,0:T(8,128)(2,1)} fusion(bf16[1024,4096]{1,0:T(8,128)(2,1)} %get-tuple-element.103, bf16[1,1024,1024]{2,1,0:T(8,128)(2,1)S(1)} %copy-done.3, f32[1024]{0:T(1024)S(1)} %copy-done.49, f32[1024]{0:T(1024)S(1)} %copy-done.38, f32[1024]{0:T(1024)S(1)} %copy-done.41, f32[1024]{0:T(1024)S(1)} %copy-done.34), kind=kOutput, calls=%fused_computation.37 | convolution fusion | flops 8600420352 | bytes 18890752 | tf_op jit(solution)/shard_map/te,tf->ef/dot_general | solution.py:229
  443.1 26.9 %reshape.631 = bf16[256,37632]{1,0:T(8,128)(2,1)} reshape(bf16[32,301056]{1,0:T(8,128)(2,1)} %dynamic-update-slice.9) | data formatting | bytes 38535168 | tf_op jit(solution)/shard_map/reshape | solution.py:149
  470.1 16.0 %fusion.11 = f32[16,64,1024]{2,1,0:T(8,128)} fusion(f32[16,512,1024]{2,1,0:T(8,128)} %get-tuple-element.99, f32[16,512]{1,0:T(8,128)S(1)} %copy-done.26, bf16[1,1024,16,64]{1,3,2,0:T(8,128)(2,1)} %bitcast.221), kind=kOutput, calls=%fused_computation.25 | convolution fusion | flops 1090519040 | bytes 38830080 | tf_op jit(solution)/shard_map/while/body/eval_jaxpr/hqk,qhd->khd/dot_general | solution.py:96
  486.1 25.0 %multiply_reduce_fusion = (f32[16,512]{1,0:T(8,128)S(1)}, f32[16,512,1024]{2,1,0:T(8,128)}) fusion(f32[16,512,1024]{2,1,0:T(8,128)} %get-tuple-element.99, f32[16,512]{1,0:T(8,128)S(1)} %copy-done.26, bf16[1,1024,16,64]{1,3,2,0:T(8,128)(2,1)} %bitcast.222, f32[1,1024,3,16,64]{1,4,3,2,0:T(8,128)} %copy-done.1), kind=kOutput, calls=%fused_computation.1 | convolution fusion | flops 1098899456 | bytes 70320128 | tf_op jit(solution)/shard_map/while/body/eval_jaxpr/qhd,khd->hqk/dot_general | solution.py:83
  511.1 24.0 %multiply_reduce_fusion.1 = (f32[16,512]{1,0:T(8,128)S(1)}, f32[16,512,1024]{2,1,0:T(8,128)}) fusion(f32[16,512,1024]{2,1,0:T(8,128)} %get-tuple-element.101, f32[16,512]{1,0:T(8,128)S(1)} %copy-done.27, bf16[1,1024,16,64]{1,3,2,0:T(8,128)(2,1)} %bitcast.223, f32[1,1024,3,16,64]{1,4,3,2,0:T(8,128)S(1)} %bitcast.217), kind=kOutput, calls=%fused_computation.4 | convolution fusion | flops 1098899456 | bytes 70320128 | tf_op jit(solution)/shard_map/while/body/eval_jaxpr/qhd,khd->hqk/dot_general | solution.py:83
  535.1 28.0 %multiply_convert_fusion.1 = bf16[16,512,1024]{2,1,0:T(8,128)(2,1)} fusion(f32[16,512,1024]{2,1,0:T(8,128)} %get-tuple-element.107, f32[16,512,1024]{2,1,0:T(8,128)} %get-tuple-element.101, f32[16,512]{1,0:T(8,128)S(1)} %get-tuple-element.106, f32[16,512]{1,0:T(8,128)S(1)} %copy-done.27), kind=kLoop, calls=%fused_computation.3 | loop fusion | flops 33554432 | bytes 83951616 | tf_op jit(solution)/shard_map/while/body/eval_jaxpr/convert_element_type | solution.py:87
  563.2 12.8 %multiply_bitcast_fusion.2 = f32[512,16,64]{0,2,1:T(8,128)} fusion(bf16[16,512,1024]{2,1,0:T(8,128)(2,1)} %multiply_convert_fusion.1, bf16[1024,16,32]{0,2,1:T(8,128)(2,1)} %copy-done.11, bf16[1024,16,32]{0,2,1:T(8,128)(2,1)S(1)} %copy-done.10), kind=kOutput, calls=%fused_computation.100 | convolution fusion | flops 1078460416 | bytes 20971520 | tf_op jit(solution)/shard_map/while/body/eval_jaxpr/hqk,khd->qhd/dot_general | solution.py:89
  586.8 16.6 %fusion.44 = bf16[1,1024,1,16,64]{1,4,3,2,0:T(8,128)(2,1)} fusion(f32[16,64,1024]{2,1,0:T(8,128)} %fusion.11, f32[16,512,1024]{2,1,0:T(8,128)} %get-tuple-element.101, f32[16,512]{1,0:T(8,128)S(1)} %copy-done.27, bf16[1,1024,16,64]{1,3,2,0:T(8,128)(2,1)} %bitcast.224), kind=kOutput, calls=%fused_computation.77 | convolution fusion | flops 1092616192 | bytes 40927232 | tf_op jit(solution)/shard_map/while/body/eval_jaxpr/hqk,qhd->khd/dot_general | solution.py:96
  603.3 28.1 %multiply_convert_fusion = bf16[16,512,1024]{2,1,0:T(8,128)(2,1)} fusion(f32[16,512,1024]{2,1,0:T(8,128)} %get-tuple-element.105, f32[16,512,1024]{2,1,0:T(8,128)} %get-tuple-element.99, f32[16,512]{1,0:T(8,128)S(1)} %get-tuple-element.104, f32[16,512]{1,0:T(8,128)S(1)} %copy-done.26), kind=kLoop, calls=%fused_computation | loop fusion | flops 33554432 | bytes 83951616 | tf_op jit(solution)/shard_map/while/body/eval_jaxpr/convert_element_type | solution.py:87
  631.4 12.6 %multiply_bitcast_fusion.1 = f32[512,16,64]{0,2,1:T(8,128)} fusion(bf16[16,512,1024]{2,1,0:T(8,128)(2,1)} %multiply_convert_fusion, bf16[1024,16,32]{0,2,1:T(8,128)(2,1)} %copy-done.11, bf16[1024,16,32]{0,2,1:T(8,128)(2,1)S(1)} %copy-done.10), kind=kOutput, calls=%fused_computation.99 | convolution fusion | flops 1078460416 | bytes 20971520 | tf_op jit(solution)/shard_map/while/body/eval_jaxpr/hqk,khd->qhd/dot_general | solution.py:89
  717.2 13.1 %fusion.105 = (bf16[1024]{0:T(1024)(128)(2,1)S(1)}, f32[1024]{0:T(1024)S(1)}, f32[1024,1024]{1,0:T(8,128)}) fusion(f32[1024]{0:T(1024)S(1)} %copy-done.39, f32[1024]{0:T(1024)S(1)} %copy-done.35, bf16[1,1024,1024]{2,1,0:T(8,128)(2,1)S(1)} %copy-done.4, f32[1024,1024]{1,0:T(8,128)S(1)} %copy-done.51, bf16[1024,4096]{1,0:T(8,128)(2,1)} %get-tuple-element.103, ...), kind=kOutput, calls=%fused_computation.178 | convolution fusion | flops 8597272576 | bytes 27277312 | tf_op jit(solution)/shard_map/tf,ef->te/dot_general | solution.py:235
  769.7 18.3 %fusion.47 = bf16[1,1024,1024]{2,1,0:T(8,128)(2,1)} fusion(f32[1024,1024]{1,0:T(8,128)S(1)} %fusion.75, bf16[1,1024,1024]{2,1,0:T(8,128)(2,1)S(1)} %copy-done.4, f32[1024]{0:T(1024)S(1)} %reshape.645, bf16[4096,1024]{1,0:T(8,128)(2,1)} %reshape.623, f32[1024,4096]{1,0:T(8,128)} %fusion.56, f32[4096]{0:T(1024)S(1)} %copy-done.47), kind=kOutput, calls=%fused_computation.80 | convolution fusion | flops 8637120512 | bytes 33574912 | tf_op jit(solution)/shard_map/dot_general | solution.py:215
  787.9 89.9 %reduce-scatter.3.cloned.1.call-done = bf16[8,13056]{1,0:T(8,128)(2,1)} async-done(((bf16[256,13056]{1,0:T(8,128)(2,1)}), bf16[8,13056]{1,0:T(8,128)(2,1)}) %reduce-scatter.3.cloned.1.call-update) | async-done | bytes 208912 | tf_op jit(solution)/shard_map/reduce_scatter | solution.py:153
  881.7 210.6 %reduce-scatter.5.cloned.1.call-done = bf16[8,37632]{1,0:T(8,128)(2,1)} async-done(((bf16[256,37632]{1,0:T(8,128)(2,1)}), bf16[8,37632]{1,0:T(8,128)(2,1)}) %reduce-scatter.5.cloned.1.call-update) | async-done | bytes 602128 | tf_op jit(solution)/shard_map/reduce_scatter | solution.py:153
  (241 shorter events, 328.6 us)
Async XLA Ops:
  7.2 82.4 %all-gather.5.cloned.1.call-start = ((), (), s32[]{:S(2)}) async-start(), calls=%async_computation.4 | async-start | bytes 6893568 | tf_op jit(solution)/shard_map/all_gather | solution.py:128
  16.2 249.8 %all-gather.7.cloned.1.call-start = ((), (), s32[]{:S(2)}) async-start(), calls=%async_computation.5 | async-start | bytes 19464192 | tf_op jit(solution)/shard_map/all_gather | solution.py:128
  19.9 857.9 %reduce-scatter.3.cloned.1.call-start = ((), (), s32[]{:S(2)}) async-start(), calls=%async_computation.2 | async-start | bytes 6893568 | tf_op jit(solution)/shard_map/reduce_scatter | solution.py:153
  23.7 97.4 %copy-start.33 = (f32[1024]{0:T(1024)}, f32[1024]{0:T(1024)S(1)}, u32[]{:S(2)}) copy-start(f32[1024]{0:T(1024)S(1)} %broadcast_multiply_fusion) | copy-start | bytes 12292
  24.4 72.9 %copy-start.43 = (f32[1024]{0:T(1024)}, f32[1024]{0:T(1024)S(1)}, u32[]{:S(2)}) copy-start(f32[1024]{0:T(1024)S(1)} %fusion.33) | copy-start | bytes 12292
  24.4 96.7 %copy-start.40 = (f32[1024]{0:T(1024)}, f32[1024]{0:T(1024)S(1)}, u32[]{:S(2)}) copy-start(f32[1024]{0:T(1024)S(1)} %fusion.93) | copy-start | bytes 12292
  24.7 125.3 %copy-start.28 = (f32[1024,16]{0,1:T(8,128)}, f32[1024,16]{0,1:T(8,128)S(1)}, u32[]{:S(2)}) copy-start(f32[1024,16]{0,1:T(8,128)S(1)} %get-tuple-element.94) | copy-start | bytes 196612
  24.7 125.3 %copy-start.30 = (f32[1024,16]{0,1:T(8,128)}, f32[1024,16]{0,1:T(8,128)S(1)}, u32[]{:S(2)}) copy-start(f32[1024,16]{0,1:T(8,128)S(1)} %get-tuple-element.95) | copy-start | bytes 196612
  140.7 42.4 %copy-start.5 = (bf16[1,1024,16,32]{1,3,2,0:T(8,128)(2,1)}, bf16[1,1024,16,32]{1,3,2,0:T(8,128)(2,1)S(1)}, u32[]{:S(2)}) copy-start(bf16[1,1024,16,32]{1,3,2,0:T(8,128)(2,1)S(1)} %slice.252) | copy-start | bytes 3145732
  163.6 19.4 %copy-start.7 = (bf16[1,1024,16,32]{1,3,2,0:T(8,128)(2,1)}, bf16[1,1024,16,32]{1,3,2,0:T(8,128)(2,1)S(1)}, u32[]{:S(2)}) copy-start(bf16[1,1024,16,32]{1,3,2,0:T(8,128)(2,1)S(1)} %concatenate.61) | copy-start | bytes 3145732
  165.5 17.6 %copy-start.9 = (bf16[1024,16,32]{0,2,1:T(8,128)(2,1)}, bf16[1024,16,32]{0,2,1:T(8,128)(2,1)S(1)}, u32[]{:S(2)}) copy-start(bf16[1024,16,32]{0,2,1:T(8,128)(2,1)S(1)} %concatenate.63) | copy-start | bytes 3145732
  197.4 21.5 %copy-start = (f32[16,512,1024]{2,1,0:T(8,128)S(1)}, f32[16,512,1024]{2,1,0:T(8,128)}, u32[]{:S(2)}) copy-start(f32[16,512,1024]{2,1,0:T(8,128)} %get-tuple-element.101) | copy-start | bytes 100663296
  218.8 24.8 %slice-start.1 = ((s8[12582912]{0:T(1024)(128)(4,1)}), s8[4194304]{0:T(1024)(128)(4,1)S(1)}, s32[]{:S(2)}) async-start(s8[12582912]{0:T(1024)(128)(4,1)} %bitcast.214), calls=%async_computation.7 | async-start | bytes 8388608
  226.5 17.2 %slice-start.2 = ((s8[12582912]{0:T(1024)(128)(4,1)}), s8[4194304]{0:T(1024)(128)(4,1)S(1)}, s32[]{:S(2)}) async-start(s8[12582912]{0:T(1024)(128)(4,1)} %bitcast.214), calls=%async_computation.8 | async-start | bytes 8388608
  264.7 106.8 %copy-start.46 = (f32[4096]{0:T(1024)}, f32[4096]{0:T(1024)S(1)}, u32[]{:S(2)}) copy-start(f32[4096]{0:T(1024)S(1)} %fusion.92) | copy-start | bytes 49156
  443.1 27.0 %copy-start.26 = (f32[16,512]{1,0:T(8,128)S(1)}, f32[16,512]{1,0:T(8,128)}, u32[]{:S(2)}) copy-start(f32[16,512]{1,0:T(8,128)} %log_add_fusion) | copy-start | bytes 98308
  470.1 41.0 %slice-start.4 = ((s8[12582912]{0:T(1024)(128)(4,1)}), s8[4194304]{0:T(1024)(128)(4,1)S(1)}, s32[]{:S(2)}) async-start(s8[12582912]{0:T(1024)(128)(4,1)} %bitcast.216), calls=%async_computation.10 | async-start | bytes 8388608
  486.1 25.1 %slice-start.5 = ((s8[12582912]{0:T(1024)(128)(4,1)}), s8[4194304]{0:T(1024)(128)(4,1)S(1)}, s32[]{:S(2)}) async-start(s8[12582912]{0:T(1024)(128)(4,1)} %bitcast.216), calls=%async_computation.11 | async-start | bytes 8388608
  486.1 25.1 %slice-start.6 = ((s8[12582912]{0:T(1024)(128)(4,1)}), s8[4194304]{0:T(1024)(128)(4,1)S(1)}, s32[]{:S(2)}) async-start(s8[12582912]{0:T(1024)(128)(4,1)} %bitcast.216), calls=%async_computation.12 | async-start | bytes 8388608
  486.1 25.1 %copy-start.27 = (f32[16,512]{1,0:T(8,128)S(1)}, f32[16,512]{1,0:T(8,128)}, u32[]{:S(2)}) copy-start(f32[16,512]{1,0:T(8,128)} %log_add_fusion.1) | copy-start | bytes 98308
  535.1 28.1 %copy-start.10 = (bf16[1024,16,32]{0,2,1:T(8,128)(2,1)S(1)}, bf16[1024,16,32]{0,2,1:T(8,128)(2,1)}, u32[]{:S(2)}) copy-start(bf16[1024,16,32]{0,2,1:T(8,128)(2,1)} %copy-done.9) | copy-start | bytes 3145732
  692.5 24.7 %slice-start.9 = ((s8[8388608]{0:T(1024)(128)(4,1)}), s8[4194304]{0:T(1024)(128)(4,1)S(1)}, s32[]{:S(2)}) async-start(s8[8388608]{0:T(1024)(128)(4,1)} %bitcast.225), calls=%async_computation.15 | async-start | bytes 8388608
  696.4 20.8 %slice-start.10 = ((s8[8388608]{0:T(1024)(128)(4,1)}), s8[4194304]{0:T(1024)(128)(4,1)S(1)}, s32[]{:S(2)}) async-start(s8[8388608]{0:T(1024)(128)(4,1)} %bitcast.225), calls=%async_computation.16 | async-start | bytes 8388608
  761.3 330.9 %reduce-scatter.5.cloned.1.call-start = ((), (), s32[]{:S(2)}) async-start(), calls=%async_computation.3 | async-start | bytes 19869696 | tf_op jit(solution)/shard_map/reduce_scatter | solution.py:153
  (43 other events, 376.7 us)
Sparse Core Ops, SparseCore 0:
  16.3 73.2 all-gather.4
  92.6 122.4 all-gather.6
  761.4 116.3 reduce-scatter.2
  884.1 208.0 reduce-scatter.4

commit v3 on v1

--- a/solution.py
+++ b/solution.py
@@ -1,10 +1,10 @@
-import functools
 import math
 
 import jax
 import jax.numpy as jnp
 from jax import lax
 from jax.sharding import PartitionSpec as P
+
 
 HEADS = 16
 HEAD_DIM = 64
@@ -109,56 +109,40 @@
 ALL = ("dp", "fsdp")
 
 
-PACK = 6144
-
-
-def padded(flat, axis):
-    size = sum(item.shape[axis] for item in flat)
-    extra = -size % PACK
+COLUMNS = 384
+
+
+def pad_columns(blocks):
+    width = sum(block.shape[1] for block in blocks)
+    extra = -width % COLUMNS
     if extra:
-        shape = list(flat[0].shape)
-        shape[axis] = extra
-        flat = flat + [jnp.zeros(shape, flat[0].dtype)]
-    return jnp.concatenate(flat, axis=axis)
-
-
-def gather_packed(parts):
-    flat = [part.reshape(-1) for part in parts]
-    packed = padded(flat, 0)
-    full = lax.all_gather(packed, ALL, axis=0, tiled=False)
+        blocks = blocks + [jnp.zeros((blocks[0].shape[0], extra), blocks[0].dtype)]
+    return jnp.concatenate(blocks, axis=1)
+
+
+def split_columns(packed, widths):
     pieces = []
     offset = 0
-    for part, item in zip(parts, flat):
-        size = item.shape[0]
-        piece = full[:, offset : offset + size]
-        pieces.append(piece.reshape((full.shape[0] * part.shape[0],) + part.shape[1:]))
-        offset += size
+    for width in widths:
+        pieces.append(packed[:, offset : offset + width])
+        offset += width
     return pieces
 
 
-SCATTER_ROWS = 8
-SCATTER_COLUMNS = 768
-
-
-def pack_for_scatter(parts, count):
-    flat = [part.astype(jnp.bfloat16).reshape(count, -1) for part in parts]
-    size = sum(item.shape[1] for item in flat)
-    extra = -size % (SCATTER_ROWS * SCATTER_COLUMNS)
-    if extra:
-        flat = flat + [jnp.zeros((count, extra), jnp.bfloat16)]
-    return jnp.concatenate(flat, axis=1).reshape(count * SCATTER_ROWS, -1)
-
-
-def scatter_packed(packed, parts, count):
-    summed = lax.psum_scatter(packed, ALL, scatter_dimension=0, tiled=True).reshape(-1)
-    pieces = []
-    offset = 0
-    for part in parts:
-        size = part.size // count
-        piece = summed[offset : offset + size].astype(jnp.float32)
-        pieces.append(piece.reshape((part.shape[0] // count,) + part.shape[1:]))
-        offset += size
-    return pieces
+def gather_columns(blocks):
+    packed = pad_columns(blocks)
+    full = lax.all_gather(packed[None], ALL, axis=0, tiled=True)
+    full = full.reshape(full.shape[0] * full.shape[1], full.shape[2])
+    return split_columns(full, [block.shape[1] for block in blocks])
+
+
+def scatter_columns(packed, widths):
+    summed = lax.psum_scatter(packed, ALL, scatter_dimension=0, tiled=True)
+    return [piece.astype(jnp.float32) for piece in split_columns(summed, widths)]
+
+
+def as_column(vector, rows):
+    return vector.reshape(rows, -1)
 
 
 def body(
@@ -173,17 +157,27 @@
     norm_gain,
     norm_shift,
     cotangent,
-    *,
-    count,
 ):
     seq_dev, seq_len, width = tokens.shape
     positions = seq_dev * seq_len
-    attend_full, gain_full, shift_full, inner_full, outer_full = gather_packed(
-        [attend_weight, norm_gain, norm_shift, inner_bias, outer_bias]
-    )
-    expand_full, project_full, contract_full = gather_packed(
-        [expand_weight, project_weight, contract_weight]
-    )
+    rows_dev = attend_weight.shape[0]
+    attend_full, gain_full, shift_full, inner_full, outer_full = gather_columns(
+        [
+            attend_weight,
+            as_column(norm_gain, rows_dev),
+            as_column(norm_shift, rows_dev),
+            as_column(inner_bias, rows_dev),
+            as_column(outer_bias, rows_dev),
+        ]
+    )
+    gain_full = gain_full.reshape(-1)
+    shift_full = shift_full.reshape(-1)
+    inner_full = inner_full.reshape(-1)
+    outer_full = outer_full.reshape(-1)
+    expand_full, project_full, contract_full = gather_columns(
+        [expand_weight, project_weight, contract_weight.reshape(rows_dev, -1)]
+    )
+    contract_full = contract_full.reshape(-1, width)
     rows = tokens.reshape(positions, width).astype(jnp.float32)
     normed, norm_pull = jax.vjp(
         layer_norm, rows, gain_full.astype(jnp.float32), shift_full.astype(jnp.float32)
@@ -229,17 +223,28 @@
         "te,tf->ef", normed_low, hidden_grad, preferred_element_type=jnp.float32
     )
     inner_grad = jnp.sum(hidden_grad, axis=0, dtype=jnp.float32)
-    early = [contract_grad, project_grad, expand_grad, inner_grad, outer_grad]
-    early_packed = pack_for_scatter(early, count)
+    rows_all = expand_grad.shape[0]
+    early = [
+        expand_grad.astype(jnp.bfloat16),
+        contract_grad.astype(jnp.bfloat16).reshape(rows_all, -1),
+        project_grad.astype(jnp.bfloat16),
+        as_column(inner_grad.astype(jnp.bfloat16), rows_all),
+        as_column(outer_grad.astype(jnp.bfloat16), rows_all),
+    ]
+    early_widths = [block.shape[1] for block in early]
+    early_packed = pad_columns(early)
     normed_grad = jnp.einsum(
         "tf,ef->te", hidden_grad, expand_full, preferred_element_type=jnp.float32
     )
     mixed_grad = jnp.einsum("td,ed->te", upstream, project_full, preferred_element_type=jnp.float32)
     mixed_grad = mixed_grad.astype(jnp.bfloat16).reshape(seq_dev, seq_len, HEADS, HEAD_DIM)
     early_packed, mixed_grad = lax.optimization_barrier((early_packed, mixed_grad))
-    contract_part, project_part, expand_part, inner_part, outer_part = scatter_packed(
-        early_packed, early, count
-    )
+    expand_part, contract_part, project_part, inner_part, outer_part = scatter_columns(
+        early_packed, early_widths
+    )
+    contract_part = contract_part.reshape(-1, width)
+    inner_part = inner_part.reshape(-1)
+    outer_part = outer_part.reshape(-1)
     query_grad, key_grad, value_grad = lax.map(
         attend_backward, (query_low, keys_low, values_low, mixed_grad, logsums, lengths)
     )
@@ -259,8 +264,16 @@
     token_grad = (
         (upstream.astype(jnp.float32) + rows_grad).astype(jnp.bfloat16).reshape(tokens.shape)
     )
-    late = [attend_grad, gain_grad, shift_grad]
-    attend_part, gain_part, shift_part = scatter_packed(pack_for_scatter(late, count), late, count)
+    late = [
+        attend_grad.astype(jnp.bfloat16),
+        as_column(gain_grad.astype(jnp.bfloat16), rows_all),
+        as_column(shift_grad.astype(jnp.bfloat16), rows_all),
+    ]
+    attend_part, gain_part, shift_part = scatter_columns(
+        pad_columns(late), [block.shape[1] for block in late]
+    )
+    gain_part = gain_part.reshape(-1)
+    shift_part = shift_part.reshape(-1)
     return (
         output,
         token_grad,
@@ -276,9 +289,8 @@
 
 
 def solution(mesh):
-    count = mesh.shape["dp"] * mesh.shape["fsdp"]
     return jax.shard_map(
-        functools.partial(body, count=count),
+        body,
         mesh=mesh,
         in_specs=(
             P(("dp", "fsdp"), None, None),

time: 1110 us -> 1020 us (0.919)
  local copies, waits for them, and re-layouts: 250 us -> 143 us
    reshape x13 -> x11, local copies, waits for them, and re-layouts: 93.7 us -> 35.3 us  [the longest x1 14.1 us: body(): contract_full = contract_full.reshape(-1, width)]
    unnamed x136 -> x118, local copies, waits for them, and re-layouts: 40.8 us -> 6.52 us
    all_gather x2 -> x0, local copies, waits for them, and re-layouts: 33.5 us -> none  [gather_packed(): full = lax.all_gather(packed, ALL, axis=0, tiled=False)]
    concatenate x3, local copies, waits for them, and re-layouts: 14.4 us -> 42.6 us  [pad_columns(): return jnp.concatenate(blocks, axis=1)]
    slice x6 -> x1, local copies, waits for them, and re-layouts: 20.9 us -> 7.73 us  [split_columns(): pieces.append(packed[:, offset:offset + width])]
where the time goes in v3:
time: 1020 us
  waiting for transfers between devices  373 us (37%)
  matrix products  338 us (33%)
  other arithmetic  147 us (14%)
  local copies, waits for them, and re-layouts  143 us (14%)
  between operations  15.4 us (2%)
    reduce_scatter x2, waiting for transfers between devices, scatter_columns(): summed = lax.psum_scatter(packed, ALL, scatter_dimension=0, tiled=True)  307 us
    all_gather x2, waiting for transfers between devices, gather_columns(): full = lax.all_gather(packed[None], ALL, axis=0, tiled=True)  65.3 us
    convert_element_type x2, other arithmetic, attend_backward(): score_grad = (probs * (upward - inner)).astype(jnp.bfloat16)  55.6 us
    dot_general x2, matrix products, attend_backward(): jnp.einsum('qhd,khd->hqk', upstream_rows, values, preferred_element_type=...  49.4 us
    concatenate x3, local copies, waits for them, and re-layouts, pad_columns(): return jnp.concatenate(blocks, axis=1)  42.6 us
    dot_general x2, matrix products, attend_backward(): jnp.einsum('hqk,qhd->khd', probs.astype(jnp.bfloat16), upstream_rows, pre...  32.4 us
    dot_general x2, matrix products, attend_forward(): jnp.einsum('hqk,khd->qhd', probs, values, preferred_element_type=jnp.floa...  29.8 us
    dot_general x2, matrix products, attend_forward(): jnp.einsum('qhd,khd->hqk', query[first:first + block], keys, preferred_el...  29.7 us
  transfers between devices with their start and end apart: 4, of which 3 were waited for; matrix products, arithmetic and copies ran while one was open for 19% of the time, Pallas kernels for 0%

profile of v3, /device:TPU:0, one launch (start us, length us, event | category | flops | bytes accessed | tf_op | source)
XLA Modules:
  0.0 1016.8 jit_solution(385937009743786415)
XLA Ops:
  21.7 65.3 %all-gather.5.cloned.1.call-done = bf16[1024,3456]{1,0:T(8,128)(2,1)} async-done(((bf16[32,3456]{1,0:T(8,128)(2,1)}), bf16[1024,3456]{1,0:T(8,128)(2,1)}) %all-gather.5.cloned.1.call-update) | async-done | bytes 7077904 | tf_op jit(solution)/shard_map/all_gather | solution.py:134
  150.8 15.5 %fusion.109 = (f32[16,512]{1,0:T(8,128)S(1)}, f32[16,512,1024]{2,1,0:T(8,128)}) fusion(bf16[1024,16,32]{0,2,1:T(8,128)(2,1)S(1)} %fusion.79, bf16[1024,16,32]{0,2,1:T(8,128)(2,1)S(1)} %concatenate.62, bf16[1,1024,16,32]{1,3,2,0:T(8,128)(2,1)S(1)} %slice.254, bf16[1,1024,16,32]{1,3,2,0:T(8,128)(2,1)S(1)} %concatenate.60, ...), kind=kOutput, calls=%fused_computation.175 | convolution fusion | flops 1105190912 | bytes 38305792 | tf_op jit(solution)/shard_map/while/body/eval_jaxpr/qhd,khd->hqk/dot_general | solution.py:52
  166.3 14.4 %fusion.1 = f32[16,512]{1,0:T(8,128)S(1)} fusion(f32[16,512,1024]{2,1,0:T(8,128)} %get-tuple-element.99, f32[16,512]{1,0:T(8,128)S(1)} %get-tuple-element.98), kind=kLoop, calls=%fused_computation.13 | loop fusion | flops 16769024 | bytes 33619968 | tf_op jit(solution)/shard_map/while/body/eval_jaxpr/reduce_sum | solution.py:58
  181.4 14.3 %fusion.110 = (f32[16,512]{1,0:T(8,128)S(1)}, f32[16,512,1024]{2,1,0:T(8,128)}) fusion(bf16[1024,16,32]{0,2,1:T(8,128)(2,1)S(1)} %fusion.79, bf16[1024,16,32]{0,2,1:T(8,128)(2,1)S(1)} %concatenate.62, bf16[1,1024,16,32]{1,3,2,0:T(8,128)(2,1)S(1)} %concatenate.60, bf16[1,1024,16,32]{1,3,2,0:T(8,128)(2,1)S(1)} %slice.254, pred[512,1024]{1,0:T(8,128)(4,1)S(1)} %copy-done.30), kind=kOutput, calls=%fused_computation.176 | convolution fusion | flops 1105190912 | bytes 38305792 | tf_op jit(solution)/shard_map/while/body/eval_jaxpr/qhd,khd->hqk/dot_general | solution.py:52
  195.7 15.3 %fusion = f32[16,512]{1,0:T(8,128)S(1)} fusion(f32[16,512,1024]{2,1,0:T(8,128)} %get-tuple-element.101, f32[16,512]{1,0:T(8,128)S(1)} %get-tuple-element.100), kind=kLoop, calls=%fused_computation.12 | loop fusion | flops 16769024 | bytes 33619968 | tf_op jit(solution)/shard_map/while/body/eval_jaxpr/reduce_sum | solution.py:58
  211.6 16.0 %fusion.75 = bf16[16,64,512]{2,1,0:T(8,128)(2,1)S(1)} fusion(f32[16,512,1024]{2,1,0:T(8,128)} %get-tuple-element.99, f32[16,512]{1,0:T(8,128)S(1)} %fusion.1, f32[16,512]{1,0:T(8,128)S(1)} %get-tuple-element.98, f32[1,1024,3,16,64]{1,4,3,2,0:T(8,128)} %copy-done), kind=kOutput, calls=%fused_computation.113 | convolution fusion | flops 1099431936 | bytes 36765696 | tf_op jit(solution)/shard_map/while/body/eval_jaxpr/hqk,khd->qhd/dot_general | solution.py:61
  227.7 13.8 %fusion.76 = bf16[16,64,512]{2,1,0:T(8,128)(2,1)S(1)} fusion(f32[16,512,1024]{2,1,0:T(8,128)} %get-tuple-element.101, f32[16,512]{1,0:T(8,128)S(1)} %fusion, f32[16,512]{1,0:T(8,128)S(1)} %get-tuple-element.100, f32[1,1024,3,16,64]{1,4,3,2,0:T(8,128)S(1)} %bitcast.198), kind=kOutput, calls=%fused_computation.114 | convolution fusion | flops 1099431936 | bytes 36765696 | tf_op jit(solution)/shard_map/while/body/eval_jaxpr/hqk,khd->qhd/dot_general | solution.py:61
  253.0 14.1 %reshape.598 = bf16[4096,1024]{1,0:T(8,128)(2,1)} reshape(bf16[1024,4096]{1,0:T(8,128)(2,1)} %slice.174) | data formatting | bytes 16777216 | tf_op jit(solution)/shard_map/reshape | solution.py:180
  267.1 15.1 %fusion.24 = f32[1024,4096]{1,0:T(8,128)} fusion(bf16[1024,9216]{1,0:T(8,128)(2,1)} %all-gather.7.cloned.1.call-done, bf16[1,1024,1024]{2,1,0:T(8,128)(2,1)S(1)} %copy-done.2, f32[1024]{0:T(1024)S(1)} %copy-done.46, f32[1024]{0:T(1024)S(1)} %copy-done.35, f32[1024]{0:T(1024)S(1)} %copy-done.38, f32[1024]{0:T(1024)S(1)} %copy-done.32), kind=kOutput, calls=%fused_computation.42 | convolution fusion | flops 8596226048 | bytes 27279360 | tf_op jit(solution)/shard_map/dot_general | solution.py:200
  282.2 18.5 %convolution_convert_fusion = bf16[4096,1024]{1,0:T(8,128)(2,1)} fusion(bf16[1,1024,1024]{2,1,0:T(8,128)(2,1)S(1)} %copy-done.14, f32[1024,4096]{1,0:T(8,128)} %fusion.24, f32[4096]{0:T(1024)S(1)} %copy-done.42), kind=kOutput, calls=%fused_computation.38 | convolution fusion | flops 8636071936 | bytes 27279360 | tf_op jit(solution)/shard_map/tf,td->fd/dot_general | solution.py:214
  300.7 13.9 %reshape.601 = bf16[1024,4096]{1,0:T(8,128)(2,1)} reshape(bf16[4096,1024]{1,0:T(8,128)(2,1)} %convolution_convert_fusion) | data formatting | bytes 16777216 | tf_op jit(solution)/shard_map/reshape | solution.py:229
  314.6 26.0 %fusion.111 = (bf16[4096]{0:T(1024)(128)(2,1)S(1)}, bf16[1024,4096]{1,0:T(8,128)(2,1)}) fusion(f32[1024,4096]{1,0:T(8,128)} %fusion.24, f32[4096]{0:T(1024)S(1)} %copy-done.42, bf16[4096,1024]{1,0:T(8,128)(2,1)} %reshape.598, bf16[1,1024,1024]{2,1,0:T(8,128)(2,1)} %param.21), kind=kOutput, calls=%fused_computation.177 | convolution fusion | flops 8682205184 | bytes 35676160 | tf_op jit(solution)/shard_map/td,fd->tf/dot_general | solution.py:218
  341.2 15.3 %convolution_convert_fusion.1 = bf16[1024,4096]{1,0:T(8,128)(2,1)} fusion(bf16[1024,4096]{1,0:T(8,128)(2,1)} %get-tuple-element.103, bf16[1,1024,1024]{2,1,0:T(8,128)(2,1)S(1)} %copy-done.2, f32[1024]{0:T(1024)S(1)} %copy-done.46, f32[1024]{0:T(1024)S(1)} %copy-done.35, f32[1024]{0:T(1024)S(1)} %copy-done.38, f32[1024]{0:T(1024)S(1)} %copy-done.32), kind=kOutput, calls=%fused_computation.39 | convolution fusion | flops 8600420352 | bytes 18890752 | tf_op jit(solution)/shard_map/te,tf->ef/dot_general | solution.py:222
  356.5 29.8 %concatenate.69 = bf16[1024,9600]{1,0:T(8,128)(2,1)} concatenate(bf16[1024,4096]{1,0:T(8,128)(2,1)} %convolution_convert_fusion.1, bf16[1024,4096]{1,0:T(8,128)(2,1)} %reshape.601, bf16[1024,1024]{1,0:T(8,128)(2,1)} %fusion.66, bf16[1024,4]{1,0:T(8,128)(2,1)S(1)} %reshape.602, bf16[1024,1]{1,0:T(8,128)(2,1)S(1)} %copy-done.25, bf16[1024,379]{1,0:T(8,128)(2,1)S(1)} %broadcast_in_dim.130), dimensions={1} | concatenate | bytes 39321600 | tf_op jit(solution)/shard_map/concatenate | solution.py:120
  391.6 15.7 %fusion.11 = f32[16,64,1024]{2,1,0:T(8,128)} fusion(f32[16,512,1024]{2,1,0:T(8,128)} %get-tuple-element.99, f32[16,512]{1,0:T(8,128)S(1)} %copy-done.23, bf16[1,1024,16,64]{1,3,2,0:T(8,128)(2,1)} %bitcast.201), kind=kOutput, calls=%fused_computation.25 | convolution fusion | flops 1090519040 | bytes 38830080 | tf_op jit(solution)/shard_map/while/body/eval_jaxpr/hqk,qhd->khd/dot_general | solution.py:96
  407.4 25.0 %multiply_reduce_fusion = (f32[16,512]{1,0:T(8,128)S(1)}, f32[16,512,1024]{2,1,0:T(8,128)}) fusion(f32[16,512,1024]{2,1,0:T(8,128)} %get-tuple-element.99, f32[16,512]{1,0:T(8,128)S(1)} %copy-done.23, bf16[1,1024,16,64]{1,3,2,0:T(8,128)(2,1)} %bitcast.202, f32[1,1024,3,16,64]{1,4,3,2,0:T(8,128)} %copy-done), kind=kOutput, calls=%fused_computation.1 | convolution fusion | flops 1098899456 | bytes 70320128 | tf_op jit(solution)/shard_map/while/body/eval_jaxpr/qhd,khd->hqk/dot_general | solution.py:83
  432.5 24.4 %multiply_reduce_fusion.1 = (f32[16,512]{1,0:T(8,128)S(1)}, f32[16,512,1024]{2,1,0:T(8,128)}) fusion(f32[16,512,1024]{2,1,0:T(8,128)} %get-tuple-element.101, f32[16,512]{1,0:T(8,128)S(1)} %copy-done.24, bf16[1,1024,16,64]{1,3,2,0:T(8,128)(2,1)} %bitcast.203, f32[1,1024,3,16,64]{1,4,3,2,0:T(8,128)S(1)} %bitcast.200), kind=kOutput, calls=%fused_computation.4 | convolution fusion | flops 1098899456 | bytes 70320128 | tf_op jit(solution)/shard_map/while/body/eval_jaxpr/qhd,khd->hqk/dot_general | solution.py:83
  456.8 27.8 %multiply_convert_fusion.1 = bf16[16,512,1024]{2,1,0:T(8,128)(2,1)} fusion(f32[16,512,1024]{2,1,0:T(8,128)} %get-tuple-element.107, f32[16,512,1024]{2,1,0:T(8,128)} %get-tuple-element.101, f32[16,512]{1,0:T(8,128)S(1)} %get-tuple-element.106, f32[16,512]{1,0:T(8,128)S(1)} %copy-done.24), kind=kLoop, calls=%fused_computation.3 | loop fusion | flops 33554432 | bytes 83951616 | tf_op jit(solution)/shard_map/while/body/eval_jaxpr/convert_element_type | solution.py:87
  508.2 16.7 %add_bitcast_fusion = bf16[1,1024,1,16,64]{1,4,3,2,0:T(8,128)(2,1)} fusion(f32[16,64,1024]{2,1,0:T(8,128)} %fusion.11, f32[16,512,1024]{2,1,0:T(8,128)} %get-tuple-element.101, f32[16,512]{1,0:T(8,128)S(1)} %copy-done.24, bf16[1,1024,16,64]{1,3,2,0:T(8,128)(2,1)} %bitcast.204), kind=kOutput, calls=%fused_computation.78 | convolution fusion | flops 1092616192 | bytes 40927232 | tf_op jit(solution)/shard_map/while/body/eval_jaxpr/hqk,qhd->khd/dot_general | solution.py:96
  524.9 27.7 %multiply_convert_fusion = bf16[16,512,1024]{2,1,0:T(8,128)(2,1)} fusion(f32[16,512,1024]{2,1,0:T(8,128)} %get-tuple-element.105, f32[16,512,1024]{2,1,0:T(8,128)} %get-tuple-element.99, f32[16,512]{1,0:T(8,128)S(1)} %get-tuple-element.104, f32[16,512]{1,0:T(8,128)S(1)} %copy-done.23), kind=kLoop, calls=%fused_computation | loop fusion | flops 33554432 | bytes 83951616 | tf_op jit(solution)/shard_map/while/body/eval_jaxpr/convert_element_type | solution.py:87
  635.0 14.6 %fusion.106 = (bf16[1024]{0:T(1024)(128)(2,1)S(1)}, f32[1024]{0:T(1024)S(1)}, f32[1024,1024]{1,0:T(8,128)S(1)}) fusion(f32[1024]{0:T(1024)S(1)} %copy-done.36, f32[1024]{0:T(1024)S(1)} %copy-done.33, bf16[1,1024,1024]{2,1,0:T(8,128)(2,1)S(1)} %copy-done.3, f32[1024,1024]{1,0:T(8,128)S(1)} %fusion.26, bf16[1024,4096]{1,0:T(8,128)(2,1)} %get-tuple-element.103, ...), kind=kOutput, calls=%fused_computation.172 | convolution fusion | flops 8597272576 | bytes 27277312 | tf_op jit(solution)/shard_map/tf,ef->te/dot_general | solution.py:236
  674.3 18.3 %fusion.53 = bf16[1,1024,1024]{2,1,0:T(8,128)(2,1)} fusion(f32[1024,1024]{1,0:T(8,128)S(1)} %fusion.73, bf16[1,1024,1024]{2,1,0:T(8,128)(2,1)S(1)} %copy-done.3, f32[1024]{0:T(1024)S(1)} %copy-done.44, bf16[4096,1024]{1,0:T(8,128)(2,1)} %reshape.598, f32[1024,4096]{1,0:T(8,128)} %fusion.24, f32[4096]{0:T(1024)S(1)} %copy-done.43), kind=kOutput, calls=%fused_computation.85 | convolution fusion | flops 8637120512 | bytes 33574912 | tf_op jit(solution)/shard_map/dot_general | solution.py:208
  692.6 93.7 %reduce-scatter.3.cloned.1.call-done = bf16[32,3456]{1,0:T(8,128)(2,1)} async-done(((bf16[1024,3456]{1,0:T(8,128)(2,1)}), bf16[32,3456]{1,0:T(8,128)(2,1)}) %reduce-scatter.3.cloned.1.call-update) | async-done | bytes 221200 | tf_op jit(solution)/shard_map/reduce_scatter | solution.py:140
  789.5 213.5 %reduce-scatter.5.cloned.1.call-done = bf16[32,9600]{1,0:T(8,128)(2,1)} async-done(((bf16[1024,9600]{1,0:T(8,128)(2,1)}), bf16[32,9600]{1,0:T(8,128)(2,1)}) %reduce-scatter.5.cloned.1.call-update) | async-done | bytes 614416 | tf_op jit(solution)/shard_map/reduce_scatter | solution.py:140
  (210 shorter events, 236.7 us)
Async XLA Ops:
  7.2 79.8 %all-gather.5.cloned.1.call-start = ((), (), s32[]{:S(2)}) async-start(), calls=%async_computation.4 | async-start | bytes 7299072 | tf_op jit(solution)/shard_map/all_gather | solution.py:134
  12.1 233.1 %all-gather.7.cloned.1.call-start = ((), (), s32[]{:S(2)}) async-start(), calls=%async_computation.5 | async-start | bytes 19464192 | tf_op jit(solution)/shard_map/all_gather | solution.py:134
  15.2 771.1 %reduce-scatter.3.cloned.1.call-start = ((), (), s32[]{:S(2)}) async-start(), calls=%async_computation.2 | async-start | bytes 7299072 | tf_op jit(solution)/shard_map/reduce_scatter | solution.py:140
  19.2 84.8 %copy-start.31 = (f32[1024]{0:T(1024)}, f32[1024]{0:T(1024)S(1)}, u32[]{:S(2)}) copy-start(f32[1024]{0:T(1024)S(1)} %broadcast_multiply_fusion) | copy-start | bytes 12292
  19.9 73.0 %copy-start.40 = (f32[1024]{0:T(1024)}, f32[1024]{0:T(1024)S(1)}, u32[]{:S(2)}) copy-start(f32[1024]{0:T(1024)S(1)} %fusion.39) | copy-start | bytes 12292
  19.9 84.0 %copy-start.37 = (f32[1024]{0:T(1024)}, f32[1024]{0:T(1024)S(1)}, u32[]{:S(2)}) copy-start(f32[1024]{0:T(1024)S(1)} %fusion.93) | copy-start | bytes 12292
  20.2 113.0 %copy-start.26 = (f32[1024,16]{0,1:T(8,128)}, f32[1024,16]{0,1:T(8,128)S(1)}, u32[]{:S(2)}) copy-start(f32[1024,16]{0,1:T(8,128)S(1)} %get-tuple-element.94) | copy-start | bytes 196612
  20.2 113.0 %copy-start.28 = (f32[1024,16]{0,1:T(8,128)}, f32[1024,16]{0,1:T(8,128)S(1)}, u32[]{:S(2)}) copy-start(f32[1024,16]{0,1:T(8,128)S(1)} %get-tuple-element.95) | copy-start | bytes 196612
  120.3 61.1 %copy-start.4 = (bf16[1,1024,16,32]{1,3,2,0:T(8,128)(2,1)}, bf16[1,1024,16,32]{1,3,2,0:T(8,128)(2,1)S(1)}, u32[]{:S(2)}) copy-start(bf16[1,1024,16,32]{1,3,2,0:T(8,128)(2,1)S(1)} %slice.254) | copy-start | bytes 3145732
  146.6 34.8 %copy-start.6 = (bf16[1,1024,16,32]{1,3,2,0:T(8,128)(2,1)}, bf16[1,1024,16,32]{1,3,2,0:T(8,128)(2,1)S(1)}, u32[]{:S(2)}) copy-start(bf16[1,1024,16,32]{1,3,2,0:T(8,128)(2,1)S(1)} %concatenate.60) | copy-start | bytes 3145732
  148.7 32.7 %copy-start.8 = (bf16[1024,16,32]{0,2,1:T(8,128)(2,1)}, bf16[1024,16,32]{0,2,1:T(8,128)(2,1)S(1)}, u32[]{:S(2)}) copy-start(bf16[1024,16,32]{0,2,1:T(8,128)(2,1)S(1)} %concatenate.62) | copy-start | bytes 3145732
  150.8 30.6 %copy-start.10 = (bf16[1024,16,32]{0,2,1:T(8,128)(2,1)}, bf16[1024,16,32]{0,2,1:T(8,128)(2,1)S(1)}, u32[]{:S(2)}) copy-start(bf16[1024,16,32]{0,2,1:T(8,128)(2,1)S(1)} %fusion.79) | copy-start | bytes 3145732
  195.6 32.0 %slice-start = ((s8[12582912]{0:T(1024)(128)(4,1)}), s8[4194304]{0:T(1024)(128)(4,1)S(1)}, s32[]{:S(2)}) async-start(s8[12582912]{0:T(1024)(128)(4,1)} %bitcast.197), calls=%async_computation.6 | async-start | bytes 8388608
  211.6 16.0 %slice-start.1 = ((s8[12582912]{0:T(1024)(128)(4,1)}), s8[4194304]{0:T(1024)(128)(4,1)S(1)}, s32[]{:S(2)}) async-start(s8[12582912]{0:T(1024)(128)(4,1)} %bitcast.197), calls=%async_computation.7 | async-start | bytes 8388608
  211.6 16.1 %slice-start.2 = ((s8[12582912]{0:T(1024)(128)(4,1)}), s8[4194304]{0:T(1024)(128)(4,1)S(1)}, s32[]{:S(2)}) async-start(s8[12582912]{0:T(1024)(128)(4,1)} %bitcast.197), calls=%async_computation.8 | async-start | bytes 8388608
  341.2 15.3 %copy-start.25 = (bf16[1024,1]{1,0:T(8,128)(2,1)S(1)}, bf16[1024,1]{1,0:T(8,128)(2,1)}, u32[]{:S(2)}) copy-start(bf16[1024,1]{1,0:T(8,128)(2,1)} %reshape.639) | copy-start | bytes 6148
  356.5 29.8 %copy-start.15 = (bf16[1,1024,1024]{2,1,0:T(8,128)(2,1)S(1)}, bf16[1,1024,1024]{2,1,0:T(8,128)(2,1)}, u32[]{:S(2)}) copy-start(bf16[1,1024,1024]{2,1,0:T(8,128)(2,1)} %param.21) | copy-start | bytes 6291460
  391.6 40.8 %slice-start.3 = ((s8[12582912]{0:T(1024)(128)(4,1)}), s8[4194304]{0:T(1024)(128)(4,1)S(1)}, s32[]{:S(2)}) async-start(s8[12582912]{0:T(1024)(128)(4,1)} %bitcast.199), calls=%async_computation.9 | async-start | bytes 8388608
  407.4 25.1 %slice-start.4 = ((s8[12582912]{0:T(1024)(128)(4,1)}), s8[4194304]{0:T(1024)(128)(4,1)S(1)}, s32[]{:S(2)}) async-start(s8[12582912]{0:T(1024)(128)(4,1)} %bitcast.199), calls=%async_computation.10 | async-start | bytes 8388608
  407.4 25.1 %slice-start.5 = ((s8[12582912]{0:T(1024)(128)(4,1)}), s8[4194304]{0:T(1024)(128)(4,1)S(1)}, s32[]{:S(2)}) async-start(s8[12582912]{0:T(1024)(128)(4,1)} %bitcast.199), calls=%async_computation.11 | async-start | bytes 8388608
  407.4 25.1 %copy-start.24 = (f32[16,512]{1,0:T(8,128)S(1)}, f32[16,512]{1,0:T(8,128)}, u32[]{:S(2)}) copy-start(f32[16,512]{1,0:T(8,128)} %log_add_fusion.1) | copy-start | bytes 98308
  456.8 27.9 %copy-start.9 = (bf16[1024,16,32]{0,2,1:T(8,128)(2,1)S(1)}, bf16[1024,16,32]{0,2,1:T(8,128)(2,1)}, u32[]{:S(2)}) copy-start(bf16[1024,16,32]{0,2,1:T(8,128)(2,1)} %copy-done.8) | copy-start | bytes 3145732
  611.8 16.5 %slice-start.6 = ((s8[7077888]{0:T(1024)(128)(4,1)}), s8[2883584]{0:T(1024)(128)(4,1)S(1)}, s32[]{:S(2)}) async-start(s8[7077888]{0:T(1024)(128)(4,1)} %bitcast.205), calls=%async_computation.12 | async-start | bytes 5767168
  665.6 337.4 %reduce-scatter.5.cloned.1.call-start = ((), (), s32[]{:S(2)}) async-start(), calls=%async_computation.3 | async-start | bytes 20275200 | tf_op jit(solution)/shard_map/reduce_scatter | solution.py:140
  (39 other events, 332.0 us)
Sparse Core Ops, SparseCore 0:
  12.3 74.7 all-gather.4
  90.0 122.4 all-gather.6
  665.7 120.5 reduce-scatter.2
  792.6 210.3 reduce-scatter.4

commit v4 on v3

--- a/solution.py
+++ b/solution.py
@@ -3,6 +3,8 @@
 import jax
 import jax.numpy as jnp
 from jax import lax
+from jax.experimental import pallas as pl
+from jax.experimental.pallas import tpu as pltpu
 from jax.sharding import PartitionSpec as P
 
 
@@ -36,70 +38,164 @@
     return jnp.concatenate([turned.reshape(field.shape[:-1] + (ROT,)), field[..., ROT:]], axis=-1)
 
 
-def allowed_keys(first, count, length, seq_len):
-    query_place = first + jnp.arange(count)[:, None]
-    key_place = jnp.arange(seq_len)[None, :]
-    return (key_place <= query_place) & (key_place < length)
-
-
-def attend_forward(item):
-    query, keys, values, length = item
-    seq_len = keys.shape[0]
-    block = min(512, seq_len)
-    results = []
-    logsums = []
-    for first in range(0, seq_len, block):
-        scores = jnp.einsum(
-            "qhd,khd->hqk", query[first : first + block], keys, preferred_element_type=jnp.float32
-        ) * HEAD_DIM ** (-0.5)
-        masked = jnp.where(allowed_keys(first, block, length, seq_len)[None], scores, -1000000000.0)
+QUERY_BLOCK = 256
+NT = (((1,), (1,)), ((), ()))
+TN = (((0,), (0,)), ((), ()))
+
+
+def head_scores(q, k, first, length, lane_mask):
+    scores = lax.dot_general(
+        jnp.where(lane_mask, q, jnp.zeros_like(q)), k, NT, preferred_element_type=jnp.float32
+    ) * HEAD_DIM ** (-0.5)
+    query_place = first + lax.broadcasted_iota(jnp.int32, scores.shape, 0)
+    key_place = lax.broadcasted_iota(jnp.int32, scores.shape, 1)
+    allowed = (key_place <= query_place) & (key_place < length)
+    return jnp.where(allowed, scores, -1000000000.0)
+
+
+def attention_forward_kernel(length_ref, q_ref, k_ref, v_ref, o_ref, top_ref, total_ref):
+    block = q_ref.shape[0]
+    first = pl.program_id(1) * block
+    length = length_ref[0]
+    q = q_ref[...]
+    k = k_ref[...]
+    v = v_ref[...]
+    lanes = lax.broadcasted_iota(jnp.int32, q.shape, 1)
+    result = None
+    for head in range(2):
+        lane_mask = (lanes >= head * HEAD_DIM) & (lanes < (head + 1) * HEAD_DIM)
+        masked = head_scores(q, k, first, length, lane_mask)
         top = jnp.max(masked, axis=-1, keepdims=True)
         weights = jnp.exp(masked - top)
         total = jnp.sum(weights, axis=-1, keepdims=True)
         probs = (weights / total).astype(jnp.bfloat16)
-        results.append(
-            jnp.einsum("hqk,khd->qhd", probs, values, preferred_element_type=jnp.float32)
-        )
-        logsums.append(top + jnp.log(total))
-    return (jnp.concatenate(results, axis=0).astype(jnp.bfloat16), jnp.concatenate(logsums, axis=1))
-
-
-def attend_backward(item):
-    query, keys, values, upstream, logsum, length = item
-    seq_len = keys.shape[0]
-    block = min(512, seq_len)
+        out = jnp.dot(probs, v, preferred_element_type=jnp.float32)
+        result = out if result is None else jnp.where(lane_mask, out, result)
+        top_ref[head] = top
+        total_ref[head] = total
+    o_ref[...] = result.astype(o_ref.dtype)
+
+
+def attention_backward_kernel(
+    length_ref, q_ref, k_ref, v_ref, g_ref, top_ref, total_ref, dq_ref, dk_ref, dv_ref
+):
+    block = q_ref.shape[0]
+    step = pl.program_id(1)
+    first = step * block
+    length = length_ref[0]
     scale = HEAD_DIM ** (-0.5)
-    query_parts = []
-    key_grad = jnp.zeros(keys.shape, jnp.float32)
-    value_grad = jnp.zeros(values.shape, jnp.float32)
-    for first in range(0, seq_len, block):
-        query_rows = query[first : first + block]
-        upstream_rows = upstream[first : first + block]
-        scores = (
-            jnp.einsum("qhd,khd->hqk", query_rows, keys, preferred_element_type=jnp.float32) * scale
-        )
-        masked = jnp.where(allowed_keys(first, block, length, seq_len)[None], scores, -1000000000.0)
-        probs = jnp.exp(masked - logsum[:, first : first + block])
-        upward = jnp.einsum(
-            "qhd,khd->hqk", upstream_rows, values, preferred_element_type=jnp.float32
+
+    @pl.when(step == 0)
+    def _():
+        dk_ref[...] = jnp.zeros_like(dk_ref)
+        dv_ref[...] = jnp.zeros_like(dv_ref)
+
+    q = q_ref[...]
+    k = k_ref[...]
+    v = v_ref[...]
+    g = g_ref[...]
+    lanes = lax.broadcasted_iota(jnp.int32, q.shape, 1)
+    key_lanes = lax.broadcasted_iota(jnp.int32, k.shape, 1)
+    dq = None
+    dk = None
+    dv = None
+    for head in range(2):
+        lane_mask = (lanes >= head * HEAD_DIM) & (lanes < (head + 1) * HEAD_DIM)
+        key_mask = (key_lanes >= head * HEAD_DIM) & (key_lanes < (head + 1) * HEAD_DIM)
+        masked = head_scores(q, k, first, length, lane_mask)
+        probs = jnp.exp(masked - top_ref[head]) / total_ref[head]
+        upward = lax.dot_general(
+            jnp.where(lane_mask, g, jnp.zeros_like(g)), v, NT, preferred_element_type=jnp.float32
         )
         inner = jnp.sum(probs * upward, axis=-1, keepdims=True)
         score_grad = (probs * (upward - inner)).astype(jnp.bfloat16)
-        query_parts.append(
-            jnp.einsum("hqk,khd->qhd", score_grad, keys, preferred_element_type=jnp.float32) * scale
+        dq_head = jnp.dot(score_grad, k, preferred_element_type=jnp.float32) * scale
+        dk_head = lax.dot_general(score_grad, q, TN, preferred_element_type=jnp.float32) * scale
+        dv_head = lax.dot_general(
+            probs.astype(jnp.bfloat16), g, TN, preferred_element_type=jnp.float32
         )
-        key_grad = (
-            key_grad
-            + jnp.einsum("hqk,qhd->khd", score_grad, query_rows, preferred_element_type=jnp.float32)
-            * scale
-        )
-        value_grad = value_grad + jnp.einsum(
-            "hqk,qhd->khd",
-            probs.astype(jnp.bfloat16),
-            upstream_rows,
-            preferred_element_type=jnp.float32,
-        )
-    return (jnp.concatenate(query_parts, axis=0), key_grad, value_grad)
+        if dq is None:
+            dq, dk, dv = dq_head, dk_head, dv_head
+        else:
+            dq = jnp.where(lane_mask, dq_head, dq)
+            dk = jnp.where(key_mask, dk_head, dk)
+            dv = jnp.where(key_mask, dv_head, dv)
+    dq_ref[...] = dq
+    dk_ref[...] += dk
+    dv_ref[...] += dv
+
+
+def attention_forward(q, k, v, length):
+    seq, width = q.shape
+    pairs = width // (2 * HEAD_DIM)
+    block = min(QUERY_BLOCK, seq)
+    grid = (pairs, seq // block)
+    lane = 2 * HEAD_DIM
+    return pl.pallas_call(
+        attention_forward_kernel,
+        out_shape=(
+            jax.ShapeDtypeStruct((seq, width), jnp.bfloat16),
+            jax.ShapeDtypeStruct((2 * pairs, seq, 1), jnp.float32),
+            jax.ShapeDtypeStruct((2 * pairs, seq, 1), jnp.float32),
+        ),
+        grid_spec=pltpu.PrefetchScalarGridSpec(
+            num_scalar_prefetch=1,
+            grid=grid,
+            in_specs=[
+                pl.BlockSpec((block, lane), lambda p, i, n: (i, p)),
+                pl.BlockSpec((seq, lane), lambda p, i, n: (0, p)),
+                pl.BlockSpec((seq, lane), lambda p, i, n: (0, p)),
+            ],
+            out_specs=[
+                pl.BlockSpec((block, lane), lambda p, i, n: (i, p)),
+                pl.BlockSpec((2, block, 1), lambda p, i, n: (p, i, 0)),
+                pl.BlockSpec((2, block, 1), lambda p, i, n: (p, i, 0)),
+            ],
+        ),
+        compiler_params=pltpu.CompilerParams(dimension_semantics=("parallel", "arbitrary")),
+        cost_estimate=pl.CostEstimate(
+            flops=8 * seq * seq * width, transcendentals=seq * seq * pairs * 2,
+            bytes_accessed=2 * seq * width * 2 * (1 + 2 * seq // block),
+        ),
+    )(length, q, k, v)
+
+
+def attention_backward(q, k, v, g, top, total, length):
+    seq, width = q.shape
+    pairs = width // (2 * HEAD_DIM)
+    block = min(QUERY_BLOCK, seq)
+    grid = (pairs, seq // block)
+    lane = 2 * HEAD_DIM
+    return pl.pallas_call(
+        attention_backward_kernel,
+        out_shape=(
+            jax.ShapeDtypeStruct((seq, width), jnp.float32),
+            jax.ShapeDtypeStruct((seq, width), jnp.float32),
+            jax.ShapeDtypeStruct((seq, width), jnp.float32),
+        ),
+        grid_spec=pltpu.PrefetchScalarGridSpec(
+            num_scalar_prefetch=1,
+            grid=grid,
+            in_specs=[
+                pl.BlockSpec((block, lane), lambda p, i, n: (i, p)),
+                pl.BlockSpec((seq, lane), lambda p, i, n: (0, p)),
+                pl.BlockSpec((seq, lane), lambda p, i, n: (0, p)),
+                pl.BlockSpec((block, lane), lambda p, i, n: (i, p)),
+                pl.BlockSpec((2, block, 1), lambda p, i, n: (p, i, 0)),
+                pl.BlockSpec((2, block, 1), lambda p, i, n: (p, i, 0)),
+            ],
+            out_specs=[
+                pl.BlockSpec((block, lane), lambda p, i, n: (i, p)),
+                pl.BlockSpec((seq, lane), lambda p, i, n: (0, p)),
+                pl.BlockSpec((seq, lane), lambda p, i, n: (0, p)),
+            ],
+        ),
+        compiler_params=pltpu.CompilerParams(dimension_semantics=("parallel", "arbitrary")),
+        cost_estimate=pl.CostEstimate(
+            flops=20 * seq * seq * width, transcendentals=seq * seq * pairs * 2,
+            bytes_accessed=2 * seq * width * 2 * (2 + 2 * seq // block) + 3 * seq * width * 4,
+        ),
+    )(length, q, k, v, g, top, total)
 
 
 def gelu_tanh(inner):
@@ -195,8 +291,14 @@
     query_low = query.astype(jnp.bfloat16)
     keys_low = keys.astype(jnp.bfloat16)
     values_low = triple[:, :, 2].astype(jnp.bfloat16)
-    attended, logsums = lax.map(attend_forward, (query_low, keys_low, values_low, lengths))
-    mixed_low = attended.reshape(positions, width)
+    flat_query = query_low.reshape(seq_dev, seq_len, width)
+    flat_keys = keys_low.reshape(seq_dev, seq_len, width)
+    flat_values = values_low.reshape(seq_dev, seq_len, width)
+    forward_parts = [
+        attention_forward(flat_query[s], flat_keys[s], flat_values[s], lengths[s : s + 1])
+        for s in range(seq_dev)
+    ]
+    mixed_low = jnp.concatenate([part[0] for part in forward_parts], axis=0)
     hidden = jnp.dot(
         normed_low, expand_full, preferred_element_type=jnp.float32
     ) + inner_full.astype(jnp.float32)
@@ -237,7 +339,7 @@
         "tf,ef->te", hidden_grad, expand_full, preferred_element_type=jnp.float32
     )
     mixed_grad = jnp.einsum("td,ed->te", upstream, project_full, preferred_element_type=jnp.float32)
-    mixed_grad = mixed_grad.astype(jnp.bfloat16).reshape(seq_dev, seq_len, HEADS, HEAD_DIM)
+    mixed_grad = mixed_grad.astype(jnp.bfloat16).reshape(seq_dev, seq_len, width)
     early_packed, mixed_grad = lax.optimization_barrier((early_packed, mixed_grad))
     expand_part, contract_part, project_part, inner_part, outer_part = scatter_columns(
         early_packed, early_widths
@@ -245,8 +347,21 @@
     contract_part = contract_part.reshape(-1, width)
     inner_part = inner_part.reshape(-1)
     outer_part = outer_part.reshape(-1)
-    query_grad, key_grad, value_grad = lax.map(
-        attend_backward, (query_low, keys_low, values_low, mixed_grad, logsums, lengths)
+    backward_parts = [
+        attention_backward(
+            flat_query[s],
+            flat_keys[s],
+            flat_values[s],
+            mixed_grad[s],
+            forward_parts[s][1],
+            forward_parts[s][2],
+            lengths[s : s + 1],
+        )
+        for s in range(seq_dev)
+    ]
+    query_grad, key_grad, value_grad = (
+        jnp.stack([part[j] for part in backward_parts]).reshape(seq_dev, seq_len, HEADS, HEAD_DIM)
+        for j in range(3)
     )
     query_turned, key_turned = turn_pull((query_grad, key_grad))
     triple_grad = (

time: 1020 us -> 874 us (0.86)
  matrix products: 338 us -> 155 us
  Pallas kernels: 0 us -> 133 us
  other arithmetic: 147 us -> 30.1 us
  local copies, waits for them, and re-layouts: 143 us -> 160 us
    dot_general x12 -> x0, matrix products: 188 us -> none  [the longest x2 49.4 us: attend_backward(): jnp.einsum('qhd,khd->hqk', upstream_rows, values, preferred_element_type=...]
    pallas_call x0 -> x2, Pallas kernels: none -> 133 us  [the longest x1 78.7 us: attention_backward(): pl.pallas_call(attention_backward_kernel, out_shape=(jax.ShapeDtypeStruct...]
    convert_element_type x2 -> x0, other arithmetic: 55.6 us -> none  [attend_backward(): score_grad = (probs * (upward - inner)).astype(jnp.bfloat16)]
    reduce_sum x2 -> x0, other arithmetic: 29.7 us -> none  [attend_forward(): total = jnp.sum(weights, axis=-1, keepdims=True)]
    pallas_call x0 -> x3, local copies, waits for them, and re-layouts: none -> 15.8 us  [attention_backward(): pl.pallas_call(attention_backward_kernel, out_shape=(jax.ShapeDtypeStruct...]
    convert_element_type x0 -> x3, local copies, waits for them, and re-layouts: none -> 12.3 us  [the longest x1 4.44 us: body(): values_low = triple[:, :, 2].astype(jnp.bfloat16)]
  transfers between devices with their start and end apart: 4 -> 4, of which waited for: 3 -> 4; matrix products, arithmetic and copies ran while one was open for 19% -> 12% of each run, Pallas kernels for 0% -> 6%
where the time goes in v4:
time: 874 us; the launch traced here: 868 us
  waiting for transfers between devices  375 us (43%)
  local copies, waits for them, and re-layouts  160 us (18%)
  matrix products  155 us (18%)
  Pallas kernels  133 us (15%)
  other arithmetic  30.1 us (3%)
  between operations  15.1 us (2%)
    reduce_scatter x2, waiting for transfers between devices, scatter_columns(): summed = lax.psum_scatter(packed, ALL, scatter_dimension=0, tiled=True)  305 us
    pallas_call x1, Pallas kernels, attention_backward(): pl.pallas_call(attention_backward_kernel, out_shape=(jax.ShapeDtypeStruct...  78.7 us
    all_gather x2, waiting for transfers between devices, gather_columns(): full = lax.all_gather(packed[None], ALL, axis=0, tiled=True)  69.2 us
    pallas_call x1, Pallas kernels, attention_forward(): pl.pallas_call(attention_forward_kernel, out_shape=(jax.ShapeDtypeStruct(...  54.1 us
    concatenate x3, local copies, waits for them, and re-layouts, pad_columns(): return jnp.concatenate(blocks, axis=1)  42.5 us
    dot_general x1, matrix products, body(): jnp.einsum('td,fd->tf', upstream, contract_full, preferred_element_type=j...  25 us
    dot_general x1, matrix products, body(): jnp.einsum('tf,td->fd', active_low, upstream, preferred_element_type=jnp....  18.6 us
    dot_general x1, matrix products, body(): jnp.dot(active_low, contract_full, preferred_element_type=jnp.float32)  18.4 us
  transfers between devices with their start and end apart: 4, of which 4 were waited for; matrix products, arithmetic and copies ran while one was open for 12% of the time, Pallas kernels for 6%

profile of v4, /device:TPU:0, one launch (start us, length us, event | category | flops | bytes accessed | tf_op | source)
XLA Modules:
  0.0 868.3 jit_solution(6871042498067438889)
XLA Ops:
  20.2 66.9 %all-gather.5.cloned.1.call-done = bf16[1024,3456]{1,0:T(8,128)(2,1)} async-done(((bf16[32,3456]{1,0:T(8,128)(2,1)}), bf16[1024,3456]{1,0:T(8,128)(2,1)}) %all-gather.5.cloned.1.call-update) | async-done | bytes 7077904 | tf_op jit(solution)/shard_map/all_gather | solution.py:230
  87.0 5.9 slice_bitcast_fusion
  92.9 9.0 %copy.39 = bf16[3072,1024]{1,0:T(8,128)(2,1)} copy(bf16[3072,1024]{0,1:T(8,128)(2,1)} %slice_bitcast_fusion) | data formatting | bytes 12582912 | tf_op jit(solution)/shard_map/dot_general | solution.py:282
  104.2 13.0 %convolution_bitcast_fusion = f32[1,1024,3,16,64]{1,4,3,2,0:T(8,128)} fusion(bf16[3,16,64,1024]{3,2,1,0:T(8,128)(2,1)} %bitcast.147, bf16[1,1024,1024]{2,1,0:T(8,128)(2,1)S(1)} %copy-done, f32[1024]{0:T(1024)S(1)} %get-tuple-element.27, f32[1024]{0:T(1024)S(1)} %get-tuple-element.28, f32[1024]{0:T(1024)S(1)} %fusion.57, f32[1024]{0:T(1024)S(1)} %broadcast_multiply_fusion), kind=kOutput, calls=%fused_computation.38 | convolution fusion | flops 6448742400 | bytes 20987904 | tf_op jit(solution)/shard_map/dot_general | solution.py:282
  150.2 54.1 %shard_map.186 = (bf16[1024,1024]{1,0:T(8,128)(2,1)}, f32[16,1024,1]{2,1,0:T(8,128)}, f32[16,1024,1]{2,1,0:T(8,128)}) custom-call(s32[1]{0:T(128)S(6)} %copy.71.length_ref, bf16[1024,1024]{1,0:T(8,128)(2,1)} %copy.46.q_ref, bf16[1024,1024]{1,0:T(8,128)(2,1)} %copy.47.k_ref, bf16[1024,1024]{1,0:T(8,128)(2,1)} %copy.48.v_ref), custom_call_target="tpu_custom_call" | custom-call | flops 8589934592 | bytes 37748736 | tf_op jit(solution)/shard_map/pallas_call | solution.py:134
  204.3 5.9 fusion.49
  212.6 7.7 slice.128
  220.3 13.9 %reshape.467 = bf16[4096,1024]{1,0:T(8,128)(2,1)} reshape(bf16[1024,4096]{1,0:T(8,128)(2,1)} %slice.128) | data formatting | bytes 16777216 | tf_op jit(solution)/shard_map/reshape | solution.py:276
  234.2 15.0 %fusion.12 = f32[1024,4096]{1,0:T(8,128)} fusion(bf16[1024,9216]{1,0:T(8,128)(2,1)} %all-gather.7.cloned.1.call-done, bf16[1,1024,1024]{2,1,0:T(8,128)(2,1)S(1)} %copy-done, f32[1024]{0:T(1024)S(1)} %get-tuple-element.27, f32[1024]{0:T(1024)S(1)} %get-tuple-element.28, f32[1024]{0:T(1024)S(1)} %fusion.57, f32[1024]{0:T(1024)S(1)} %broadcast_multiply_fusion), kind=kOutput, calls=%fused_computation.20 | convolution fusion | flops 8596226048 | bytes 27279360 | tf_op jit(solution)/shard_map/dot_general | solution.py:302
  249.2 18.6 %convolution_convert_fusion = bf16[4096,1024]{1,0:T(8,128)(2,1)} fusion(bf16[1,1024,1024]{2,1,0:T(8,128)(2,1)S(1)} %copy-done.3, f32[1024,4096]{1,0:T(8,128)} %fusion.12, f32[4096]{0:T(1024)S(1)} %reshape.491), kind=kOutput, calls=%fused_computation.16 | convolution fusion | flops 8636071936 | bytes 27279360 | tf_op jit(solution)/shard_map/tf,td->fd/dot_general | solution.py:316
  267.8 25.0 %fusion.66 = (bf16[4096]{0:T(1024)(128)(2,1)S(1)}, bf16[1024,4096]{1,0:T(8,128)(2,1)}) fusion(f32[1024,4096]{1,0:T(8,128)} %fusion.12, f32[4096]{0:T(1024)S(1)} %reshape.491, bf16[4096,1024]{1,0:T(8,128)(2,1)} %reshape.467, bf16[1,1024,1024]{2,1,0:T(8,128)(2,1)S(1)} %copy-done.3), kind=kOutput, calls=%fused_computation.115 | convolution fusion | flops 8682205184 | bytes 35676160 | tf_op jit(solution)/shard_map/td,fd->tf/dot_general | solution.py:320
  292.8 15.3 %convolution_convert_fusion.1 = bf16[1024,4096]{1,0:T(8,128)(2,1)} fusion(bf16[1024,4096]{1,0:T(8,128)(2,1)} %get-tuple-element.58, bf16[1,1024,1024]{2,1,0:T(8,128)(2,1)S(1)} %copy-done, f32[1024]{0:T(1024)S(1)} %get-tuple-element.27, f32[1024]{0:T(1024)S(1)} %get-tuple-element.28, f32[1024]{0:T(1024)S(1)} %fusion.57, f32[1024]{0:T(1024)S(1)} %broadcast_multiply_fusion), kind=kOutput, calls=%fused_computation.17 | convolution fusion | flops 8600420352 | bytes 18890752 | tf_op jit(solution)/shard_map/te,tf->ef/dot_general | solution.py:324
  308.1 13.9 %reshape.470 = bf16[1024,4096]{1,0:T(8,128)(2,1)} reshape(bf16[4096,1024]{1,0:T(8,128)(2,1)} %convolution_convert_fusion) | data formatting | bytes 16777216 | tf_op jit(solution)/shard_map/reshape | solution.py:331
  322.7 29.6 %concatenate.40 = bf16[1024,9600]{1,0:T(8,128)(2,1)} concatenate(bf16[1024,4096]{1,0:T(8,128)(2,1)} %convolution_convert_fusion.1, bf16[1024,4096]{1,0:T(8,128)(2,1)} %reshape.470, bf16[1024,1024]{1,0:T(8,128)(2,1)} %fusion.49, bf16[1024,4]{1,0:T(8,128)(2,1)S(1)} %reshape.471, bf16[1024,1]{1,0:T(8,128)(2,1)S(1)} %copy-done.8, bf16[1024,379]{1,0:T(8,128)(2,1)S(1)} %broadcast_in_dim.17), dimensions={1} | concatenate | bytes 39321600 | tf_op jit(solution)/shard_map/concatenate | solution.py:216
  352.3 5.9 convert_bitcast_fusion.1
  358.2 78.7 %shard_map.187 = (f32[1024,1024]{1,0:T(8,128)}, f32[1024,1024]{1,0:T(8,128)}, f32[1024,1024]{1,0:T(8,128)}) custom-call(s32[1]{0:T(128)S(6)} %copy.71.length_ref, bf16[1024,1024]{1,0:T(8,128)(2,1)} %copy.46.q_ref, bf16[1024,1024]{1,0:T(8,128)(2,1)} %copy.47.k_ref, bf16[1024,1024]{1,0:T(8,128)(2,1)} %copy.48.v_ref, bf16[1024,1024]{1,0:T(8,128)(2,1)} %bitcast.153, ...), custom_call_target="tpu_custom_call" | custom-call | flops 21474836480 | bytes 54525952 | tf_op jit(solution)/shard_map/pallas_call | solution.py:169
  441.5 5.7 copy.55
  470.2 9.9 %convolution_convert_fusion.2 = bf16[1024,3072]{1,0:T(8,128)(2,1)} fusion(bf16[1024,3072]{0,1:T(8,128)(2,1)S(1)} %bitcast.145, bf16[1,1024,1024]{2,1,0:T(8,128)(2,1)S(1)} %copy-done, f32[1024]{0:T(1024)S(1)} %get-tuple-element.27, f32[1024]{0:T(1024)S(1)} %get-tuple-element.28, f32[1024]{0:T(1024)S(1)} %fusion.57, f32[1024]{0:T(1024)S(1)} %broadcast_multiply_fusion), kind=kOutput, calls=%fused_computation.26 | convolution fusion | flops 6451888128 | bytes 14696448 | tf_op jit(solution)/shard_map/te,tc->ec/dot_general | solution.py:372
  480.1 8.4 fusion.14
  488.5 14.9 %fusion.63 = (bf16[1024]{0:T(1024)(128)(2,1)S(1)}, f32[1024]{0:T(1024)S(1)}, f32[1024,1024]{1,0:T(8,128)S(1)}) fusion(f32[1024]{0:T(1024)S(1)} %get-tuple-element.28, f32[1024]{0:T(1024)S(1)} %broadcast_multiply_fusion, bf16[1,1024,1024]{2,1,0:T(8,128)(2,1)S(1)} %copy-done, f32[1024,1024]{1,0:T(8,128)} %fusion.14, ...), kind=kOutput, calls=%fused_computation.112 | convolution fusion | flops 8597272576 | bytes 27277312 | tf_op jit(solution)/shard_map/tf,ef->te/dot_general | solution.py:338
  508.7 11.1 %concatenate.41 = bf16[1024,3456]{1,0:T(8,128)(2,1)} concatenate(bf16[1024,3072]{1,0:T(8,128)(2,1)} %convolution_convert_fusion.2, bf16[1024,1]{1,0:T(8,128)(2,1)S(1)} %convert_element_type.287, bf16[1024,1]{1,0:T(8,128)(2,1)S(1)} %convert_element_type.288, bf16[1024,382]{1,0:T(8,128)(2,1)S(1)} %broadcast_in_dim.39), dimensions={1} | concatenate | bytes 14155776 | tf_op jit(solution)/shard_map/concatenate | solution.py:216
  528.0 18.4 %fusion.40 = bf16[1,1024,1024]{2,1,0:T(8,128)(2,1)} fusion(f32[1024,1024]{1,0:T(8,128)S(1)} %fusion.55, bf16[1,1024,1024]{2,1,0:T(8,128)(2,1)S(1)} %copy-done, f32[1024]{0:T(1024)S(1)} %copy-done.17, bf16[4096,1024]{1,0:T(8,128)(2,1)} %reshape.467, f32[1024,4096]{1,0:T(8,128)} %fusion.12, f32[4096]{0:T(1024)S(1)} %copy-done.16), kind=kOutput, calls=%fused_computation.59 | convolution fusion | flops 8637120512 | bytes 33574912 | tf_op jit(solution)/shard_map/dot_general | solution.py:310
  546.3 91.5 %reduce-scatter.3.cloned.1.call-done = bf16[32,3456]{1,0:T(8,128)(2,1)} async-done(((bf16[1024,3456]{1,0:T(8,128)(2,1)}), bf16[32,3456]{1,0:T(8,128)(2,1)}) %reduce-scatter.3.cloned.1.call-update) | async-done | bytes 221200 | tf_op jit(solution)/shard_map/reduce_scatter | solution.py:236
  641.0 213.5 %reduce-scatter.5.cloned.1.call-done = bf16[32,9600]{1,0:T(8,128)(2,1)} async-done(((bf16[1024,9600]{1,0:T(8,128)(2,1)}), bf16[32,9600]{1,0:T(8,128)(2,1)}) %reduce-scatter.5.cloned.1.call-update) | async-done | bytes 614416 | tf_op jit(solution)/shard_map/reduce_scatter | solution.py:236
  (119 shorter events, 101.3 us)
Async XLA Ops:
  7.2 11.6 %copy-start = (bf16[1,1024,1024]{2,1,0:T(8,128)(2,1)S(1)}, bf16[1,1024,1024]{2,1,0:T(8,128)(2,1)}, u32[]{:S(2)}) copy-start(bf16[1,1024,1024]{2,1,0:T(8,128)(2,1)} %param.11) | copy-start | bytes 6291460
  7.2 79.8 %all-gather.5.cloned.1.call-start = ((), (), s32[]{:S(2)}) async-start(), calls=%async_computation.4 | async-start | bytes 7299072 | tf_op jit(solution)/shard_map/all_gather | solution.py:230
  12.1 200.4 %all-gather.7.cloned.1.call-start = ((), (), s32[]{:S(2)}) async-start(), calls=%async_computation.5 | async-start | bytes 19464192 | tf_op jit(solution)/shard_map/all_gather | solution.py:230
  15.2 622.6 %reduce-scatter.3.cloned.1.call-start = ((), (), s32[]{:S(2)}) async-start(), calls=%async_computation.2 | async-start | bytes 7299072 | tf_op jit(solution)/shard_map/reduce_scatter | solution.py:236
  19.8 73.1 %copy-start.13 = (f32[1024]{0:T(1024)}, f32[1024]{0:T(1024)S(1)}, u32[]{:S(2)}) copy-start(f32[1024]{0:T(1024)S(1)} %fusion.27) | copy-start | bytes 12292
  20.1 108.9 %copy-start.9 = (f32[1024,16]{0,1:T(8,128)}, f32[1024,16]{0,1:T(8,128)S(1)}, u32[]{:S(2)}) copy-start(f32[1024,16]{0,1:T(8,128)S(1)} %get-tuple-element.55) | copy-start | bytes 196612
  20.2 108.9 %copy-start.11 = (f32[1024,16]{0,1:T(8,128)}, f32[1024,16]{0,1:T(8,128)S(1)}, u32[]{:S(2)}) copy-start(f32[1024,16]{0,1:T(8,128)S(1)} %get-tuple-element.56) | copy-start | bytes 196612
  150.2 117.7 %copy-start.15 = (f32[4096]{0:T(1024)}, f32[4096]{0:T(1024)S(1)}, u32[]{:S(2)}) copy-start(f32[4096]{0:T(1024)S(1)} %reshape.491) | copy-start | bytes 49156
  234.2 15.0 %copy-start.3 = (bf16[1,1024,1024]{2,1,0:T(8,128)(2,1)S(1)}, bf16[1,1024,1024]{2,1,0:T(8,128)(2,1)}, u32[]{:S(2)}) copy-start(bf16[1,1024,1024]{2,1,0:T(8,128)(2,1)} %param.21) | copy-start | bytes 6291460
  308.1 14.6 %copy-start.8 = (bf16[1024,1]{1,0:T(8,128)(2,1)S(1)}, bf16[1024,1]{1,0:T(8,128)(2,1)}, u32[]{:S(2)}) copy-start(bf16[1024,1]{1,0:T(8,128)(2,1)} %reshape.508) | copy-start | bytes 6148
  462.0 1.6 copy-start.7
  462.0 1.6 copy-start.10
  462.0 1.6 copy-start.12
  467.2 1.6 copy-start.6
  467.5 2.0 copy-start.5
  469.5 10.6 %slice-start = ((s8[7077888]{0:T(1024)(128)(4,1)}), s8[2883584]{0:T(1024)(128)(4,1)S(1)}, s32[]{:S(2)}) async-start(s8[7077888]{0:T(1024)(128)(4,1)} %bitcast.143), calls=%async_computation.6 | async-start | bytes 5767168
  470.2 10.0 %slice-start.1 = ((s8[7077888]{0:T(1024)(128)(4,1)}), s8[4194304]{0:T(1024)(128)(4,1)S(1)}, s32[]{:S(2)}) async-start(s8[7077888]{0:T(1024)(128)(4,1)} %bitcast.143), calls=%async_computation.7 | async-start | bytes 8388608
  488.5 14.9 %copy-start.14 = (f32[1024]{0:T(1024)S(1)}, f32[1024]{0:T(1024)}, u32[]{:S(2)}) copy-start(f32[1024]{0:T(1024)} %copy-done.13) | copy-start | bytes 12292
  503.4 2.2 copy-start.1
  519.8 334.6 %reduce-scatter.5.cloned.1.call-start = ((), (), s32[]{:S(2)}) async-start(), calls=%async_computation.3 | async-start | bytes 20275200 | tf_op jit(solution)/shard_map/reduce_scatter | solution.py:236
  520.4 4.7 copy-start.2
  520.4 4.7 copy-start.4
  525.2 2.8 copy-start.16
  525.2 2.8 copy-start.17
Sparse Core Ops, SparseCore 0:
  12.3 74.7 all-gather.4
  90.0 122.4 all-gather.6
  520.0 117.7 reduce-scatter.2
  644.1 210.3 reduce-scatter.4

commit v5 on v4

--- a/solution.py
+++ b/solution.py
@@ -312,23 +312,26 @@
     )
     output = result.astype(jnp.bfloat16).reshape(tokens.shape)
     upstream = cotangent.reshape(positions, width)
-    outer_grad = jnp.sum(upstream, axis=0, dtype=jnp.float32)
     contract_grad = jnp.einsum(
         "tf,td->fd", active_low, upstream, preferred_element_type=jnp.float32
     )
+    rows_all = normed_low.shape[1]
+    first = [contract_grad.astype(jnp.bfloat16).reshape(rows_all, -1)]
+    first_packed = pad_columns(first)
+    first_packed, contract_back = lax.optimization_barrier((first_packed, contract_full))
+    (contract_part,) = scatter_columns(first_packed, [block.shape[1] for block in first])
+    outer_grad = jnp.sum(upstream, axis=0, dtype=jnp.float32)
     project_grad = jnp.einsum("te,td->ed", mixed_low, upstream, preferred_element_type=jnp.float32)
     active_grad = jnp.einsum(
-        "td,fd->tf", upstream, contract_full, preferred_element_type=jnp.float32
+        "td,fd->tf", upstream, contract_back, preferred_element_type=jnp.float32
     )
     hidden_grad = gelu_pull(active_grad)[0].astype(jnp.bfloat16)
     expand_grad = jnp.einsum(
         "te,tf->ef", normed_low, hidden_grad, preferred_element_type=jnp.float32
     )
     inner_grad = jnp.sum(hidden_grad, axis=0, dtype=jnp.float32)
-    rows_all = expand_grad.shape[0]
     early = [
         expand_grad.astype(jnp.bfloat16),
-        contract_grad.astype(jnp.bfloat16).reshape(rows_all, -1),
         project_grad.astype(jnp.bfloat16),
         as_column(inner_grad.astype(jnp.bfloat16), rows_all),
         as_column(outer_grad.astype(jnp.bfloat16), rows_all),
@@ -341,9 +344,7 @@
     mixed_grad = jnp.einsum("td,ed->te", upstream, project_full, preferred_element_type=jnp.float32)
     mixed_grad = mixed_grad.astype(jnp.bfloat16).reshape(seq_dev, seq_len, width)
     early_packed, mixed_grad = lax.optimization_barrier((early_packed, mixed_grad))
-    expand_part, contract_part, project_part, inner_part, outer_part = scatter_columns(
-        early_packed, early_widths
-    )
+    expand_part, project_part, inner_part, outer_part = scatter_columns(early_packed, early_widths)
     contract_part = contract_part.reshape(-1, width)
     inner_part = inner_part.reshape(-1)
     outer_part = outer_part.reshape(-1)

time: 874 us -> 939 us (1.074)
  waiting for transfers between devices: 375 us -> 443 us
    reduce_scatter x2 -> x3, waiting for transfers between devices: 305 us -> 372 us  [scatter_columns(): summed = lax.psum_scatter(packed, ALL, scatter_dimension=0, tiled=True)]
    concatenate x3 -> x4, local copies, waits for them, and re-layouts: 42.5 us -> 38 us  [pad_columns(): return jnp.concatenate(blocks, axis=1)]
  transfers between devices with their start and end apart: 4 -> 5, of which waited for: 4 -> 5; matrix products, arithmetic and copies ran while one was open for 12% -> 11% of each run, Pallas kernels for 6% -> 6%
where the time goes in v5:
time: 939 us; the launch traced here: 933 us
  waiting for transfers between devices  443 us (47%)
  matrix products  156 us (17%)
  local copies, waits for them, and re-layouts  155 us (17%)
  Pallas kernels  133 us (14%)
  other arithmetic  30.9 us (3%)
  between operations  15.1 us (2%)
    reduce_scatter x3, waiting for transfers between devices, scatter_columns(): summed = lax.psum_scatter(packed, ALL, scatter_dimension=0, tiled=True)  372 us
    pallas_call x1, Pallas kernels, attention_backward(): pl.pallas_call(attention_backward_kernel, out_shape=(jax.ShapeDtypeStruct...  78.7 us
    all_gather x2, waiting for transfers between devices, gather_columns(): full = lax.all_gather(packed[None], ALL, axis=0, tiled=True)  69.5 us
    pallas_call x1, Pallas kernels, attention_forward(): pl.pallas_call(attention_forward_kernel, out_shape=(jax.ShapeDtypeStruct(...  54.1 us
    concatenate x4, local copies, waits for them, and re-layouts, pad_columns(): return jnp.concatenate(blocks, axis=1)  38 us
    dot_general x1, matrix products, body(): jnp.einsum('td,fd->tf', upstream, contract_back, preferred_element_type=j...  26.1 us
  transfers between devices with their start and end apart: 5, of which 5 were waited for; matrix products, arithmetic and copies ran while one was open for 11% of the time, Pallas kernels for 6%

profile of v5, /device:TPU:0, one launch (start us, length us, event | category | flops | bytes accessed | tf_op | source)
XLA Modules:
  0.0 933.3 jit_solution(8739529298473820674)
XLA Ops:
  20.2 66.8 %all-gather.5.cloned.1.call-done = bf16[1024,3456]{1,0:T(8,128)(2,1)} async-done(((bf16[32,3456]{1,0:T(8,128)(2,1)}), bf16[1024,3456]{1,0:T(8,128)(2,1)}) %all-gather.5.cloned.1.call-update) | async-done | bytes 7077904 | tf_op jit(solution)/shard_map/all_gather | solution.py:230
  92.8 9.2 copy.39
  104.3 13.0 %convolution_bitcast_fusion = f32[1,1024,3,16,64]{1,4,3,2,0:T(8,128)} fusion(bf16[3,16,64,1024]{3,2,1,0:T(8,128)(2,1)} %bitcast.147, bf16[1,1024,1024]{2,1,0:T(8,128)(2,1)S(1)} %copy-done, f32[1024]{0:T(1024)S(1)} %get-tuple-element.31, f32[1024]{0:T(1024)S(1)} %get-tuple-element.32, f32[1024]{0:T(1024)S(1)} %fusion.57, f32[1024]{0:T(1024)S(1)} %broadcast_multiply_fusion), kind=kOutput, calls=%fused_computation.38 | convolution fusion | flops 6448742400 | bytes 20987904 | tf_op jit(solution)/shard_map/dot_general | solution.py:282
  149.8 54.1 %shard_map.186 = (bf16[1024,1024]{1,0:T(8,128)(2,1)}, f32[16,1024,1]{2,1,0:T(8,128)}, f32[16,1024,1]{2,1,0:T(8,128)}) custom-call(s32[1]{0:T(128)S(6)} %copy.71.length_ref, bf16[1024,1024]{1,0:T(8,128)(2,1)} %copy.46.q_ref, bf16[1024,1024]{1,0:T(8,128)(2,1)} %copy.47.k_ref, bf16[1024,1024]{1,0:T(8,128)(2,1)} %copy.48.v_ref), custom_call_target="tpu_custom_call" | custom-call | flops 8589934592 | bytes 37748736 | tf_op jit(solution)/shard_map/pallas_call | solution.py:134
  203.9 5.9 fusion.49
  212.5 7.7 slice.128
  220.2 14.0 %reshape.467 = bf16[4096,1024]{1,0:T(8,128)(2,1)} reshape(bf16[1024,4096]{1,0:T(8,128)(2,1)} %slice.128) | data formatting | bytes 16777216 | tf_op jit(solution)/shard_map/reshape | solution.py:276
  234.2 15.0 %fusion.12 = f32[1024,4096]{1,0:T(8,128)} fusion(bf16[1024,9216]{1,0:T(8,128)(2,1)} %all-gather.7.cloned.1.call-done, bf16[1,1024,1024]{2,1,0:T(8,128)(2,1)S(1)} %copy-done, f32[1024]{0:T(1024)S(1)} %get-tuple-element.31, f32[1024]{0:T(1024)S(1)} %get-tuple-element.32, f32[1024]{0:T(1024)S(1)} %fusion.57, f32[1024]{0:T(1024)S(1)} %broadcast_multiply_fusion), kind=kOutput, calls=%fused_computation.20 | convolution fusion | flops 8596226048 | bytes 27279360 | tf_op jit(solution)/shard_map/dot_general | solution.py:302
  249.2 18.7 %convolution_convert_fusion.1 = bf16[4096,1024]{1,0:T(8,128)(2,1)} fusion(bf16[1,1024,1024]{2,1,0:T(8,128)(2,1)S(1)} %copy-done.3, f32[1024,4096]{1,0:T(8,128)} %fusion.12, f32[4096]{0:T(1024)S(1)} %reshape.491), kind=kOutput, calls=%fused_computation.17 | convolution fusion | flops 8636071936 | bytes 27279360 | tf_op jit(solution)/shard_map/tf,td->fd/dot_general | solution.py:315
  267.8 13.9 %reshape.470 = bf16[1024,4096]{1,0:T(8,128)(2,1)} reshape(bf16[4096,1024]{1,0:T(8,128)(2,1)} %convolution_convert_fusion.1) | data formatting | bytes 16777216 | tf_op jit(solution)/shard_map/reshape | solution.py:319
  281.7 7.5 concatenate.43
  289.2 26.1 %fusion.66 = (bf16[4096]{0:T(1024)(128)(2,1)S(1)}, bf16[1024,4096]{1,0:T(8,128)(2,1)}) fusion(f32[1024,4096]{1,0:T(8,128)} %fusion.12, f32[4096]{0:T(1024)S(1)} %reshape.491, bf16[4096,1024]{1,0:T(8,128)(2,1)} %reshape.467, bf16[1,1024,1024]{2,1,0:T(8,128)(2,1)} %param.21), kind=kOutput, calls=%fused_computation.115 | convolution fusion | flops 8682205184 | bytes 35676160 | tf_op jit(solution)/shard_map/td,fd->tf/dot_general | solution.py:325
  315.3 15.5 %convolution_convert_fusion = bf16[1024,4096]{1,0:T(8,128)(2,1)} fusion(bf16[1024,4096]{1,0:T(8,128)(2,1)} %get-tuple-element.60, bf16[1,1024,1024]{2,1,0:T(8,128)(2,1)S(1)} %copy-done, f32[1024]{0:T(1024)S(1)} %get-tuple-element.31, f32[1024]{0:T(1024)S(1)} %get-tuple-element.32, f32[1024]{0:T(1024)S(1)} %fusion.57, f32[1024]{0:T(1024)S(1)} %broadcast_multiply_fusion), kind=kOutput, calls=%fused_computation.16 | convolution fusion | flops 8600420352 | bytes 18890752 | tf_op jit(solution)/shard_map/te,tf->ef/dot_general | solution.py:329
  331.4 17.6 %concatenate.44 = bf16[1024,5376]{1,0:T(8,128)(2,1)} concatenate(bf16[1024,4096]{1,0:T(8,128)(2,1)} %convolution_convert_fusion, bf16[1024,1024]{1,0:T(8,128)(2,1)} %fusion.49, bf16[1024,4]{1,0:T(8,128)(2,1)S(1)} %reshape.471, bf16[1024,1]{1,0:T(8,128)(2,1)S(1)} %copy-done.8, bf16[1024,251]{1,0:T(8,128)(2,1)S(1)} %broadcast_in_dim.17), dimensions={1} | concatenate | bytes 22020096 | tf_op jit(solution)/shard_map/concatenate | solution.py:216
  349.1 5.9 convert_bitcast_fusion.1
  355.0 78.7 %shard_map.187 = (f32[1024,1024]{1,0:T(8,128)}, f32[1024,1024]{1,0:T(8,128)}, f32[1024,1024]{1,0:T(8,128)}) custom-call(s32[1]{0:T(128)S(6)} %copy.71.length_ref, bf16[1024,1024]{1,0:T(8,128)(2,1)} %copy.46.q_ref, bf16[1024,1024]{1,0:T(8,128)(2,1)} %copy.47.k_ref, bf16[1024,1024]{1,0:T(8,128)(2,1)} %copy.48.v_ref, bf16[1024,1024]{1,0:T(8,128)(2,1)} %bitcast.153, ...), custom_call_target="tpu_custom_call" | custom-call | flops 21474836480 | bytes 54525952 | tf_op jit(solution)/shard_map/pallas_call | solution.py:169
  466.7 9.7 %convolution_convert_fusion.2 = bf16[1024,3072]{1,0:T(8,128)(2,1)} fusion(bf16[1024,3072]{0,1:T(8,128)(2,1)S(1)} %bitcast.145, bf16[1,1024,1024]{2,1,0:T(8,128)(2,1)S(1)} %copy-done, f32[1024]{0:T(1024)S(1)} %get-tuple-element.31, f32[1024]{0:T(1024)S(1)} %get-tuple-element.32, f32[1024]{0:T(1024)S(1)} %fusion.57, f32[1024]{0:T(1024)S(1)} %broadcast_multiply_fusion), kind=kOutput, calls=%fused_computation.26 | convolution fusion | flops 6451888128 | bytes 14696448 | tf_op jit(solution)/shard_map/te,tc->ec/dot_general | solution.py:373
  476.5 8.6 fusion.14
  485.0 14.9 %fusion.63 = (bf16[1024]{0:T(1024)(128)(2,1)S(1)}, f32[1024]{0:T(1024)S(1)}, f32[1024,1024]{1,0:T(8,128)S(1)}) fusion(f32[1024]{0:T(1024)S(1)} %get-tuple-element.32, f32[1024]{0:T(1024)S(1)} %broadcast_multiply_fusion, bf16[1,1024,1024]{2,1,0:T(8,128)(2,1)S(1)} %copy-done, f32[1024,1024]{1,0:T(8,128)} %fusion.14, ...), kind=kOutput, calls=%fused_computation.112 | convolution fusion | flops 8597272576 | bytes 27277312 | tf_op jit(solution)/shard_map/tf,ef->te/dot_general | solution.py:341
  504.9 11.1 %concatenate.45 = bf16[1024,3456]{1,0:T(8,128)(2,1)} concatenate(bf16[1024,3072]{1,0:T(8,128)(2,1)} %convolution_convert_fusion.2, bf16[1024,1]{1,0:T(8,128)(2,1)S(1)} %convert_element_type.287, bf16[1024,1]{1,0:T(8,128)(2,1)S(1)} %convert_element_type.288, bf16[1024,382]{1,0:T(8,128)(2,1)S(1)} %broadcast_in_dim.40), dimensions={1} | concatenate | bytes 14155776 | tf_op jit(solution)/shard_map/concatenate | solution.py:216
  525.1 18.3 %fusion.40 = bf16[1,1024,1024]{2,1,0:T(8,128)(2,1)} fusion(f32[1024,1024]{1,0:T(8,128)S(1)} %fusion.55, bf16[1,1024,1024]{2,1,0:T(8,128)(2,1)S(1)} %copy-done, f32[1024]{0:T(1024)S(1)} %copy-done.15, bf16[4096,1024]{1,0:T(8,128)(2,1)} %reshape.467, f32[1024,4096]{1,0:T(8,128)} %fusion.12, f32[4096]{0:T(1024)S(1)} %reshape.491), kind=kOutput, calls=%fused_computation.59 | convolution fusion | flops 8637120512 | bytes 33574912 | tf_op jit(solution)/shard_map/dot_general | solution.py:310
  543.3 90.8 %reduce-scatter.4.cloned.1.call-done = bf16[32,3456]{1,0:T(8,128)(2,1)} async-done(((bf16[1024,3456]{1,0:T(8,128)(2,1)}), bf16[32,3456]{1,0:T(8,128)(2,1)}) %reduce-scatter.4.cloned.1.call-update) | async-done | bytes 221200 | tf_op jit(solution)/shard_map/reduce_scatter | solution.py:236
  637.3 134.4 %reduce-scatter.8.cloned.1.call-done = bf16[32,4224]{1,0:T(8,128)(2,1)} async-done(((bf16[1024,4224]{1,0:T(8,128)(2,1)}), bf16[32,4224]{1,0:T(8,128)(2,1)}) %reduce-scatter.8.cloned.1.call-update) | async-done | bytes 270352 | tf_op jit(solution)/shard_map/reduce_scatter | solution.py:236
  773.6 146.9 %reduce-scatter.6.cloned.1.call-done = bf16[32,5376]{1,0:T(8,128)(2,1)} async-done(((bf16[1024,5376]{1,0:T(8,128)(2,1)}), bf16[32,5376]{1,0:T(8,128)(2,1)}) %reduce-scatter.6.cloned.1.call-update) | async-done | bytes 344080 | tf_op jit(solution)/shard_map/reduce_scatter | solution.py:236
  (120 shorter events, 113.9 us)
Async XLA Ops:
  7.2 11.6 %copy-start = (bf16[1,1024,1024]{2,1,0:T(8,128)(2,1)S(1)}, bf16[1,1024,1024]{2,1,0:T(8,128)(2,1)}, u32[]{:S(2)}) copy-start(bf16[1,1024,1024]{2,1,0:T(8,128)(2,1)} %param.11) | copy-start | bytes 6291460
  7.2 79.8 %all-gather.5.cloned.1.call-start = ((), (), s32[]{:S(2)}) async-start(), calls=%async_computation.6 | async-start | bytes 7299072 | tf_op jit(solution)/shard_map/all_gather | solution.py:230
  12.1 200.4 %all-gather.7.cloned.1.call-start = ((), (), s32[]{:S(2)}) async-start(), calls=%async_computation.7 | async-start | bytes 19464192 | tf_op jit(solution)/shard_map/all_gather | solution.py:230
  15.2 618.9 %reduce-scatter.4.cloned.1.call-start = ((), (), s32[]{:S(2)}) async-start(), calls=%async_computation.3 | async-start | bytes 7299072 | tf_op jit(solution)/shard_map/reduce_scatter | solution.py:236
  19.8 73.0 %copy-start.13 = (f32[1024]{0:T(1024)}, f32[1024]{0:T(1024)S(1)}, u32[]{:S(2)}) copy-start(f32[1024]{0:T(1024)S(1)} %fusion.27) | copy-start | bytes 12292
  20.2 108.9 %copy-start.9 = (f32[1024,16]{0,1:T(8,128)}, f32[1024,16]{0,1:T(8,128)S(1)}, u32[]{:S(2)}) copy-start(f32[1024,16]{0,1:T(8,128)S(1)} %get-tuple-element.57) | copy-start | bytes 196612
  20.2 108.9 %copy-start.11 = (f32[1024,16]{0,1:T(8,128)}, f32[1024,16]{0,1:T(8,128)S(1)}, u32[]{:S(2)}) copy-start(f32[1024,16]{0,1:T(8,128)S(1)} %get-tuple-element.58) | copy-start | bytes 196612
  234.2 15.0 %copy-start.3 = (bf16[1,1024,1024]{2,1,0:T(8,128)(2,1)S(1)}, bf16[1,1024,1024]{2,1,0:T(8,128)(2,1)}, u32[]{:S(2)}) copy-start(bf16[1,1024,1024]{2,1,0:T(8,128)(2,1)} %param.21) | copy-start | bytes 6291460
  315.3 16.2 %copy-start.8 = (bf16[1024,1]{1,0:T(8,128)(2,1)S(1)}, bf16[1024,1]{1,0:T(8,128)(2,1)}, u32[]{:S(2)}) copy-start(bf16[1024,1]{1,0:T(8,128)(2,1)} %reshape.508) | copy-start | bytes 6148
  458.5 1.6 copy-start.7
  458.5 1.6 copy-start.10
  458.6 1.6 copy-start.12
  463.7 1.6 copy-start.6
  464.1 2.0 copy-start.5
  466.0 10.4 %slice-start = ((s8[7077888]{0:T(1024)(128)(4,1)}), s8[2883584]{0:T(1024)(128)(4,1)S(1)}, s32[]{:S(2)}) async-start(s8[7077888]{0:T(1024)(128)(4,1)} %bitcast.143), calls=%async_computation.8 | async-start | bytes 5767168
  466.7 9.8 %slice-start.1 = ((s8[7077888]{0:T(1024)(128)(4,1)}), s8[4194304]{0:T(1024)(128)(4,1)S(1)}, s32[]{:S(2)}) async-start(s8[7077888]{0:T(1024)(128)(4,1)} %bitcast.143), calls=%async_computation.9 | async-start | bytes 8388608
  485.0 14.9 %copy-start.14 = (f32[1024]{0:T(1024)S(1)}, f32[1024]{0:T(1024)}, u32[]{:S(2)}) copy-start(f32[1024]{0:T(1024)} %copy-done.13) | copy-start | bytes 12292
  499.9 2.2 copy-start.1
  516.1 255.6 %reduce-scatter.8.cloned.1.call-start = ((), (), s32[]{:S(2)}) async-start(), calls=%async_computation.5 | async-start | bytes 8921088 | tf_op jit(solution)/shard_map/reduce_scatter | solution.py:236
  516.7 403.8 %reduce-scatter.6.cloned.1.call-start = ((), (), s32[]{:S(2)}) async-start(), calls=%async_computation.4 | async-start | bytes 11354112 | tf_op jit(solution)/shard_map/reduce_scatter | solution.py:236
  517.3 4.7 copy-start.2
  517.3 4.7 copy-start.4
  522.0 3.0 copy-start.15
Sparse Core Ops, SparseCore 0:
  12.3 74.7 all-gather.4
  90.0 122.4 all-gather.6
  516.2 117.8 reduce-scatter.3
  639.9 131.7 reduce-scatter.7
  777.5 142.9 reduce-scatter.5

commit v6 on v5

--- a/solution.py
+++ b/solution.py
@@ -264,16 +264,14 @@
             as_column(norm_shift, rows_dev),
             as_column(inner_bias, rows_dev),
             as_column(outer_bias, rows_dev),
-        ]
+        ],
     )
     gain_full = gain_full.reshape(-1)
     shift_full = shift_full.reshape(-1)
     inner_full = inner_full.reshape(-1)
     outer_full = outer_full.reshape(-1)
-    expand_full, project_full, contract_full = gather_columns(
-        [expand_weight, project_weight, contract_weight.reshape(rows_dev, -1)]
-    )
-    contract_full = contract_full.reshape(-1, width)
+    expand_full, project_full = gather_columns([expand_weight, project_weight])
+    (contract_full,) = gather_columns([contract_weight])
     rows = tokens.reshape(positions, width).astype(jnp.float32)
     normed, norm_pull = jax.vjp(
         layer_norm, rows, gain_full.astype(jnp.float32), shift_full.astype(jnp.float32)
@@ -316,14 +314,17 @@
         "tf,td->fd", active_low, upstream, preferred_element_type=jnp.float32
     )
     rows_all = normed_low.shape[1]
-    first = [contract_grad.astype(jnp.bfloat16).reshape(rows_all, -1)]
+    first = [contract_grad.astype(jnp.bfloat16)]
     first_packed = pad_columns(first)
-    first_packed, contract_back = lax.optimization_barrier((first_packed, contract_full))
+    first_packed, upstream_back = lax.optimization_barrier((first_packed, upstream))
     (contract_part,) = scatter_columns(first_packed, [block.shape[1] for block in first])
-    outer_grad = jnp.sum(upstream, axis=0, dtype=jnp.float32)
-    project_grad = jnp.einsum("te,td->ed", mixed_low, upstream, preferred_element_type=jnp.float32)
+    contract_part = contract_part.reshape(-1, width)
+    outer_grad = jnp.sum(upstream_back, axis=0, dtype=jnp.float32)
+    project_grad = jnp.einsum(
+        "te,td->ed", mixed_low, upstream_back, preferred_element_type=jnp.float32
+    )
     active_grad = jnp.einsum(
-        "td,fd->tf", upstream, contract_back, preferred_element_type=jnp.float32
+        "td,fd->tf", upstream_back, contract_full, preferred_element_type=jnp.float32
     )
     hidden_grad = gelu_pull(active_grad)[0].astype(jnp.bfloat16)
     expand_grad = jnp.einsum(
@@ -345,7 +346,6 @@
     mixed_grad = mixed_grad.astype(jnp.bfloat16).reshape(seq_dev, seq_len, width)
     early_packed, mixed_grad = lax.optimization_barrier((early_packed, mixed_grad))
     expand_part, project_part, inner_part, outer_part = scatter_columns(early_packed, early_widths)
-    contract_part = contract_part.reshape(-1, width)
     inner_part = inner_part.reshape(-1)
     outer_part = outer_part.reshape(-1)
     backward_parts = [

time: 939 us -> 917 us (0.977)
  local copies, waits for them, and re-layouts: 155 us -> 119 us
  waiting for transfers between devices: 443 us -> 458 us
    reshape x4 -> x0, local copies, waits for them, and re-layouts: 29.9 us -> none  [the longest x1 14 us: body(): contract_full = contract_full.reshape(-1, width)]
    all_gather x2 -> x3, waiting for transfers between devices: 69.5 us -> 81 us  [gather_columns(): full = lax.all_gather(packed[None], ALL, axis=0, tiled=True)]
    concatenate x4 -> x6, local copies, waits for them, and re-layouts: 38 us -> 40.2 us  [pad_columns(): return jnp.concatenate(blocks, axis=1)]
  transfers between devices with their start and end apart: 5 -> 6, of which waited for: 5 -> 5; matrix products, arithmetic and copies ran while one was open for 11% -> 16% of each run, Pallas kernels for 6% -> 6%
where the time goes in v6:
time: 917 us; the launch traced here: 913 us
  waiting for transfers between devices  458 us (50%)
  matrix products  154 us (17%)
  Pallas kernels  133 us (15%)
  local copies, waits for them, and re-layouts  119 us (13%)
  other arithmetic  33.4 us (4%)
  between operations  15.5 us (2%)
    reduce_scatter x3, waiting for transfers between devices, scatter_columns(): summed = lax.psum_scatter(packed, ALL, scatter_dimension=0, tiled=True)  376 us
    all_gather x3, waiting for transfers between devices, gather_columns(): full = lax.all_gather(packed[None], ALL, axis=0, tiled=True)  81 us
    pallas_call x1, Pallas kernels, attention_backward(): pl.pallas_call(attention_backward_kernel, out_shape=(jax.ShapeDtypeStruct...  78.7 us
    pallas_call x1, Pallas kernels, attention_forward(): pl.pallas_call(attention_forward_kernel, out_shape=(jax.ShapeDtypeStruct(...  54.1 us
    concatenate x6, local copies, waits for them, and re-layouts, pad_columns(): return jnp.concatenate(blocks, axis=1)  40.2 us
    dot_general x1, matrix products, body(): jnp.einsum('td,fd->tf', upstream_back, contract_full, preferred_element_t...  25.8 us
    dot_general x1, matrix products, body(): jnp.einsum('tf,td->fd', active_low, upstream, preferred_element_type=jnp....  18.6 us
    dot_general x1, matrix products, body(): jnp.dot(active_low, contract_full, preferred_element_type=jnp.float32)  18.4 us
  transfers between devices with their start and end apart: 6, of which 5 were waited for; matrix products, arithmetic and copies ran while one was open for 16% of the time, Pallas kernels for 6%

profile of v6, /device:TPU:0, one launch (start us, length us, event | category | flops | bytes accessed | tf_op | source)
XLA Modules:
  0.0 912.9 jit_solution(8689788570075770565)
XLA Ops:
  19.5 67.5 %all-gather.7.cloned.1.call-done = bf16[1024,3456]{1,0:T(8,128)(2,1)} async-done(((bf16[32,3456]{1,0:T(8,128)(2,1)}), bf16[1024,3456]{1,0:T(8,128)(2,1)}) %all-gather.7.cloned.1.call-update) | async-done | bytes 7077904 | tf_op jit(solution)/shard_map/all_gather | solution.py:230
  87.0 5.9 slice_bitcast_fusion
  92.9 9.0 copy.39
  104.3 13.0 %convolution_bitcast_fusion = f32[1,1024,3,16,64]{1,4,3,2,0:T(8,128)} fusion(bf16[3,16,64,1024]{3,2,1,0:T(8,128)(2,1)} %bitcast.127, bf16[1,1024,1024]{2,1,0:T(8,128)(2,1)S(1)} %copy-done, f32[1024]{0:T(1024)S(1)} %get-tuple-element.31, f32[1024]{0:T(1024)S(1)} %get-tuple-element.30, f32[1024]{0:T(1024)S(1)} %fusion.53, f32[1024]{0:T(1024)S(1)} %broadcast_multiply_fusion), kind=kOutput, calls=%fused_computation.37 | convolution fusion | flops 6448742400 | bytes 20987904 | tf_op jit(solution)/shard_map/dot_general | solution.py:280
  149.9 54.1 %shard_map.186 = (bf16[1024,1024]{1,0:T(8,128)(2,1)}, f32[16,1024,1]{2,1,0:T(8,128)}, f32[16,1024,1]{2,1,0:T(8,128)}) custom-call(s32[1]{0:T(128)S(6)} %copy.71.length_ref, bf16[1024,1024]{1,0:T(8,128)(2,1)} %copy.46.q_ref, bf16[1024,1024]{1,0:T(8,128)(2,1)} %copy.47.k_ref, bf16[1024,1024]{1,0:T(8,128)(2,1)} %copy.48.v_ref), custom_call_target="tpu_custom_call" | custom-call | flops 8589934592 | bytes 37748736 | tf_op jit(solution)/shard_map/pallas_call | solution.py:134
  203.9 15.0 %fusion.13 = f32[1024,4096]{1,0:T(8,128)} fusion(bf16[1024,5376]{1,0:T(8,128)(2,1)} %all-gather.9.cloned.1.call-done, bf16[1,1024,1024]{2,1,0:T(8,128)(2,1)S(1)} %copy-done, f32[1024]{0:T(1024)S(1)} %get-tuple-element.31, f32[1024]{0:T(1024)S(1)} %get-tuple-element.30, f32[1024]{0:T(1024)S(1)} %fusion.53, f32[1024]{0:T(1024)S(1)} %broadcast_multiply_fusion), kind=kOutput, calls=%fused_computation.19 | convolution fusion | flops 8596226048 | bytes 27279360 | tf_op jit(solution)/shard_map/dot_general | solution.py:300
  218.9 18.6 %convolution_convert_fusion.1 = bf16[4096,1024]{1,0:T(8,128)(2,1)} fusion(bf16[1,1024,1024]{2,1,0:T(8,128)(2,1)S(1)} %copy-done.3, f32[1024,4096]{1,0:T(8,128)} %fusion.13, f32[4096]{0:T(1024)S(1)} %reshape.475), kind=kOutput, calls=%fused_computation.12 | convolution fusion | flops 8636071936 | bytes 27279360 | tf_op jit(solution)/shard_map/tf,td->fd/dot_general | solution.py:313
  237.6 8.0 concatenate.47
  247.6 13.5 %all-gather.11.cloned.1.call-done = bf16[4096,1152]{1,0:T(8,128)(2,1)} async-done(((bf16[128,1152]{1,0:T(8,128)(2,1)}), bf16[4096,1152]{1,0:T(8,128)(2,1)}) %all-gather.11.cloned.1.call-update) | async-done | bytes 9437200 | tf_op jit(solution)/shard_map/all_gather | solution.py:230
  261.1 25.8 %fusion.64 = (bf16[4096]{0:T(1024)(128)(2,1)S(1)}, bf16[1024,4096]{1,0:T(8,128)(2,1)}) fusion(f32[1024,4096]{1,0:T(8,128)} %fusion.13, f32[4096]{0:T(1024)S(1)} %reshape.475, bf16[1024,1024]{1,0:T(8,128)(2,1)} %bitcast.111, bf16[4096,1152]{1,0:T(8,128)(2,1)} %all-gather.11.cloned.1.call-done), kind=kOutput, calls=%fused_computation.110 | convolution fusion | flops 8682205184 | bytes 35676160 | tf_op jit(solution)/shard_map/td,fd->tf/dot_general | solution.py:326
  287.0 15.4 %convolution_convert_fusion = bf16[1024,4096]{1,0:T(8,128)(2,1)} fusion(bf16[1024,4096]{1,0:T(8,128)(2,1)} %get-tuple-element.60, bf16[1,1024,1024]{2,1,0:T(8,128)(2,1)S(1)} %copy-done, f32[1024]{0:T(1024)S(1)} %get-tuple-element.31, f32[1024]{0:T(1024)S(1)} %get-tuple-element.30, f32[1024]{0:T(1024)S(1)} %fusion.53, f32[1024]{0:T(1024)S(1)} %broadcast_multiply_fusion), kind=kOutput, calls=%fused_computation.11 | convolution fusion | flops 8600420352 | bytes 18890752 | tf_op jit(solution)/shard_map/te,tf->ef/dot_general | solution.py:330
  306.8 17.6 %concatenate.48 = bf16[1024,5376]{1,0:T(8,128)(2,1)} concatenate(bf16[1024,4096]{1,0:T(8,128)(2,1)} %convolution_convert_fusion, bf16[1024,1024]{1,0:T(8,128)(2,1)} %convolution_convert_fusion.3, bf16[1024,4]{1,0:T(8,128)(2,1)S(1)} %reshape.457, bf16[1024,1]{1,0:T(8,128)(2,1)S(1)} %reshape.492, bf16[1024,251]{1,0:T(8,128)(2,1)S(1)} %broadcast_in_dim.46), dimensions={1} | concatenate | bytes 22020096 | tf_op jit(solution)/shard_map/concatenate | solution.py:216
  324.5 5.9 convert_bitcast_fusion.1
  330.4 78.7 %shard_map.187 = (f32[1024,1024]{1,0:T(8,128)}, f32[1024,1024]{1,0:T(8,128)}, f32[1024,1024]{1,0:T(8,128)}) custom-call(s32[1]{0:T(128)S(6)} %copy.71.length_ref, bf16[1024,1024]{1,0:T(8,128)(2,1)} %copy.46.q_ref, bf16[1024,1024]{1,0:T(8,128)(2,1)} %copy.47.k_ref, bf16[1024,1024]{1,0:T(8,128)(2,1)} %copy.48.v_ref, bf16[1024,1024]{1,0:T(8,128)(2,1)} %bitcast.133, ...), custom_call_target="tpu_custom_call" | custom-call | flops 21474836480 | bytes 54525952 | tf_op jit(solution)/shard_map/pallas_call | solution.py:169
  413.7 5.8 copy.55
  425.9 5.4 copy.58
  442.2 9.9 %convolution_convert_fusion.2 = bf16[1024,3072]{1,0:T(8,128)(2,1)} fusion(bf16[1024,3072]{0,1:T(8,128)(2,1)S(1)} %bitcast.125, bf16[1,1024,1024]{2,1,0:T(8,128)(2,1)S(1)} %copy-done, f32[1024]{0:T(1024)S(1)} %get-tuple-element.31, f32[1024]{0:T(1024)S(1)} %get-tuple-element.30, f32[1024]{0:T(1024)S(1)} %fusion.53, f32[1024]{0:T(1024)S(1)} %broadcast_multiply_fusion), kind=kOutput, calls=%fused_computation.25 | convolution fusion | flops 6451888128 | bytes 14696448 | tf_op jit(solution)/shard_map/te,tc->ec/dot_general | solution.py:373
  452.2 8.3 fusion.17
  460.5 14.9 %fusion.61 = (bf16[1024]{0:T(1024)(128)(2,1)S(1)}, f32[1024]{0:T(1024)S(1)}, f32[1024,1024]{1,0:T(8,128)S(1)}) fusion(f32[1024]{0:T(1024)S(1)} %get-tuple-element.30, f32[1024]{0:T(1024)S(1)} %broadcast_multiply_fusion, bf16[1,1024,1024]{2,1,0:T(8,128)(2,1)S(1)} %copy-done, f32[1024,1024]{1,0:T(8,128)} %fusion.17, ...), kind=kOutput, calls=%fused_computation.107 | convolution fusion | flops 8597272576 | bytes 27277312 | tf_op jit(solution)/shard_map/tf,ef->te/dot_general | solution.py:342
  480.5 11.1 %concatenate.49 = bf16[1024,3456]{1,0:T(8,128)(2,1)} concatenate(bf16[1024,3072]{1,0:T(8,128)(2,1)} %convolution_convert_fusion.2, bf16[1024,1]{1,0:T(8,128)(2,1)S(1)} %convert_element_type.290, bf16[1024,1]{1,0:T(8,128)(2,1)S(1)} %convert_element_type.291, bf16[1024,382]{1,0:T(8,128)(2,1)S(1)} %broadcast_in_dim.49), dimensions={1} | concatenate | bytes 14155776 | tf_op jit(solution)/shard_map/concatenate | solution.py:216
  500.3 18.4 %fusion.50 = bf16[1,1024,1024]{2,1,0:T(8,128)(2,1)} fusion(f32[1024]{0:T(1024)S(1)} %copy-done.17, bf16[4096,1152]{1,0:T(8,128)(2,1)} %all-gather.11.cloned.1.call-done, f32[1024,1024]{1,0:T(8,128)S(1)} %fusion.48, bf16[1,1024,1024]{2,1,0:T(8,128)(2,1)S(1)} %copy-done, f32[1024,4096]{1,0:T(8,128)} %fusion.13, f32[4096]{0:T(1024)S(1)} %copy-done.16), kind=kOutput, calls=%fused_computation.71 | convolution fusion | flops 8637120512 | bytes 33574912 | tf_op jit(solution)/shard_map/dot_general | solution.py:308
  518.7 91.2 %reduce-scatter.4.cloned.1.call-done = bf16[32,3456]{1,0:T(8,128)(2,1)} async-done(((bf16[1024,3456]{1,0:T(8,128)(2,1)}), bf16[32,3456]{1,0:T(8,128)(2,1)}) %reduce-scatter.4.cloned.1.call-update) | async-done | bytes 221200 | tf_op jit(solution)/shard_map/reduce_scatter | solution.py:236
  613.0 138.0 %reduce-scatter.8.cloned.1.call-done = bf16[128,1152]{1,0:T(8,128)(2,1)} async-done(((bf16[4096,1152]{1,0:T(8,128)(2,1)}), bf16[128,1152]{1,0:T(8,128)(2,1)}) %reduce-scatter.8.cloned.1.call-update) | async-done | bytes 294928 | tf_op jit(solution)/shard_map/reduce_scatter | solution.py:236
  752.8 147.0 %reduce-scatter.6.cloned.1.call-done = bf16[32,5376]{1,0:T(8,128)(2,1)} async-done(((bf16[1024,5376]{1,0:T(8,128)(2,1)}), bf16[32,5376]{1,0:T(8,128)(2,1)}) %reduce-scatter.6.cloned.1.call-update) | async-done | bytes 344080 | tf_op jit(solution)/shard_map/reduce_scatter | solution.py:236
  (127 shorter events, 99.5 us)
Async XLA Ops:
  7.2 11.3 %copy-start = (bf16[1,1024,1024]{2,1,0:T(8,128)(2,1)S(1)}, bf16[1,1024,1024]{2,1,0:T(8,128)(2,1)}, u32[]{:S(2)}) copy-start(bf16[1,1024,1024]{2,1,0:T(8,128)(2,1)} %param.11) | copy-start | bytes 6291460
  7.2 79.8 %all-gather.7.cloned.1.call-start = ((), (), s32[]{:S(2)}) async-start(), calls=%async_computation.6 | async-start | bytes 7299072 | tf_op jit(solution)/shard_map/all_gather | solution.py:230
  12.1 191.8 %all-gather.9.cloned.1.call-start = ((), (), s32[]{:S(2)}) async-start(), calls=%async_computation.7 | async-start | bytes 11354112 | tf_op jit(solution)/shard_map/all_gather | solution.py:230
  14.0 247.1 %all-gather.11.cloned.1.call-start = ((), (), s32[]{:S(2)}) async-start(), calls=%async_computation.8 | async-start | bytes 9732096 | tf_op jit(solution)/shard_map/all_gather | solution.py:230
  15.8 594.1 %reduce-scatter.4.cloned.1.call-start = ((), (), s32[]{:S(2)}) async-start(), calls=%async_computation.3 | async-start | bytes 7299072 | tf_op jit(solution)/shard_map/reduce_scatter | solution.py:236
  19.1 73.7 %copy-start.13 = (f32[1024]{0:T(1024)}, f32[1024]{0:T(1024)S(1)}, u32[]{:S(2)}) copy-start(f32[1024]{0:T(1024)S(1)} %fusion.30) | copy-start | bytes 12292
  19.5 109.0 %copy-start.9 = (f32[1024,16]{0,1:T(8,128)}, f32[1024,16]{0,1:T(8,128)S(1)}, u32[]{:S(2)}) copy-start(f32[1024,16]{0,1:T(8,128)S(1)} %get-tuple-element.57) | copy-start | bytes 196612
  19.5 109.0 %copy-start.11 = (f32[1024,16]{0,1:T(8,128)}, f32[1024,16]{0,1:T(8,128)S(1)}, u32[]{:S(2)}) copy-start(f32[1024,16]{0,1:T(8,128)S(1)} %get-tuple-element.58) | copy-start | bytes 196612
  149.9 111.2 %copy-start.15 = (f32[4096]{0:T(1024)}, f32[4096]{0:T(1024)S(1)}, u32[]{:S(2)}) copy-start(f32[4096]{0:T(1024)S(1)} %reshape.475) | copy-start | bytes 49156
  203.9 15.0 %copy-start.3 = (bf16[1,1024,1024]{2,1,0:T(8,128)(2,1)S(1)}, bf16[1,1024,1024]{2,1,0:T(8,128)(2,1)}, u32[]{:S(2)}) copy-start(bf16[1,1024,1024]{2,1,0:T(8,128)(2,1)} %param.21) | copy-start | bytes 6291460
  286.9 15.4 %copy-start.4 = (bf16[1,1024,1024]{2,1,0:T(8,128)(2,1)S(1)}, bf16[1,1024,1024]{2,1,0:T(8,128)(2,1)}, u32[]{:S(2)}) copy-start(bf16[1,1024,1024]{2,1,0:T(8,128)(2,1)} %param.21) | copy-start | bytes 6291460
  286.9 15.4 %copy-start.18 = (bf16[1024,1024]{1,0:T(8,128)(2,1)S(1)}, bf16[1024,1024]{1,0:T(8,128)(2,1)}, u32[]{:S(2)}) copy-start(bf16[1024,1024]{1,0:T(8,128)(2,1)} %get-tuple-element.20) | copy-start | bytes 6291460
  439.2 1.6 copy-start.7
  439.6 2.0 copy-start.6
  441.5 10.6 %slice-start = ((s8[7077888]{0:T(1024)(128)(4,1)}), s8[2883584]{0:T(1024)(128)(4,1)S(1)}, s32[]{:S(2)}) async-start(s8[7077888]{0:T(1024)(128)(4,1)} %bitcast.123), calls=%async_computation.9 | async-start | bytes 5767168
  442.2 10.0 %slice-start.1 = ((s8[7077888]{0:T(1024)(128)(4,1)}), s8[4194304]{0:T(1024)(128)(4,1)S(1)}, s32[]{:S(2)}) async-start(s8[7077888]{0:T(1024)(128)(4,1)} %bitcast.123), calls=%async_computation.10 | async-start | bytes 8388608
  460.5 14.9 %copy-start.14 = (f32[1024]{0:T(1024)S(1)}, f32[1024]{0:T(1024)}, u32[]{:S(2)}) copy-start(f32[1024]{0:T(1024)} %copy-done.13) | copy-start | bytes 12292
  475.4 2.0 copy-start.1
  491.6 259.4 %reduce-scatter.8.cloned.1.call-start = ((), (), s32[]{:S(2)}) async-start(), calls=%async_computation.5 | async-start | bytes 9732096 | tf_op jit(solution)/shard_map/reduce_scatter | solution.py:236
  492.2 407.6 %reduce-scatter.6.cloned.1.call-start = ((), (), s32[]{:S(2)}) async-start(), calls=%async_computation.4 | async-start | bytes 11354112 | tf_op jit(solution)/shard_map/reduce_scatter | solution.py:236
  492.8 4.7 copy-start.2
  492.8 4.7 copy-start.5
  497.5 2.8 copy-start.16
  497.6 2.8 copy-start.17
  (3 other events, 4.8 us)
Sparse Core Ops, SparseCore 0:
  12.3 74.7 all-gather.6
  90.6 86.8 all-gather.8
  181.0 80.0 all-gather.10
  491.7 118.0 reduce-scatter.3
  615.6 135.3 reduce-scatter.7
  756.8 142.9 reduce-scatter.5

commit v7 on v6

--- a/solution.py
+++ b/solution.py
@@ -257,9 +257,9 @@
     seq_dev, seq_len, width = tokens.shape
     positions = seq_dev * seq_len
     rows_dev = attend_weight.shape[0]
-    attend_full, gain_full, shift_full, inner_full, outer_full = gather_columns(
+    expand_full, gain_full, shift_full, inner_full, outer_full = gather_columns(
         [
-            attend_weight,
+            expand_weight,
             as_column(norm_gain, rows_dev),
             as_column(norm_shift, rows_dev),
             as_column(inner_bias, rows_dev),
@@ -270,16 +270,34 @@
     shift_full = shift_full.reshape(-1)
     inner_full = inner_full.reshape(-1)
     outer_full = outer_full.reshape(-1)
-    expand_full, project_full = gather_columns([expand_weight, project_weight])
-    (contract_full,) = gather_columns([contract_weight])
+    attend_full, project_full, contract_full = gather_columns(
+        [attend_weight, project_weight, contract_weight.reshape(rows_dev, -1)]
+    )
+    contract_full = contract_full.reshape(-1, width)
     rows = tokens.reshape(positions, width).astype(jnp.float32)
     normed, norm_pull = jax.vjp(
         layer_norm, rows, gain_full.astype(jnp.float32), shift_full.astype(jnp.float32)
     )
     normed_low = normed.astype(jnp.bfloat16)
-    triple = jnp.dot(normed_low, attend_full, preferred_element_type=jnp.float32).reshape(
-        seq_dev, seq_len, 3, HEADS, HEAD_DIM
-    )
+    upstream = cotangent.reshape(positions, width)
+    hidden = jnp.dot(
+        normed_low, expand_full, preferred_element_type=jnp.float32
+    ) + inner_full.astype(jnp.float32)
+    active, gelu_pull = jax.vjp(gelu_tanh, hidden)
+    active_low = active.astype(jnp.bfloat16)
+    contract_grad = jnp.einsum(
+        "tf,td->fd", active_low, upstream, preferred_element_type=jnp.float32
+    )
+    rows_all = normed_low.shape[1]
+    first = [contract_grad.astype(jnp.bfloat16)]
+    first_packed = pad_columns(first)
+    first_packed, upstream_back, attend_full = lax.optimization_barrier(
+        (first_packed, upstream, attend_full)
+    )
+    (contract_part,) = scatter_columns(first_packed, [block.shape[1] for block in first])
+    contract_part = contract_part.reshape(-1, width)
+    triple = jnp.dot(normed_low, attend_full, preferred_element_type=jnp.float32)
+    triple = triple.reshape(seq_dev, seq_len, 3, HEADS, HEAD_DIM)
     cosine, sine = rotary_tables(seq_len)
 
     def turn(query, keys):
@@ -297,11 +315,6 @@
         for s in range(seq_dev)
     ]
     mixed_low = jnp.concatenate([part[0] for part in forward_parts], axis=0)
-    hidden = jnp.dot(
-        normed_low, expand_full, preferred_element_type=jnp.float32
-    ) + inner_full.astype(jnp.float32)
-    active, gelu_pull = jax.vjp(gelu_tanh, hidden)
-    active_low = active.astype(jnp.bfloat16)
     result = rows + jnp.dot(mixed_low, project_full, preferred_element_type=jnp.float32)
     result = (
         result
@@ -309,16 +322,6 @@
         + outer_full.astype(jnp.float32)
     )
     output = result.astype(jnp.bfloat16).reshape(tokens.shape)
-    upstream = cotangent.reshape(positions, width)
-    contract_grad = jnp.einsum(
-        "tf,td->fd", active_low, upstream, preferred_element_type=jnp.float32
-    )
-    rows_all = normed_low.shape[1]
-    first = [contract_grad.astype(jnp.bfloat16)]
-    first_packed = pad_columns(first)
-    first_packed, upstream_back = lax.optimization_barrier((first_packed, upstream))
-    (contract_part,) = scatter_columns(first_packed, [block.shape[1] for block in first])
-    contract_part = contract_part.reshape(-1, width)
     outer_grad = jnp.sum(upstream_back, axis=0, dtype=jnp.float32)
     project_grad = jnp.einsum(
         "te,td->ed", mixed_low, upstream_back, preferred_element_type=jnp.float32

time: 917 us -> 1010 us (1.10)
  waiting for transfers between devices: 458 us -> 526 us
  local copies, waits for them, and re-layouts: 119 us -> 139 us
    all_gather x3 -> x2, waiting for transfers between devices: 81 us -> 149 us  [gather_columns(): full = lax.all_gather(packed[None], ALL, axis=0, tiled=True)]
    reshape x0 -> x2, local copies, waits for them, and re-layouts: none -> 15.1 us  [the longest x1 13.9 us: body(): contract_full = contract_full.reshape(-1, width)]
    slice x0 -> x2, local copies, waits for them, and re-layouts: none -> 13.8 us  [split_columns(): pieces.append(packed[:, offset:offset + width])]
    concatenate x6 -> x5, local copies, waits for them, and re-layouts: 40.2 us -> 38.6 us  [pad_columns(): return jnp.concatenate(blocks, axis=1)]
  transfers between devices with their start and end apart: 6 -> 5, of which waited for: 5 -> 5; matrix products, arithmetic and copies ran while one was open for 16% -> 8% of each run, Pallas kernels for 6% -> 0%
where the time goes in v7:
time: 1010 us; the launch traced here: 1000 us
  waiting for transfers between devices  526 us (52%)
  matrix products  156 us (15%)
  local copies, waits for them, and re-layouts  139 us (14%)
  Pallas kernels  133 us (13%)
  other arithmetic  34.2 us (3%)
  between operations  15.1 us (1%)
    reduce_scatter x3, waiting for transfers between devices, scatter_columns(): summed = lax.psum_scatter(packed, ALL, scatter_dimension=0, tiled=True)  376 us
    all_gather x2, waiting for transfers between devices, gather_columns(): full = lax.all_gather(packed[None], ALL, axis=0, tiled=True)  149 us
    pallas_call x1, Pallas kernels, attention_backward(): pl.pallas_call(attention_backward_kernel, out_shape=(jax.ShapeDtypeStruct...  79.1 us
    pallas_call x1, Pallas kernels, attention_forward(): pl.pallas_call(attention_forward_kernel, out_shape=(jax.ShapeDtypeStruct(...  54 us
    concatenate x5, local copies, waits for them, and re-layouts, pad_columns(): return jnp.concatenate(blocks, axis=1)  38.6 us
    dot_general x1, matrix products, body(): jnp.einsum('td,fd->tf', upstream_back, contract_full, preferred_element_t...  25.9 us
  transfers between devices with their start and end apart: 5, of which 5 were waited for; matrix products, arithmetic and copies ran while one was open for 8% of the time, Pallas kernels for 0%

profile of v7, /device:TPU:0, one launch (start us, length us, event | category | flops | bytes accessed | tf_op | source)
XLA Modules:
  0.0 1004.3 jit_solution(4363353964035950176)
XLA Ops:
  17.4 75.8 %all-gather.5.cloned.1.call-done = bf16[1024,4224]{1,0:T(8,128)(2,1)} async-done(((bf16[32,4224]{1,0:T(8,128)(2,1)}), bf16[1024,4224]{1,0:T(8,128)(2,1)}) %all-gather.5.cloned.1.call-update) | async-done | bytes 8650768 | tf_op jit(solution)/shard_map/all_gather | solution.py:230
  96.8 15.4 %fusion.9 = f32[1024,4096]{1,0:T(8,128)} fusion(bf16[1024,4224]{1,0:T(8,128)(2,1)} %all-gather.5.cloned.1.call-done, bf16[1,1024,1024]{2,1,0:T(8,128)(2,1)S(1)} %copy-done, f32[1024]{0:T(1024)S(1)} %get-tuple-element.33, f32[1024]{0:T(1024)S(1)} %get-tuple-element.34, f32[1024]{0:T(1024)S(1)} %fusion.41, f32[1024]{0:T(1024)S(1)} %broadcast_multiply_fusion), kind=kOutput, calls=%fused_computation.15 | convolution fusion | flops 8596226048 | bytes 27279360 | tf_op jit(solution)/shard_map/dot_general | solution.py:283
  112.1 18.5 %convolution_convert_fusion.1 = bf16[4096,1024]{1,0:T(8,128)(2,1)} fusion(bf16[1,1024,1024]{2,1,0:T(8,128)(2,1)S(1)} %copy-done.3, f32[1024,4096]{1,0:T(8,128)} %fusion.9, f32[4096]{0:T(1024)S(1)} %reshape.479), kind=kOutput, calls=%fused_computation.12 | convolution fusion | flops 8636071936 | bytes 27279360 | tf_op jit(solution)/shard_map/tf,td->fd/dot_general | solution.py:288
  130.6 8.1 concatenate.38
  138.7 73.5 %all-gather.7.cloned.1.call-done = bf16[1024,8448]{1,0:T(8,128)(2,1)} async-done(((bf16[32,8448]{1,0:T(8,128)(2,1)}), bf16[1024,8448]{1,0:T(8,128)(2,1)}) %all-gather.7.cloned.1.call-update) | async-done | bytes 17301520 | tf_op jit(solution)/shard_map/all_gather | solution.py:230
  218.1 8.7 copy.39
  226.8 13.5 %convolution_bitcast_fusion = f32[1,1024,3,16,64]{1,4,3,2,0:T(8,128)} fusion(bf16[3,16,64,1024]{3,2,1,0:T(8,128)(2,1)} %bitcast.130, bf16[1,1024,1024]{2,1,0:T(8,128)(2,1)S(1)} %copy-done, f32[1024]{0:T(1024)S(1)} %get-tuple-element.33, f32[1024]{0:T(1024)S(1)} %get-tuple-element.34, f32[1024]{0:T(1024)S(1)} %fusion.41, f32[1024]{0:T(1024)S(1)} %broadcast_multiply_fusion), kind=kOutput, calls=%fused_computation.30 | convolution fusion | flops 6448742400 | bytes 20987904 | tf_op jit(solution)/shard_map/dot_general | solution.py:299
  271.0 7.9 slice.128
  278.9 13.9 %reshape.459 = bf16[4096,1024]{1,0:T(8,128)(2,1)} reshape(bf16[1024,4096]{1,0:T(8,128)(2,1)} %slice.128) | data formatting | bytes 16777216 | tf_op jit(solution)/shard_map/reshape | solution.py:276
  294.8 25.9 %fusion.50 = (bf16[4096]{0:T(1024)(128)(2,1)S(1)}, bf16[1024,4096]{1,0:T(8,128)(2,1)}) fusion(f32[1024,4096]{1,0:T(8,128)} %fusion.9, f32[4096]{0:T(1024)S(1)} %reshape.479, bf16[1024,1024]{1,0:T(8,128)(2,1)} %bitcast.116, bf16[4096,1024]{1,0:T(8,128)(2,1)} %reshape.459), kind=kOutput, calls=%fused_computation.101 | convolution fusion | flops 8682205184 | bytes 35676160 | tf_op jit(solution)/shard_map/td,fd->tf/dot_general | solution.py:329
  320.7 15.3 %convolution_convert_fusion = bf16[1024,4096]{1,0:T(8,128)(2,1)} fusion(bf16[1024,4096]{1,0:T(8,128)(2,1)} %get-tuple-element.42, bf16[1,1024,1024]{2,1,0:T(8,128)(2,1)S(1)} %copy-done, f32[1024]{0:T(1024)S(1)} %get-tuple-element.33, f32[1024]{0:T(1024)S(1)} %get-tuple-element.34, f32[1024]{0:T(1024)S(1)} %fusion.41, f32[1024]{0:T(1024)S(1)} %broadcast_multiply_fusion), kind=kOutput, calls=%fused_computation.11 | convolution fusion | flops 8600420352 | bytes 18890752 | tf_op jit(solution)/shard_map/te,tf->ef/dot_general | solution.py:333
  336.0 54.0 %shard_map.186 = (bf16[1024,1024]{1,0:T(8,128)(2,1)}, f32[16,1024,1]{2,1,0:T(8,128)}, f32[16,1024,1]{2,1,0:T(8,128)}) custom-call(s32[1]{0:T(128)S(6)} %copy.71.length_ref, bf16[1024,1024]{1,0:T(8,128)(2,1)} %copy.46.q_ref, bf16[1024,1024]{1,0:T(8,128)(2,1)} %copy.47.k_ref, bf16[1024,1024]{1,0:T(8,128)(2,1)} %copy.48.v_ref), custom_call_target="tpu_custom_call" | custom-call | flops 8589934592 | bytes 37748736 | tf_op jit(solution)/shard_map/pallas_call | solution.py:134
  390.0 5.9 convolution_convert_fusion.3
  396.8 17.6 %concatenate.44 = bf16[1024,5376]{1,0:T(8,128)(2,1)} concatenate(bf16[1024,4096]{1,0:T(8,128)(2,1)} %convolution_convert_fusion, bf16[1024,1024]{1,0:T(8,128)(2,1)} %convolution_convert_fusion.3, bf16[1024,4]{1,0:T(8,128)(2,1)S(1)} %reshape.461, bf16[1024,1]{1,0:T(8,128)(2,1)S(1)} %reshape.494, bf16[1024,251]{1,0:T(8,128)(2,1)S(1)} %broadcast_in_dim.20), dimensions={1} | concatenate | bytes 22020096 | tf_op jit(solution)/shard_map/concatenate | solution.py:216
  414.4 5.9 convert_bitcast_fusion.1
  420.3 79.1 %shard_map.187 = (f32[1024,1024]{1,0:T(8,128)}, f32[1024,1024]{1,0:T(8,128)}, f32[1024,1024]{1,0:T(8,128)}) custom-call(s32[1]{0:T(128)S(6)} %copy.71.length_ref, bf16[1024,1024]{1,0:T(8,128)(2,1)} %copy.46.q_ref, bf16[1024,1024]{1,0:T(8,128)(2,1)} %copy.47.k_ref, bf16[1024,1024]{1,0:T(8,128)(2,1)} %copy.48.v_ref, bf16[1024,1024]{1,0:T(8,128)(2,1)} %bitcast.138, ...), custom_call_target="tpu_custom_call" | custom-call | flops 21474836480 | bytes 54525952 | tf_op jit(solution)/shard_map/pallas_call | solution.py:169
  534.7 10.5 %fusion.54 = f32[1024,1024]{1,0:T(8,128)} fusion(bf16[1024,3072]{0,1:T(8,128)(2,1)} %bitcast.128, bf16[1024,3072]{1,0:T(8,128)(2,1)S(1)} %bitcast.112), kind=kOutput, calls=%fused_computation.104 | convolution fusion | flops 6442450944 | bytes 16777216 | tf_op jit(solution)/shard_map/tc,ec->te/dot_general | solution.py:379
  545.2 9.6 convolution_convert_fusion.2
  554.9 12.5 %fusion.49 = (bf16[1024]{0:T(1024)(128)(2,1)S(1)}, f32[1024]{0:T(1024)S(1)}, f32[1024,1024]{1,0:T(8,128)S(1)}) fusion(f32[1024]{0:T(1024)S(1)} %get-tuple-element.34, f32[1024]{0:T(1024)S(1)} %broadcast_multiply_fusion, bf16[1,1024,1024]{2,1,0:T(8,128)(2,1)S(1)} %copy-done, f32[1024,1024]{1,0:T(8,128)} %fusion.54, ...), kind=kOutput, calls=%fused_computation.100 | convolution fusion | flops 8597272576 | bytes 27277312 | tf_op jit(solution)/shard_map/tf,ef->te/dot_general | solution.py:345
  572.4 11.1 %concatenate.45 = bf16[1024,3456]{1,0:T(8,128)(2,1)} concatenate(bf16[1024,3072]{1,0:T(8,128)(2,1)} %convolution_convert_fusion.2, bf16[1024,1]{1,0:T(8,128)(2,1)S(1)} %convert_element_type.290, bf16[1024,1]{1,0:T(8,128)(2,1)S(1)} %convert_element_type.291, bf16[1024,382]{1,0:T(8,128)(2,1)S(1)} %broadcast_in_dim.44), dimensions={1} | concatenate | bytes 14155776 | tf_op jit(solution)/shard_map/concatenate | solution.py:216
  592.3 18.4 %fusion.35 = bf16[1,1024,1024]{2,1,0:T(8,128)(2,1)} fusion(f32[1024,1024]{1,0:T(8,128)S(1)} %fusion.39, bf16[1,1024,1024]{2,1,0:T(8,128)(2,1)S(1)} %copy-done, f32[1024]{0:T(1024)S(1)} %copy-done.13, bf16[4096,1024]{1,0:T(8,128)(2,1)} %reshape.459, f32[1024,4096]{1,0:T(8,128)} %fusion.9, f32[4096]{0:T(1024)S(1)} %copy-done.12), kind=kOutput, calls=%fused_computation.51 | convolution fusion | flops 8637120512 | bytes 33574912 | tf_op jit(solution)/shard_map/dot_general | solution.py:321
  610.7 90.9 %reduce-scatter.4.cloned.1.call-done = bf16[32,3456]{1,0:T(8,128)(2,1)} async-done(((bf16[1024,3456]{1,0:T(8,128)(2,1)}), bf16[32,3456]{1,0:T(8,128)(2,1)}) %reduce-scatter.4.cloned.1.call-update) | async-done | bytes 221200 | tf_op jit(solution)/shard_map/reduce_scatter | solution.py:236
  704.8 138.0 %reduce-scatter.8.cloned.1.call-done = bf16[128,1152]{1,0:T(8,128)(2,1)} async-done(((bf16[4096,1152]{1,0:T(8,128)(2,1)}), bf16[128,1152]{1,0:T(8,128)(2,1)}) %reduce-scatter.8.cloned.1.call-update) | async-done | bytes 294928 | tf_op jit(solution)/shard_map/reduce_scatter | solution.py:236
  844.6 147.0 %reduce-scatter.6.cloned.1.call-done = bf16[32,5376]{1,0:T(8,128)(2,1)} async-done(((bf16[1024,5376]{1,0:T(8,128)(2,1)}), bf16[32,5376]{1,0:T(8,128)(2,1)}) %reduce-scatter.6.cloned.1.call-update) | async-done | bytes 344080 | tf_op jit(solution)/shard_map/reduce_scatter | solution.py:236
  (123 shorter events, 112.2 us)
Async XLA Ops:
  7.2 8.8 copy-start
  7.2 85.9 %all-gather.5.cloned.1.call-start = ((), (), s32[]{:S(2)}) async-start(), calls=%async_computation.6 | async-start | bytes 8921088 | tf_op jit(solution)/shard_map/all_gather | solution.py:230
  12.2 200.1 %all-gather.7.cloned.1.call-start = ((), (), s32[]{:S(2)}) async-start(), calls=%async_computation.7 | async-start | bytes 17842176 | tf_op jit(solution)/shard_map/all_gather | solution.py:230
  15.3 686.3 %reduce-scatter.4.cloned.1.call-start = ((), (), s32[]{:S(2)}) async-start(), calls=%async_computation.3 | async-start | bytes 7299072 | tf_op jit(solution)/shard_map/reduce_scatter | solution.py:236
  17.0 77.2 %copy-start.9 = (f32[1024]{0:T(1024)}, f32[1024]{0:T(1024)S(1)}, u32[]{:S(2)}) copy-start(f32[1024]{0:T(1024)S(1)} %fusion.22) | copy-start | bytes 12292
  94.5 200.3 %copy-start.11 = (f32[4096]{0:T(1024)}, f32[4096]{0:T(1024)S(1)}, u32[]{:S(2)}) copy-start(f32[4096]{0:T(1024)S(1)} %reshape.479) | copy-start | bytes 49156
  96.7 15.4 %copy-start.3 = (bf16[1,1024,1024]{2,1,0:T(8,128)(2,1)S(1)}, bf16[1,1024,1024]{2,1,0:T(8,128)(2,1)}, u32[]{:S(2)}) copy-start(bf16[1,1024,1024]{2,1,0:T(8,128)(2,1)} %param.21) | copy-start | bytes 6291460
  524.0 1.6 copy-start.7
  529.0 1.6 copy-start.6
  529.4 2.0 copy-start.5
  530.6 4.0 slice-start
  531.4 3.3 slice-start.1
  534.7 10.5 %copy-start.8 = (bf16[1,1024,3,16,64]{1,4,3,2,0:T(8,128)(2,1)S(1)}, bf16[1,1024,3,16,64]{1,4,3,2,0:T(8,128)(2,1)}, u32[]{:S(2)}) copy-start(bf16[1,1024,3,16,64]{1,4,3,2,0:T(8,128)(2,1)} %maximum_convert_fusion) | copy-start | bytes 18874372
  534.7 20.2 %slice-start.2 = ((s8[8650752]{0:T(1024)(128)(4,1)}), s8[262144]{0:T(1024)(128)(4,1)S(1)}, s32[]{:S(2)}) async-start(s8[8650752]{0:T(1024)(128)(4,1)} %bitcast.133), calls=%async_computation.10 | async-start | bytes 524288
  534.7 20.2 %slice-start.3 = ((s8[8650752]{0:T(1024)(128)(4,1)}), s8[4194304]{0:T(1024)(128)(4,1)S(1)}, s32[]{:S(2)}) async-start(s8[8650752]{0:T(1024)(128)(4,1)} %bitcast.133), calls=%async_computation.11 | async-start | bytes 8388608
  545.2 9.7 slice-start.4
  554.9 12.5 %copy-start.10 = (f32[1024]{0:T(1024)S(1)}, f32[1024]{0:T(1024)}, u32[]{:S(2)}) copy-start(f32[1024]{0:T(1024)} %copy-done.9) | copy-start | bytes 12292
  567.4 2.0 copy-start.1
  583.6 259.2 %reduce-scatter.8.cloned.1.call-start = ((), (), s32[]{:S(2)}) async-start(), calls=%async_computation.5 | async-start | bytes 9732096 | tf_op jit(solution)/shard_map/reduce_scatter | solution.py:236
  584.2 407.4 %reduce-scatter.6.cloned.1.call-start = ((), (), s32[]{:S(2)}) async-start(), calls=%async_computation.4 | async-start | bytes 11354112 | tf_op jit(solution)/shard_map/reduce_scatter | solution.py:236
  584.8 4.7 copy-start.2
  584.8 4.7 copy-start.4
  589.5 2.8 copy-start.12
  589.5 2.8 copy-start.13
Sparse Core Ops, SparseCore 0:
  12.3 80.7 all-gather.4
  96.7 115.4 all-gather.6
  583.7 117.8 reduce-scatter.3
  707.3 135.4 reduce-scatter.7
  848.6 142.8 reduce-scatter.5

commit v8 on v6

--- a/solution.py
+++ b/solution.py
@@ -206,11 +206,12 @@
 
 
 COLUMNS = 384
-
-
-def pad_columns(blocks):
+GATHER_COLUMNS = 128
+
+
+def pad_columns(blocks, multiple=COLUMNS):
     width = sum(block.shape[1] for block in blocks)
-    extra = -width % COLUMNS
+    extra = -width % multiple
     if extra:
         blocks = blocks + [jnp.zeros((blocks[0].shape[0], extra), blocks[0].dtype)]
     return jnp.concatenate(blocks, axis=1)
@@ -226,7 +227,7 @@
 
 
 def gather_columns(blocks):
-    packed = pad_columns(blocks)
+    packed = pad_columns(blocks, GATHER_COLUMNS)
     full = lax.all_gather(packed[None], ALL, axis=0, tiled=True)
     full = full.reshape(full.shape[0] * full.shape[1], full.shape[2])
     return split_columns(full, [block.shape[1] for block in blocks])
@@ -333,7 +334,6 @@
     inner_grad = jnp.sum(hidden_grad, axis=0, dtype=jnp.float32)
     early = [
         expand_grad.astype(jnp.bfloat16),
-        project_grad.astype(jnp.bfloat16),
         as_column(inner_grad.astype(jnp.bfloat16), rows_all),
         as_column(outer_grad.astype(jnp.bfloat16), rows_all),
     ]
@@ -345,7 +345,7 @@
     mixed_grad = jnp.einsum("td,ed->te", upstream, project_full, preferred_element_type=jnp.float32)
     mixed_grad = mixed_grad.astype(jnp.bfloat16).reshape(seq_dev, seq_len, width)
     early_packed, mixed_grad = lax.optimization_barrier((early_packed, mixed_grad))
-    expand_part, project_part, inner_part, outer_part = scatter_columns(early_packed, early_widths)
+    expand_part, inner_part, outer_part = scatter_columns(early_packed, early_widths)
     inner_part = inner_part.reshape(-1)
     outer_part = outer_part.reshape(-1)
     backward_parts = [
@@ -382,10 +382,11 @@
     )
     late = [
         attend_grad.astype(jnp.bfloat16),
+        project_grad.astype(jnp.bfloat16),
         as_column(gain_grad.astype(jnp.bfloat16), rows_all),
         as_column(shift_grad.astype(jnp.bfloat16), rows_all),
     ]
-    attend_part, gain_part, shift_part = scatter_columns(
+    attend_part, project_part, gain_part, shift_part = scatter_columns(
         pad_columns(late), [block.shape[1] for block in late]
     )
     gain_part = gain_part.reshape(-1)

time: 917 us -> 825 us (0.90)
  waiting for transfers between devices: 458 us -> 365 us
    reduce_scatter x3, waiting for transfers between devices: 376 us -> 237 us  [scatter_columns(): summed = lax.psum_scatter(packed, ALL, scatter_dimension=0, tiled=True)]
    all_gather x3, waiting for transfers between devices: 81 us -> 127 us  [gather_columns(): full = lax.all_gather(packed[None], ALL, axis=0, tiled=True)]
    concatenate x6 -> x4, local copies, waits for them, and re-layouts: 40.2 us -> 37.1 us  [pad_columns(): return jnp.concatenate(blocks, axis=1)]
  transfers between devices with their start and end apart: 6 -> 6, of which waited for: 5 -> 5; matrix products, arithmetic and copies ran while one was open for 16% -> 29% of each run, Pallas kernels for 6% -> 16%
where the time goes in v8:
time: 825 us; the launch traced here: 820 us
  waiting for transfers between devices  365 us (44%)
  matrix products  156 us (19%)
  Pallas kernels  133 us (16%)
  local copies, waits for them, and re-layouts  115 us (14%)
  other arithmetic  35.7 us (4%)
  between operations  15.5 us (2%)
    reduce_scatter x3, waiting for transfers between devices, scatter_columns(): summed = lax.psum_scatter(packed, ALL, scatter_dimension=0, tiled=True)  237 us
    all_gather x3, waiting for transfers between devices, gather_columns(): full = lax.all_gather(packed[None], ALL, axis=0, tiled=True)  127 us
    pallas_call x1, Pallas kernels, attention_backward(): pl.pallas_call(attention_backward_kernel, out_shape=(jax.ShapeDtypeStruct...  78.7 us
    pallas_call x1, Pallas kernels, attention_forward(): pl.pallas_call(attention_forward_kernel, out_shape=(jax.ShapeDtypeStruct(...  54.4 us
    concatenate x4, local copies, waits for them, and re-layouts, pad_columns(): return jnp.concatenate(blocks, axis=1)  37.1 us
    dot_general x1, matrix products, body(): jnp.einsum('td,fd->tf', upstream_back, contract_full, preferred_element_t...  26 us
    dot_general x1, matrix products, body(): jnp.einsum('tf,td->fd', active_low, upstream, preferred_element_type=jnp....  18.5 us
    dot_general x1, matrix products, body(): jnp.dot(active_low, contract_full, preferred_element_type=jnp.float32)  18.4 us
  transfers between devices with their start and end apart: 6, of which 5 were waited for; matrix products, arithmetic and copies ran while one was open for 29% of the time, Pallas kernels for 16%

profile of v8, /device:TPU:0, one launch (start us, length us, event | category | flops | bytes accessed | tf_op | source)
XLA Modules:
  0.0 820.3 jit_solution(76994555506703625)
XLA Ops:
  18.4 66.9 %all-gather.7.cloned.1.call-done = bf16[1024,3200]{1,0:T(8,128)(2,1)} async-done(((bf16[32,3200]{1,0:T(8,128)(2,1)}), bf16[1024,3200]{1,0:T(8,128)(2,1)}) %all-gather.7.cloned.1.call-update) | async-done | bytes 6553616 | tf_op jit(solution)/shard_map/all_gather | solution.py:231
  85.3 5.9 slice_bitcast_fusion
  91.2 9.0 %copy.39 = bf16[3072,1024]{1,0:T(8,128)(2,1)} copy(bf16[3072,1024]{0,1:T(8,128)(2,1)} %slice_bitcast_fusion) | data formatting | bytes 12582912 | tf_op jit(solution)/shard_map/dot_general | solution.py:281
  102.4 13.0 %convolution_bitcast_fusion = f32[1,1024,3,16,64]{1,4,3,2,0:T(8,128)} fusion(bf16[3,16,64,1024]{3,2,1,0:T(8,128)(2,1)} %bitcast.131, bf16[1,1024,1024]{2,1,0:T(8,128)(2,1)S(1)} %copy-done, f32[1024]{0:T(1024)S(1)} %get-tuple-element.31, f32[1024]{0:T(1024)S(1)} %get-tuple-element.32, f32[1024]{0:T(1024)S(1)} %fusion.43, f32[1024]{0:T(1024)S(1)} %broadcast_multiply_fusion), kind=kOutput, calls=%fused_computation.33 | convolution fusion | flops 6448742400 | bytes 20987904 | tf_op jit(solution)/shard_map/dot_general | solution.py:281
  148.0 25.5 %all-gather.9.cloned.1.call-done = bf16[1024,5120]{1,0:T(8,128)(2,1)} async-done(((bf16[32,5120]{1,0:T(8,128)(2,1)}), bf16[1024,5120]{1,0:T(8,128)(2,1)}) %all-gather.9.cloned.1.call-update) | async-done | bytes 10485776 | tf_op jit(solution)/shard_map/all_gather | solution.py:231
  173.5 15.1 %fusion.9 = f32[1024,4096]{1,0:T(8,128)} fusion(bf16[1024,5120]{1,0:T(8,128)(2,1)} %all-gather.9.cloned.1.call-done, bf16[1,1024,1024]{2,1,0:T(8,128)(2,1)S(1)} %copy-done, f32[1024]{0:T(1024)S(1)} %get-tuple-element.31, f32[1024]{0:T(1024)S(1)} %get-tuple-element.32, f32[1024]{0:T(1024)S(1)} %fusion.43, f32[1024]{0:T(1024)S(1)} %broadcast_multiply_fusion), kind=kOutput, calls=%fused_computation.15 | convolution fusion | flops 8596226048 | bytes 27279360 | tf_op jit(solution)/shard_map/dot_general | solution.py:301
  188.6 18.5 %convolution_convert_fusion.1 = bf16[4096,1024]{1,0:T(8,128)(2,1)} fusion(bf16[1,1024,1024]{2,1,0:T(8,128)(2,1)S(1)} %copy-done.3, f32[1024,4096]{1,0:T(8,128)} %fusion.9, f32[4096]{0:T(1024)S(1)} %reshape.475), kind=kOutput, calls=%fused_computation.12 | convolution fusion | flops 8636071936 | bytes 27279360 | tf_op jit(solution)/shard_map/tf,td->fd/dot_general | solution.py:314
  207.1 8.2 concatenate.43
  217.2 34.9 %all-gather.11.cloned.1.call-done = bf16[4096,1024]{1,0:T(8,128)(2,1)} async-done(((bf16[128,1024]{1,0:T(8,128)(2,1)}), bf16[4096,1024]{1,0:T(8,128)(2,1)}) %all-gather.11.cloned.1.call-update) | async-done | bytes 8388624 | tf_op jit(solution)/shard_map/all_gather | solution.py:231
  252.1 26.0 %fusion.52 = (bf16[4096]{0:T(1024)(128)(2,1)S(1)}, bf16[1024,4096]{1,0:T(8,128)(2,1)}) fusion(f32[1024,4096]{1,0:T(8,128)} %fusion.9, f32[4096]{0:T(1024)S(1)} %reshape.475, bf16[1024,1024]{1,0:T(8,128)(2,1)} %bitcast.113, bf16[4096,1024]{1,0:T(8,128)(2,1)} %all-gather.11.cloned.1.call-done), kind=kOutput, calls=%fused_computation.104 | convolution fusion | flops 8682205184 | bytes 35676160 | tf_op jit(solution)/shard_map/td,fd->tf/dot_general | solution.py:327
  278.1 15.3 %convolution_convert_fusion = bf16[1024,4096]{1,0:T(8,128)(2,1)} fusion(bf16[1024,4096]{1,0:T(8,128)(2,1)} %get-tuple-element.40, bf16[1,1024,1024]{2,1,0:T(8,128)(2,1)S(1)} %copy-done, f32[1024]{0:T(1024)S(1)} %get-tuple-element.31, f32[1024]{0:T(1024)S(1)} %get-tuple-element.32, f32[1024]{0:T(1024)S(1)} %fusion.43, f32[1024]{0:T(1024)S(1)} %broadcast_multiply_fusion), kind=kOutput, calls=%fused_computation.11 | convolution fusion | flops 8600420352 | bytes 18890752 | tf_op jit(solution)/shard_map/te,tf->ef/dot_general | solution.py:331
  294.3 13.7 %concatenate.44 = bf16[1024,4224]{1,0:T(8,128)(2,1)} concatenate(bf16[1024,4096]{1,0:T(8,128)(2,1)} %convolution_convert_fusion, bf16[1024,4]{1,0:T(8,128)(2,1)S(1)} %reshape.457, bf16[1024,1]{1,0:T(8,128)(2,1)S(1)} %reshape.492, bf16[1024,123]{1,0:T(8,128)(2,1)S(1)} %broadcast_in_dim.20), dimensions={1} | concatenate | bytes 17301504 | tf_op jit(solution)/shard_map/concatenate | solution.py:217
  308.0 5.9 convert_bitcast_fusion.1
  314.0 54.4 %shard_map.186 = (bf16[1024,1024]{1,0:T(8,128)(2,1)}, f32[16,1024,1]{2,1,0:T(8,128)}, f32[16,1024,1]{2,1,0:T(8,128)}) custom-call(s32[1]{0:T(128)S(6)} %copy.71.length_ref, bf16[1024,1024]{1,0:T(8,128)(2,1)} %copy.46.q_ref, bf16[1024,1024]{1,0:T(8,128)(2,1)} %copy.47.k_ref, bf16[1024,1024]{1,0:T(8,128)(2,1)} %copy.48.v_ref), custom_call_target="tpu_custom_call" | custom-call | flops 8589934592 | bytes 37748736 | tf_op jit(solution)/shard_map/pallas_call | solution.py:134
  368.3 78.7 %shard_map.187 = (f32[1024,1024]{1,0:T(8,128)}, f32[1024,1024]{1,0:T(8,128)}, f32[1024,1024]{1,0:T(8,128)}) custom-call(s32[1]{0:T(128)S(6)} %copy.71.length_ref, bf16[1024,1024]{1,0:T(8,128)(2,1)} %copy.46.q_ref, bf16[1024,1024]{1,0:T(8,128)(2,1)} %copy.47.k_ref, bf16[1024,1024]{1,0:T(8,128)(2,1)} %copy.48.v_ref, bf16[1024,1024]{1,0:T(8,128)(2,1)} %bitcast.137, ...), custom_call_target="tpu_custom_call" | custom-call | flops 21474836480 | bytes 54525952 | tf_op jit(solution)/shard_map/pallas_call | solution.py:169
  451.6 5.3 copy.54
  463.5 5.8 copy.57
  483.0 10.2 %fusion.11 = f32[1024,1024]{1,0:T(8,128)} fusion(bf16[1024,3072]{0,1:T(8,128)(2,1)} %bitcast.127, bf16[1024,3200]{1,0:T(8,128)(2,1)S(1)} %bitcast.126), kind=kOutput, calls=%fused_computation.22 | convolution fusion | flops 6442450944 | bytes 16777216 | tf_op jit(solution)/shard_map/tc,ec->te/dot_general | solution.py:376
  493.2 15.0 %fusion.51 = (bf16[1024]{0:T(1024)(128)(2,1)S(1)}, f32[1024]{0:T(1024)S(1)}, f32[1024,1024]{1,0:T(8,128)S(1)}) fusion(f32[1024]{0:T(1024)S(1)} %get-tuple-element.32, f32[1024]{0:T(1024)S(1)} %broadcast_multiply_fusion, bf16[1,1024,1024]{2,1,0:T(8,128)(2,1)S(1)} %copy-done, f32[1024,1024]{1,0:T(8,128)} %fusion.11, ...), kind=kOutput, calls=%fused_computation.103 | convolution fusion | flops 8597272576 | bytes 27277312 | tf_op jit(solution)/shard_map/tf,ef->te/dot_general | solution.py:342
  515.8 9.6 %convolution_convert_fusion.2 = bf16[1024,3072]{1,0:T(8,128)(2,1)} fusion(bf16[1024,3072]{0,1:T(8,128)(2,1)S(1)} %bitcast.130, bf16[1,1024,1024]{2,1,0:T(8,128)(2,1)S(1)} %copy-done, f32[1024]{0:T(1024)S(1)} %get-tuple-element.31, f32[1024]{0:T(1024)S(1)} %get-tuple-element.32, f32[1024]{0:T(1024)S(1)} %fusion.43, f32[1024]{0:T(1024)S(1)} %broadcast_multiply_fusion), kind=kOutput, calls=%fused_computation.21 | convolution fusion | flops 6451888128 | bytes 14696448 | tf_op jit(solution)/shard_map/te,tc->ec/dot_general | solution.py:373
  525.4 13.5 %concatenate.45 = bf16[1024,4224]{1,0:T(8,128)(2,1)} concatenate(bf16[1024,3072]{1,0:T(8,128)(2,1)} %convolution_convert_fusion.2, bf16[1024,1024]{1,0:T(8,128)(2,1)} %convolution_convert_fusion.3, bf16[1024,1]{1,0:T(8,128)(2,1)S(1)} %convert_element_type.290, bf16[1024,1]{1,0:T(8,128)(2,1)S(1)} %convert_element_type.291, bf16[1024,126]{1,0:T(8,128)(2,1)S(1)} %broadcast_in_dim.44), dimensions={1} | concatenate | bytes 17301504 | tf_op jit(solution)/shard_map/concatenate | solution.py:217
  547.1 18.4 %fusion.37 = bf16[1,1024,1024]{2,1,0:T(8,128)(2,1)} fusion(f32[1024,1024]{1,0:T(8,128)S(1)} %fusion.41, bf16[1,1024,1024]{2,1,0:T(8,128)(2,1)S(1)} %copy-done, f32[1024]{0:T(1024)S(1)} %copy-done.17, bf16[4096,1024]{1,0:T(8,128)(2,1)} %all-gather.11.cloned.1.call-done, f32[1024,4096]{1,0:T(8,128)} %fusion.9, f32[4096]{0:T(1024)S(1)} %copy-done.16), kind=kOutput, calls=%fused_computation.54 | convolution fusion | flops 8637120512 | bytes 33574912 | tf_op jit(solution)/shard_map/dot_general | solution.py:309
  568.3 102.3 %reduce-scatter.4.cloned.1.call-done = bf16[32,4224]{1,0:T(8,128)(2,1)} async-done(((bf16[1024,4224]{1,0:T(8,128)(2,1)}), bf16[32,4224]{1,0:T(8,128)(2,1)}) %reduce-scatter.4.cloned.1.call-update) | async-done | bytes 270352 | tf_op jit(solution)/shard_map/reduce_scatter | solution.py:237
  677.1 134.4 %reduce-scatter.8.cloned.1.call-done = bf16[128,1152]{1,0:T(8,128)(2,1)} async-done(((bf16[4096,1152]{1,0:T(8,128)(2,1)}), bf16[128,1152]{1,0:T(8,128)(2,1)}) %reduce-scatter.8.cloned.1.call-update) | async-done | bytes 294928 | tf_op jit(solution)/shard_map/reduce_scatter | solution.py:237
  (129 shorter events, 99.3 us)
Async XLA Ops:
  7.2 10.2 %copy-start = (bf16[1,1024,1024]{2,1,0:T(8,128)(2,1)S(1)}, bf16[1,1024,1024]{2,1,0:T(8,128)(2,1)}, u32[]{:S(2)}) copy-start(bf16[1,1024,1024]{2,1,0:T(8,128)(2,1)} %param.11) | copy-start | bytes 6291460
  7.2 78.2 %all-gather.7.cloned.1.call-start = ((), (), s32[]{:S(2)}) async-start(), calls=%async_computation.6 | async-start | bytes 6758400 | tf_op jit(solution)/shard_map/all_gather | solution.py:231
  12.1 161.4 %all-gather.9.cloned.1.call-start = ((), (), s32[]{:S(2)}) async-start(), calls=%async_computation.7 | async-start | bytes 10813440 | tf_op jit(solution)/shard_map/all_gather | solution.py:231
  13.9 238.2 %all-gather.11.cloned.1.call-start = ((), (), s32[]{:S(2)}) async-start(), calls=%async_computation.8 | async-start | bytes 8650752 | tf_op jit(solution)/shard_map/all_gather | solution.py:231
  14.7 550.9 %reduce-scatter.6.cloned.1.call-start = ((), (), s32[]{:S(2)}) async-start(), calls=%async_computation.4 | async-start | bytes 8921088 | tf_op jit(solution)/shard_map/reduce_scatter | solution.py:237
  18.0 73.2 %copy-start.13 = (f32[1024]{0:T(1024)}, f32[1024]{0:T(1024)S(1)}, u32[]{:S(2)}) copy-start(f32[1024]{0:T(1024)S(1)} %fusion.24) | copy-start | bytes 12292
  18.4 108.3 %copy-start.9 = (f32[1024,16]{0,1:T(8,128)}, f32[1024,16]{0,1:T(8,128)S(1)}, u32[]{:S(2)}) copy-start(f32[1024,16]{0,1:T(8,128)S(1)} %get-tuple-element.59) | copy-start | bytes 196612
  18.4 108.3 %copy-start.11 = (f32[1024,16]{0,1:T(8,128)}, f32[1024,16]{0,1:T(8,128)S(1)}, u32[]{:S(2)}) copy-start(f32[1024,16]{0,1:T(8,128)S(1)} %get-tuple-element.60) | copy-start | bytes 196612
  148.0 104.1 %copy-start.15 = (f32[4096]{0:T(1024)}, f32[4096]{0:T(1024)S(1)}, u32[]{:S(2)}) copy-start(f32[4096]{0:T(1024)S(1)} %reshape.475) | copy-start | bytes 49156
  173.5 15.1 %copy-start.3 = (bf16[1,1024,1024]{2,1,0:T(8,128)(2,1)S(1)}, bf16[1,1024,1024]{2,1,0:T(8,128)(2,1)}, u32[]{:S(2)}) copy-start(bf16[1,1024,1024]{2,1,0:T(8,128)(2,1)} %param.21) | copy-start | bytes 6291460
  313.9 356.7 %reduce-scatter.4.cloned.1.call-start = ((), (), s32[]{:S(2)}) async-start(), calls=%async_computation.3 | async-start | bytes 8921088 | tf_op jit(solution)/shard_map/reduce_scatter | solution.py:237
  478.8 4.1 slice-start
  479.5 3.5 slice-start.1
  493.2 15.1 %copy-start.14 = (f32[1024]{0:T(1024)S(1)}, f32[1024]{0:T(1024)}, u32[]{:S(2)}) copy-start(f32[1024]{0:T(1024)} %copy-done.13) | copy-start | bytes 12292
  508.3 7.5 copy-start.1
  508.3 3.1 copy-start.4
  508.3 3.7 copy-start.18
  508.3 7.5 slice-start.2
  512.0 3.8 slice-start.3
  539.0 272.5 %reduce-scatter.8.cloned.1.call-start = ((), (), s32[]{:S(2)}) async-start(), calls=%async_computation.5 | async-start | bytes 9732096 | tf_op jit(solution)/shard_map/reduce_scatter | solution.py:237
  539.6 4.7 copy-start.2
  539.6 4.7 copy-start.5
  544.3 2.8 copy-start.16
  544.3 2.8 copy-start.17
  (5 other events, 8.3 us)
Sparse Core Ops, SparseCore 0:
  12.2 73.0 all-gather.6
  88.8 84.6 all-gather.8
  176.5 75.6 all-gather.10
  314.0 131.4 reduce-scatter.5
  539.1 131.4 reduce-scatter.3
  676.4 135.0 reduce-scatter.7

commit v9 on v8

--- a/solution.py
+++ b/solution.py
@@ -207,6 +207,7 @@
 
 COLUMNS = 384
 GATHER_COLUMNS = 128
+PROJECT_LATE = 382
 
 
 def pad_columns(blocks, multiple=COLUMNS):
@@ -334,6 +335,7 @@
     inner_grad = jnp.sum(hidden_grad, axis=0, dtype=jnp.float32)
     early = [
         expand_grad.astype(jnp.bfloat16),
+        project_grad.astype(jnp.bfloat16)[:, PROJECT_LATE:],
         as_column(inner_grad.astype(jnp.bfloat16), rows_all),
         as_column(outer_grad.astype(jnp.bfloat16), rows_all),
     ]
@@ -345,7 +347,7 @@
     mixed_grad = jnp.einsum("td,ed->te", upstream, project_full, preferred_element_type=jnp.float32)
     mixed_grad = mixed_grad.astype(jnp.bfloat16).reshape(seq_dev, seq_len, width)
     early_packed, mixed_grad = lax.optimization_barrier((early_packed, mixed_grad))
-    expand_part, inner_part, outer_part = scatter_columns(early_packed, early_widths)
+    expand_part, project_part, inner_part, outer_part = scatter_columns(early_packed, early_widths)
     inner_part = inner_part.reshape(-1)
     outer_part = outer_part.reshape(-1)
     backward_parts = [
@@ -382,15 +384,16 @@
     )
     late = [
         attend_grad.astype(jnp.bfloat16),
-        project_grad.astype(jnp.bfloat16),
         as_column(gain_grad.astype(jnp.bfloat16), rows_all),
         as_column(shift_grad.astype(jnp.bfloat16), rows_all),
+        project_grad.astype(jnp.bfloat16)[:, :PROJECT_LATE],
     ]
-    attend_part, project_part, gain_part, shift_part = scatter_columns(
+    attend_part, gain_part, shift_part, project_head = scatter_columns(
         pad_columns(late), [block.shape[1] for block in late]
     )
     gain_part = gain_part.reshape(-1)
     shift_part = shift_part.reshape(-1)
+    project_part = jnp.concatenate([project_head, project_part], axis=1)
     return (
         output,
         token_grad,

time: 825 us -> 899 us (1.090)
  waiting for transfers between devices: 365 us -> 440 us
    reduce_scatter x3, waiting for transfers between devices: 237 us -> 371 us  [scatter_columns(): summed = lax.psum_scatter(packed, ALL, scatter_dimension=0, tiled=True)]
    all_gather x3, waiting for transfers between devices: 127 us -> 66.9 us  [gather_columns(): full = lax.all_gather(packed[None], ALL, axis=0, tiled=True)]
  transfers between devices with their start and end apart: 6 -> 6, of which waited for: 5 -> 4; matrix products, arithmetic and copies ran while one was open for 29% -> 17% of each run, Pallas kernels for 16% -> 6%
where the time goes in v9:
time: 899 us; the launch traced here: 894 us
  waiting for transfers between devices  440 us (49%)
  matrix products  155 us (17%)
  Pallas kernels  133 us (15%)
  local copies, waits for them, and re-layouts  119 us (13%)
  other arithmetic  32.6 us (4%)
  between operations  15.5 us (2%)
    reduce_scatter x3, waiting for transfers between devices, scatter_columns(): summed = lax.psum_scatter(packed, ALL, scatter_dimension=0, tiled=True)  371 us
    pallas_call x1, Pallas kernels, attention_backward(): pl.pallas_call(attention_backward_kernel, out_shape=(jax.ShapeDtypeStruct...  78.6 us
    all_gather x3, waiting for transfers between devices, gather_columns(): full = lax.all_gather(packed[None], ALL, axis=0, tiled=True)  66.9 us
    pallas_call x1, Pallas kernels, attention_forward(): pl.pallas_call(attention_forward_kernel, out_shape=(jax.ShapeDtypeStruct(...  54 us
    concatenate x4, local copies, waits for them, and re-layouts, pad_columns(): return jnp.concatenate(blocks, axis=1)  36.4 us
    dot_general x1, matrix products, body(): jnp.einsum('td,fd->tf', upstream_back, contract_full, preferred_element_t...  25.8 us
    dot_general x1, matrix products, body(): jnp.einsum('tf,td->fd', active_low, upstream, preferred_element_type=jnp....  18.7 us
    dot_general x1, matrix products, body(): jnp.dot(active_low, contract_full, preferred_element_type=jnp.float32)  18.3 us
  transfers between devices with their start and end apart: 6, of which 4 were waited for; matrix products, arithmetic and copies ran while one was open for 17% of the time, Pallas kernels for 6%

profile of v9, /device:TPU:0, one launch (start us, length us, event | category | flops | bytes accessed | tf_op | source)
XLA Modules:
  0.0 894.3 jit_solution(17710734877509385865)
XLA Ops:
  18.4 66.9 %all-gather.7.cloned.1.call-done = bf16[1024,3200]{1,0:T(8,128)(2,1)} async-done(((bf16[32,3200]{1,0:T(8,128)(2,1)}), bf16[1024,3200]{1,0:T(8,128)(2,1)}) %all-gather.7.cloned.1.call-update) | async-done | bytes 6553616 | tf_op jit(solution)/shard_map/all_gather | solution.py:232
  85.3 5.8 slice_bitcast_fusion
  91.2 9.2 %copy.39 = bf16[3072,1024]{1,0:T(8,128)(2,1)} copy(bf16[3072,1024]{0,1:T(8,128)(2,1)} %slice_bitcast_fusion) | data formatting | bytes 12582912 | tf_op jit(solution)/shard_map/dot_general | solution.py:282
  102.6 13.0 %convolution_bitcast_fusion = f32[1,1024,3,16,64]{1,4,3,2,0:T(8,128)} fusion(bf16[3,16,64,1024]{3,2,1,0:T(8,128)(2,1)} %bitcast.129, bf16[1,1024,1024]{2,1,0:T(8,128)(2,1)S(1)} %copy-done, f32[1024]{0:T(1024)S(1)} %get-tuple-element.31, f32[1024]{0:T(1024)S(1)} %get-tuple-element.32, f32[1024]{0:T(1024)S(1)} %fusion.43, f32[1024]{0:T(1024)S(1)} %broadcast_multiply_fusion), kind=kOutput, calls=%fused_computation.33 | convolution fusion | flops 6448742400 | bytes 20987904 | tf_op jit(solution)/shard_map/dot_general | solution.py:282
  147.8 54.0 %shard_map.186 = (bf16[1024,1024]{1,0:T(8,128)(2,1)}, f32[16,1024,1]{2,1,0:T(8,128)}, f32[16,1024,1]{2,1,0:T(8,128)}) custom-call(s32[1]{0:T(128)S(6)} %copy.71.length_ref, bf16[1024,1024]{1,0:T(8,128)(2,1)} %copy.46.q_ref, bf16[1024,1024]{1,0:T(8,128)(2,1)} %copy.47.k_ref, bf16[1024,1024]{1,0:T(8,128)(2,1)} %copy.48.v_ref), custom_call_target="tpu_custom_call" | custom-call | flops 8589934592 | bytes 37748736 | tf_op jit(solution)/shard_map/pallas_call | solution.py:134
  201.9 15.0 %fusion.9 = f32[1024,4096]{1,0:T(8,128)} fusion(bf16[1024,5120]{1,0:T(8,128)(2,1)} %all-gather.9.cloned.1.call-done, bf16[1,1024,1024]{2,1,0:T(8,128)(2,1)S(1)} %copy-done, f32[1024]{0:T(1024)S(1)} %get-tuple-element.31, f32[1024]{0:T(1024)S(1)} %get-tuple-element.32, f32[1024]{0:T(1024)S(1)} %fusion.43, f32[1024]{0:T(1024)S(1)} %broadcast_multiply_fusion), kind=kOutput, calls=%fused_computation.15 | convolution fusion | flops 8596226048 | bytes 27279360 | tf_op jit(solution)/shard_map/dot_general | solution.py:302
  216.8 18.7 %convolution_convert_fusion.1 = bf16[4096,1024]{1,0:T(8,128)(2,1)} fusion(bf16[1,1024,1024]{2,1,0:T(8,128)(2,1)S(1)} %copy-done.3, f32[1024,4096]{1,0:T(8,128)} %fusion.9, f32[4096]{0:T(1024)S(1)} %reshape.475), kind=kOutput, calls=%fused_computation.12 | convolution fusion | flops 8636071936 | bytes 27279360 | tf_op jit(solution)/shard_map/tf,td->fd/dot_general | solution.py:315
  235.5 8.1 concatenate.49
  252.2 25.8 %fusion.52 = (bf16[4096]{0:T(1024)(128)(2,1)S(1)}, bf16[1024,4096]{1,0:T(8,128)(2,1)}) fusion(f32[1024,4096]{1,0:T(8,128)} %fusion.9, f32[4096]{0:T(1024)S(1)} %reshape.475, bf16[1024,1024]{1,0:T(8,128)(2,1)} %bitcast.114, bf16[4096,1024]{1,0:T(8,128)(2,1)} %all-gather.11.cloned.1.call-done), kind=kOutput, calls=%fused_computation.104 | convolution fusion | flops 8682205184 | bytes 35676160 | tf_op jit(solution)/shard_map/td,fd->tf/dot_general | solution.py:328
  278.0 15.4 %convolution_convert_fusion = bf16[1024,4096]{1,0:T(8,128)(2,1)} fusion(bf16[1024,4096]{1,0:T(8,128)(2,1)} %get-tuple-element.40, bf16[1,1024,1024]{2,1,0:T(8,128)(2,1)S(1)} %copy-done, f32[1024]{0:T(1024)S(1)} %get-tuple-element.31, f32[1024]{0:T(1024)S(1)} %get-tuple-element.32, f32[1024]{0:T(1024)S(1)} %fusion.43, f32[1024]{0:T(1024)S(1)} %broadcast_multiply_fusion), kind=kOutput, calls=%fused_computation.11 | convolution fusion | flops 8600420352 | bytes 18890752 | tf_op jit(solution)/shard_map/te,tf->ef/dot_general | solution.py:332
  294.2 15.6 %concatenate.50 = bf16[1024,4992]{1,0:T(8,128)(2,1)} concatenate(bf16[1024,4096]{1,0:T(8,128)(2,1)} %convolution_convert_fusion, bf16[1024,642]{1,0:T(8,128)(2,1)} %slice.137, bf16[1024,4]{1,0:T(8,128)(2,1)S(1)} %reshape.457, bf16[1024,1]{1,0:T(8,128)(2,1)S(1)} %reshape.492, bf16[1024,249]{1,0:T(8,128)(2,1)S(1)} %broadcast_in_dim.18), dimensions={1} | concatenate | bytes 20447232 | tf_op jit(solution)/shard_map/concatenate | solution.py:218
  309.8 5.9 convert_bitcast_fusion.1
  315.7 78.6 %shard_map.187 = (f32[1024,1024]{1,0:T(8,128)}, f32[1024,1024]{1,0:T(8,128)}, f32[1024,1024]{1,0:T(8,128)}) custom-call(s32[1]{0:T(128)S(6)} %copy.71.length_ref, bf16[1024,1024]{1,0:T(8,128)(2,1)} %copy.46.q_ref, bf16[1024,1024]{1,0:T(8,128)(2,1)} %copy.47.k_ref, bf16[1024,1024]{1,0:T(8,128)(2,1)} %copy.48.v_ref, bf16[1024,1024]{1,0:T(8,128)(2,1)} %bitcast.135, ...), custom_call_target="tpu_custom_call" | custom-call | flops 21474836480 | bytes 54525952 | tf_op jit(solution)/shard_map/pallas_call | solution.py:169
  399.0 5.3 copy.55
  411.0 5.5 copy.58
  427.4 9.8 %convolution_convert_fusion.2 = bf16[1024,3072]{1,0:T(8,128)(2,1)} fusion(bf16[1024,3072]{0,1:T(8,128)(2,1)S(1)} %bitcast.127, bf16[1,1024,1024]{2,1,0:T(8,128)(2,1)S(1)} %copy-done, f32[1024]{0:T(1024)S(1)} %get-tuple-element.31, f32[1024]{0:T(1024)S(1)} %get-tuple-element.32, f32[1024]{0:T(1024)S(1)} %fusion.43, f32[1024]{0:T(1024)S(1)} %broadcast_multiply_fusion), kind=kOutput, calls=%fused_computation.21 | convolution fusion | flops 6451888128 | bytes 14696448 | tf_op jit(solution)/shard_map/te,tc->ec/dot_general | solution.py:375
  437.3 8.5 fusion.11
  445.8 14.9 %fusion.51 = (bf16[1024]{0:T(1024)(128)(2,1)S(1)}, f32[1024]{0:T(1024)S(1)}, f32[1024,1024]{1,0:T(8,128)S(1)}) fusion(f32[1024]{0:T(1024)S(1)} %get-tuple-element.32, f32[1024]{0:T(1024)S(1)} %broadcast_multiply_fusion, bf16[1,1024,1024]{2,1,0:T(8,128)(2,1)S(1)} %copy-done, f32[1024,1024]{1,0:T(8,128)} %fusion.11, ...), kind=kOutput, calls=%fused_computation.103 | convolution fusion | flops 8597272576 | bytes 27277312 | tf_op jit(solution)/shard_map/tf,ef->te/dot_general | solution.py:344
  465.5 11.1 %concatenate.51 = bf16[1024,3456]{1,0:T(8,128)(2,1)} concatenate(bf16[1024,3072]{1,0:T(8,128)(2,1)} %convolution_convert_fusion.2, bf16[1024,1]{1,0:T(8,128)(2,1)S(1)} %convert_element_type.289, bf16[1024,1]{1,0:T(8,128)(2,1)S(1)} %convert_element_type.290, bf16[1024,382]{1,0:T(8,128)(2,1)S(1)} %slice-done.2), dimensions={1} | concatenate | bytes 14155776 | tf_op jit(solution)/shard_map/concatenate | solution.py:218
  477.9 4.7 fusion.41
  485.6 18.3 %fusion.37 = bf16[1,1024,1024]{2,1,0:T(8,128)(2,1)} fusion(f32[1024,1024]{1,0:T(8,128)S(1)} %fusion.41, bf16[1,1024,1024]{2,1,0:T(8,128)(2,1)S(1)} %copy-done, f32[1024]{0:T(1024)S(1)} %copy-done.15, bf16[4096,1024]{1,0:T(8,128)(2,1)} %all-gather.11.cloned.1.call-done, f32[1024,4096]{1,0:T(8,128)} %fusion.9, f32[4096]{0:T(1024)S(1)} %reshape.475), kind=kOutput, calls=%fused_computation.54 | convolution fusion | flops 8637120512 | bytes 33574912 | tf_op jit(solution)/shard_map/dot_general | solution.py:310
  503.9 91.5 %reduce-scatter.4.cloned.1.call-done = bf16[32,3456]{1,0:T(8,128)(2,1)} async-done(((bf16[1024,3456]{1,0:T(8,128)(2,1)}), bf16[32,3456]{1,0:T(8,128)(2,1)}) %reduce-scatter.4.cloned.1.call-update) | async-done | bytes 221200 | tf_op jit(solution)/shard_map/reduce_scatter | solution.py:238
  599.4 136.9 %reduce-scatter.8.cloned.1.call-done = bf16[128,1152]{1,0:T(8,128)(2,1)} async-done(((bf16[4096,1152]{1,0:T(8,128)(2,1)}), bf16[128,1152]{1,0:T(8,128)(2,1)}) %reduce-scatter.8.cloned.1.call-update) | async-done | bytes 294928 | tf_op jit(solution)/shard_map/reduce_scatter | solution.py:238
  738.1 142.9 %reduce-scatter.6.cloned.1.call-done = bf16[32,4992]{1,0:T(8,128)(2,1)} async-done(((bf16[1024,4992]{1,0:T(8,128)(2,1)}), bf16[32,4992]{1,0:T(8,128)(2,1)}) %reduce-scatter.6.cloned.1.call-update) | async-done | bytes 319504 | tf_op jit(solution)/shard_map/reduce_scatter | solution.py:238
  (122 shorter events, 97.3 us)
Async XLA Ops:
  7.2 10.2 %copy-start = (bf16[1,1024,1024]{2,1,0:T(8,128)(2,1)S(1)}, bf16[1,1024,1024]{2,1,0:T(8,128)(2,1)}, u32[]{:S(2)}) copy-start(bf16[1,1024,1024]{2,1,0:T(8,128)(2,1)} %param.11) | copy-start | bytes 6291460
  7.2 78.2 %all-gather.7.cloned.1.call-start = ((), (), s32[]{:S(2)}) async-start(), calls=%async_computation.6 | async-start | bytes 6758400 | tf_op jit(solution)/shard_map/all_gather | solution.py:232
  12.1 189.7 %all-gather.9.cloned.1.call-start = ((), (), s32[]{:S(2)}) async-start(), calls=%async_computation.7 | async-start | bytes 10813440 | tf_op jit(solution)/shard_map/all_gather | solution.py:232
  13.9 238.3 %all-gather.11.cloned.1.call-start = ((), (), s32[]{:S(2)}) async-start(), calls=%async_computation.8 | async-start | bytes 8650752 | tf_op jit(solution)/shard_map/all_gather | solution.py:232
  14.7 580.8 %reduce-scatter.4.cloned.1.call-start = ((), (), s32[]{:S(2)}) async-start(), calls=%async_computation.3 | async-start | bytes 7299072 | tf_op jit(solution)/shard_map/reduce_scatter | solution.py:238
  18.0 73.1 %copy-start.13 = (f32[1024]{0:T(1024)}, f32[1024]{0:T(1024)S(1)}, u32[]{:S(2)}) copy-start(f32[1024]{0:T(1024)S(1)} %fusion.24) | copy-start | bytes 12292
  18.4 108.4 %copy-start.9 = (f32[1024,16]{0,1:T(8,128)}, f32[1024,16]{0,1:T(8,128)S(1)}, u32[]{:S(2)}) copy-start(f32[1024,16]{0,1:T(8,128)S(1)} %get-tuple-element.59) | copy-start | bytes 196612
  18.4 108.4 %copy-start.11 = (f32[1024,16]{0,1:T(8,128)}, f32[1024,16]{0,1:T(8,128)S(1)}, u32[]{:S(2)}) copy-start(f32[1024,16]{0,1:T(8,128)S(1)} %get-tuple-element.60) | copy-start | bytes 196612
  201.9 15.0 %copy-start.3 = (bf16[1,1024,1024]{2,1,0:T(8,128)(2,1)S(1)}, bf16[1,1024,1024]{2,1,0:T(8,128)(2,1)}, u32[]{:S(2)}) copy-start(bf16[1,1024,1024]{2,1,0:T(8,128)(2,1)} %param.21) | copy-start | bytes 6291460
  250.2 2.0 copy-start.8
  419.3 1.6 copy-start.7
  419.3 1.6 copy-start.10
  424.4 1.6 copy-start.6
  424.8 2.0 copy-start.5
  426.7 10.5 %slice-start = ((s8[6553600]{0:T(1024)(128)(4,1)}), s8[2359296]{0:T(1024)(128)(4,1)S(1)}, s32[]{:S(2)}) async-start(s8[6553600]{0:T(1024)(128)(4,1)} %bitcast.125), calls=%async_computation.9 | async-start | bytes 4718592
  427.4 9.8 %slice-start.1 = ((s8[6553600]{0:T(1024)(128)(4,1)}), s8[4194304]{0:T(1024)(128)(4,1)S(1)}, s32[]{:S(2)}) async-start(s8[6553600]{0:T(1024)(128)(4,1)} %bitcast.125), calls=%async_computation.10 | async-start | bytes 8388608
  445.8 14.9 %copy-start.14 = (f32[1024]{0:T(1024)S(1)}, f32[1024]{0:T(1024)}, u32[]{:S(2)}) copy-start(f32[1024]{0:T(1024)} %copy-done.13) | copy-start | bytes 12292
  460.7 2.1 copy-start.1
  460.7 4.8 slice-start.2
  476.7 259.7 %reduce-scatter.8.cloned.1.call-start = ((), (), s32[]{:S(2)}) async-start(), calls=%async_computation.5 | async-start | bytes 9732096 | tf_op jit(solution)/shard_map/reduce_scatter | solution.py:238
  477.3 403.8 %reduce-scatter.6.cloned.1.call-start = ((), (), s32[]{:S(2)}) async-start(), calls=%async_computation.4 | async-start | bytes 10543104 | tf_op jit(solution)/shard_map/reduce_scatter | solution.py:238
  477.9 4.7 copy-start.2
  477.9 4.7 copy-start.4
  482.6 3.0 copy-start.15
  (1 other events, 1.6 us)
Sparse Core Ops, SparseCore 0:
  12.2 73.0 all-gather.6
  88.8 84.6 all-gather.8
  176.5 75.6 all-gather.10
  476.8 118.5 reduce-scatter.3
  601.2 135.1 reduce-scatter.7
  742.2 138.8 reduce-scatter.5

commit v10 on v9

--- a/solution.py
+++ b/solution.py
@@ -316,15 +316,21 @@
         "tf,td->fd", active_low, upstream, preferred_element_type=jnp.float32
     )
     rows_all = normed_low.shape[1]
-    first = [contract_grad.astype(jnp.bfloat16)]
+    project_grad = jnp.einsum(
+        "te,td->ed", mixed_low, upstream, preferred_element_type=jnp.float32
+    ).astype(jnp.bfloat16)
+    ratio = contract_grad.shape[0] // rows_all
+    quarter = width // ratio
+    spare = -width % COLUMNS
+    project_rows = project_grad.reshape(ratio * rows_all, quarter)
+    project_rest = project_grad.reshape(rows_all, ratio, quarter)[:, :, : quarter - spare]
+    project_rest = project_rest.reshape(rows_all, -1)
+    first = [contract_grad.astype(jnp.bfloat16), project_rows[:, quarter - spare :]]
     first_packed = pad_columns(first)
     first_packed, upstream_back = lax.optimization_barrier((first_packed, upstream))
-    (contract_part,) = scatter_columns(first_packed, [block.shape[1] for block in first])
+    contract_part, project_tail = scatter_columns(first_packed, [block.shape[1] for block in first])
     contract_part = contract_part.reshape(-1, width)
     outer_grad = jnp.sum(upstream_back, axis=0, dtype=jnp.float32)
-    project_grad = jnp.einsum(
-        "te,td->ed", mixed_low, upstream_back, preferred_element_type=jnp.float32
-    )
     active_grad = jnp.einsum(
         "td,fd->tf", upstream_back, contract_full, preferred_element_type=jnp.float32
     )
@@ -335,7 +341,7 @@
     inner_grad = jnp.sum(hidden_grad, axis=0, dtype=jnp.float32)
     early = [
         expand_grad.astype(jnp.bfloat16),
-        project_grad.astype(jnp.bfloat16)[:, PROJECT_LATE:],
+        project_rest[:, PROJECT_LATE:],
         as_column(inner_grad.astype(jnp.bfloat16), rows_all),
         as_column(outer_grad.astype(jnp.bfloat16), rows_all),
     ]
@@ -386,14 +392,21 @@
         attend_grad.astype(jnp.bfloat16),
         as_column(gain_grad.astype(jnp.bfloat16), rows_all),
         as_column(shift_grad.astype(jnp.bfloat16), rows_all),
-        project_grad.astype(jnp.bfloat16)[:, :PROJECT_LATE],
+        project_rest[:, :PROJECT_LATE],
     ]
     attend_part, gain_part, shift_part, project_head = scatter_columns(
         pad_columns(late), [block.shape[1] for block in late]
     )
     gain_part = gain_part.reshape(-1)
     shift_part = shift_part.reshape(-1)
-    project_part = jnp.concatenate([project_head, project_part], axis=1)
+    rows_dev_out = project_head.shape[0]
+    project_front = jnp.concatenate([project_head, project_part], axis=1).reshape(
+        rows_dev_out, ratio, quarter - spare
+    )
+    project_back = project_tail.reshape(rows_dev_out, ratio, spare)
+    project_part = jnp.concatenate([project_front, project_back], axis=2).reshape(
+        rows_dev_out, width
+    )
     return (
         output,
         token_grad,

time: 899 us -> 910 us (1.012)
  local copies, waits for them, and re-layouts: 119 us -> 143 us
  waiting for transfers between devices: 440 us -> 425 us
    unnamed x36 -> x45, local copies, waits for them, and re-layouts: 4.05 us -> 23.7 us
    reduce_scatter x3, waiting for transfers between devices: 371 us -> 356 us  [scatter_columns(): summed = lax.psum_scatter(packed, ALL, scatter_dimension=0, tiled=True)]
    concatenate x4 -> x3, local copies, waits for them, and re-layouts: 36.4 us -> 28.2 us  [pad_columns(): return jnp.concatenate(blocks, axis=1)]
  transfers between devices with their start and end apart: 6 -> 6, of which waited for: 4 -> 4; matrix products, arithmetic and copies ran while one was open for 17% -> 19% of each run, Pallas kernels for 6% -> 6%
where the time goes in v10:
time: 910 us; the launch traced here: 905 us
  waiting for transfers between devices  425 us (47%)
  matrix products  152 us (17%)
  local copies, waits for them, and re-layouts  143 us (16%)
  Pallas kernels  133 us (15%)
  other arithmetic  37.5 us (4%)
  between operations  15.4 us (2%)
    reduce_scatter x3, waiting for transfers between devices, scatter_columns(): summed = lax.psum_scatter(packed, ALL, scatter_dimension=0, tiled=True)  356 us
    pallas_call x1, Pallas kernels, attention_backward(): pl.pallas_call(attention_backward_kernel, out_shape=(jax.ShapeDtypeStruct...  78.6 us
    all_gather x3, waiting for transfers between devices, gather_columns(): full = lax.all_gather(packed[None], ALL, axis=0, tiled=True)  67 us
    pallas_call x1, Pallas kernels, attention_forward(): pl.pallas_call(attention_forward_kernel, out_shape=(jax.ShapeDtypeStruct(...  54.1 us
    concatenate x3, local copies, waits for them, and re-layouts, pad_columns(): return jnp.concatenate(blocks, axis=1)  28.2 us
    dot_general x1, matrix products, body(): jnp.einsum('td,fd->tf', upstream_back, contract_full, preferred_element_t...  26.2 us
    unnamed x45, local copies, waits for them, and re-layouts  23.7 us
    dot_general x1, matrix products, body(): jnp.dot(active_low, contract_full, preferred_element_type=jnp.float32)  18.3 us
  transfers between devices with their start and end apart: 6, of which 4 were waited for; matrix products, arithmetic and copies ran while one was open for 19% of the time, Pallas kernels for 6%

profile of v10, /device:TPU:0, one launch (start us, length us, event | category | flops | bytes accessed | tf_op | source)
XLA Modules:
  0.0 905.2 jit_solution(2482997471825832187)
XLA Ops:
  18.4 66.9 %all-gather.7.cloned.1.call-done = bf16[1024,3200]{1,0:T(8,128)(2,1)} async-done(((bf16[32,3200]{1,0:T(8,128)(2,1)}), bf16[1024,3200]{1,0:T(8,128)(2,1)}) %all-gather.7.cloned.1.call-update) | async-done | bytes 6553616 | tf_op jit(solution)/shard_map/all_gather | solution.py:232
  85.3 5.9 slice_bitcast_fusion
  91.2 9.2 %copy.74 = bf16[3072,1024]{1,0:T(8,128)(2,1)} copy(bf16[3072,1024]{0,1:T(8,128)(2,1)} %slice_bitcast_fusion) | data formatting | bytes 12582912 | tf_op jit(solution)/shard_map/dot_general | solution.py:282
  102.6 12.9 %convolution_bitcast_fusion = f32[1,1024,3,16,64]{1,4,3,2,0:T(8,128)} fusion(bf16[3,16,64,1024]{3,2,1,0:T(8,128)(2,1)} %bitcast.135, bf16[1,1024,1024]{2,1,0:T(8,128)(2,1)S(1)} %copy-done, f32[1024]{0:T(1024)S(1)} %get-tuple-element.61, f32[1024]{0:T(1024)S(1)} %get-tuple-element.62, f32[1024]{0:T(1024)S(1)} %fusion.43, f32[1024]{0:T(1024)S(1)} %broadcast_multiply_fusion), kind=kOutput, calls=%fused_computation.34 | convolution fusion | flops 6448742400 | bytes 20987904 | tf_op jit(solution)/shard_map/dot_general | solution.py:282
  146.5 54.1 %shard_map.186 = (bf16[1024,1024]{1,0:T(8,128)(2,1)}, f32[16,1024,1]{2,1,0:T(8,128)}, f32[16,1024,1]{2,1,0:T(8,128)}) custom-call(s32[1]{0:T(128)S(6)} %copy.117.length_ref, bf16[1024,1024]{1,0:T(8,128)(2,1)} %copy.81.q_ref, bf16[1024,1024]{1,0:T(8,128)(2,1)} %copy.82.k_ref, bf16[1024,1024]{1,0:T(8,128)(2,1)} %copy.83.v_ref), custom_call_target="tpu_custom_call" | custom-call | flops 8589934592 | bytes 37748736 | tf_op jit(solution)/shard_map/pallas_call | solution.py:134
  200.6 6.1 convolution_convert_fusion.3
  224.9 15.1 %fusion.9 = f32[1024,4096]{1,0:T(8,128)} fusion(bf16[1024,5120]{1,0:T(8,128)(2,1)} %all-gather.9.cloned.1.call-done, bf16[1,1024,1024]{2,1,0:T(8,128)(2,1)S(1)} %copy-done, f32[1024]{0:T(1024)S(1)} %get-tuple-element.61, f32[1024]{0:T(1024)S(1)} %get-tuple-element.62, f32[1024]{0:T(1024)S(1)} %fusion.43, f32[1024]{0:T(1024)S(1)} %broadcast_multiply_fusion), kind=kOutput, calls=%fused_computation.16 | convolution fusion | flops 8596226048 | bytes 27279360 | tf_op jit(solution)/shard_map/dot_general | solution.py:302
  240.0 13.6 %convolution_convert_fusion.1 = bf16[4096,1024]{0,1:T(8,128)(2,1)S(1)} fusion(bf16[1,1024,1024]{2,1,0:T(8,128)(2,1)S(1)} %copy-done.3, f32[1024,4096]{1,0:T(8,128)} %fusion.9, f32[4096]{0:T(1024)S(1)} %reshape.505), kind=kOutput, calls=%fused_computation.13 | convolution fusion | flops 8636071936 | bytes 27279360 | tf_op jit(solution)/shard_map/tf,td->fd/dot_general | solution.py:315
  253.6 7.7 pad_maximum_fusion
  263.2 26.2 %fusion.53 = (bf16[4096]{0:T(1024)(128)(2,1)S(1)}, bf16[1024,4096]{1,0:T(8,128)(2,1)}) fusion(f32[1024,4096]{1,0:T(8,128)} %fusion.9, f32[4096]{0:T(1024)S(1)} %reshape.505, bf16[1024,1024]{1,0:T(8,128)(2,1)} %bitcast.120, bf16[4096,1024]{1,0:T(8,128)(2,1)} %all-gather.11.cloned.1.call-done), kind=kOutput, calls=%fused_computation.106 | convolution fusion | flops 8682205184 | bytes 35676160 | tf_op jit(solution)/shard_map/td,fd->tf/dot_general | solution.py:334
  289.5 15.3 %convolution_convert_fusion = bf16[1024,4096]{1,0:T(8,128)(2,1)} fusion(bf16[1024,4096]{1,0:T(8,128)(2,1)} %get-tuple-element.70, bf16[1,1024,1024]{2,1,0:T(8,128)(2,1)S(1)} %copy-done, f32[1024]{0:T(1024)S(1)} %get-tuple-element.61, f32[1024]{0:T(1024)S(1)} %get-tuple-element.62, f32[1024]{0:T(1024)S(1)} %fusion.43, f32[1024]{0:T(1024)S(1)} %broadcast_multiply_fusion), kind=kOutput, calls=%fused_computation.12 | convolution fusion | flops 8600420352 | bytes 18890752 | tf_op jit(solution)/shard_map/te,tf->ef/dot_general | solution.py:338
  307.0 15.4 %concatenate.52 = bf16[1024,4608]{1,0:T(8,128)(2,1)} concatenate(bf16[1024,4096]{1,0:T(8,128)(2,1)} %convolution_convert_fusion, bf16[1024,130]{1,0:T(8,128)(2,1)S(1)} %copy-done.9, bf16[1024,4]{1,0:T(8,128)(2,1)} %reshape.483, bf16[1024,1]{1,0:T(8,128)(2,1)} %reshape.524, bf16[1024,377]{1,0:T(8,128)(2,1)S(1)} %broadcast_in_dim.18), dimensions={1} | concatenate | bytes 18874368 | tf_op jit(solution)/shard_map/concatenate | solution.py:218
  322.4 5.9 convert_bitcast_fusion.1
  328.3 78.6 %shard_map.187 = (f32[1024,1024]{1,0:T(8,128)}, f32[1024,1024]{1,0:T(8,128)}, f32[1024,1024]{1,0:T(8,128)}) custom-call(s32[1]{0:T(128)S(6)} %copy.117.length_ref, bf16[1024,1024]{1,0:T(8,128)(2,1)} %copy.81.q_ref, bf16[1024,1024]{1,0:T(8,128)(2,1)} %copy.82.k_ref, bf16[1024,1024]{1,0:T(8,128)(2,1)} %copy.83.v_ref, bf16[1024,1024]{1,0:T(8,128)(2,1)} %bitcast.147, ...), custom_call_target="tpu_custom_call" | custom-call | flops 21474836480 | bytes 54525952 | tf_op jit(solution)/shard_map/pallas_call | solution.py:169
  423.4 5.6 copy.95
  439.9 9.7 %convolution_convert_fusion.2 = bf16[1024,3072]{1,0:T(8,128)(2,1)} fusion(bf16[1024,3072]{0,1:T(8,128)(2,1)S(1)} %bitcast.133, bf16[1,1024,1024]{2,1,0:T(8,128)(2,1)S(1)} %copy-done, f32[1024]{0:T(1024)S(1)} %get-tuple-element.61, f32[1024]{0:T(1024)S(1)} %get-tuple-element.62, f32[1024]{0:T(1024)S(1)} %fusion.43, f32[1024]{0:T(1024)S(1)} %broadcast_multiply_fusion), kind=kOutput, calls=%fused_computation.22 | convolution fusion | flops 6451888128 | bytes 14696448 | tf_op jit(solution)/shard_map/te,tc->ec/dot_general | solution.py:381
  449.7 8.7 fusion.11
  458.4 14.9 %fusion.52 = (bf16[1024]{0:T(1024)(128)(2,1)S(1)}, f32[1024]{0:T(1024)S(1)}, f32[1024,1024]{1,0:T(8,128)S(1)}) fusion(f32[1024]{0:T(1024)S(1)} %get-tuple-element.62, f32[1024]{0:T(1024)S(1)} %broadcast_multiply_fusion, bf16[1,1024,1024]{2,1,0:T(8,128)(2,1)S(1)} %copy-done, f32[1024,1024]{1,0:T(8,128)} %fusion.11, ...), kind=kOutput, calls=%fused_computation.105 | convolution fusion | flops 8597272576 | bytes 27277312 | tf_op jit(solution)/shard_map/tf,ef->te/dot_general | solution.py:350
  478.1 11.2 %concatenate.53 = bf16[1024,3456]{1,0:T(8,128)(2,1)} concatenate(bf16[1024,3072]{1,0:T(8,128)(2,1)} %convolution_convert_fusion.2, bf16[1024,1]{1,0:T(8,128)(2,1)S(1)} %convert_element_type.289, bf16[1024,1]{1,0:T(8,128)(2,1)S(1)} %convert_element_type.290, bf16[1024,382]{1,0:T(8,128)(2,1)S(1)} %copy-done.8), dimensions={1} | concatenate | bytes 14155776 | tf_op jit(solution)/shard_map/concatenate | solution.py:218
  489.9 13.1 %copy.108 = bf16[4096,1152]{1,0:T(8,128)(2,1)} copy(bf16[4096,1152]{0,1:T(8,128)(2,1)} %pad_maximum_fusion) | data formatting | bytes 18874368
  510.7 18.3 %fusion.37 = bf16[1,1024,1024]{2,1,0:T(8,128)(2,1)} fusion(f32[1024,1024]{1,0:T(8,128)S(1)} %fusion.41, bf16[1,1024,1024]{2,1,0:T(8,128)(2,1)S(1)} %copy-done, f32[1024]{0:T(1024)S(1)} %copy-done.16, bf16[4096,1024]{1,0:T(8,128)(2,1)} %all-gather.11.cloned.1.call-done, f32[1024,4096]{1,0:T(8,128)} %fusion.9, f32[4096]{0:T(1024)S(1)} %reshape.505), kind=kOutput, calls=%fused_computation.55 | convolution fusion | flops 8637120512 | bytes 33574912 | tf_op jit(solution)/shard_map/dot_general | solution.py:310
  529.0 79.3 %reduce-scatter.6.cloned.1.call-done = bf16[32,3456]{1,0:T(8,128)(2,1)} async-done(((bf16[1024,3456]{1,0:T(8,128)(2,1)}), bf16[32,3456]{1,0:T(8,128)(2,1)}) %reduce-scatter.6.cloned.1.call-update) | async-done | bytes 221200 | tf_op jit(solution)/shard_map/reduce_scatter | solution.py:238
  612.2 136.9 %reduce-scatter.8.cloned.1.call-done = bf16[32,4608]{1,0:T(8,128)(2,1)} async-done(((bf16[1024,4608]{1,0:T(8,128)(2,1)}), bf16[32,4608]{1,0:T(8,128)(2,1)}) %reduce-scatter.8.cloned.1.call-update) | async-done | bytes 294928 | tf_op jit(solution)/shard_map/reduce_scatter | solution.py:238
  750.0 140.1 %reduce-scatter.10.cloned.1.call-done = bf16[128,1152]{1,0:T(8,128)(2,1)} async-done(((bf16[4096,1152]{1,0:T(8,128)(2,1)}), bf16[128,1152]{1,0:T(8,128)(2,1)}) %reduce-scatter.10.cloned.1.call-update) | async-done | bytes 294928 | tf_op jit(solution)/shard_map/reduce_scatter | solution.py:238
  (137 shorter events, 119.2 us)
Async XLA Ops:
  7.2 10.2 %copy-start = (bf16[1,1024,1024]{2,1,0:T(8,128)(2,1)S(1)}, bf16[1,1024,1024]{2,1,0:T(8,128)(2,1)}, u32[]{:S(2)}) copy-start(bf16[1,1024,1024]{2,1,0:T(8,128)(2,1)} %param.11) | copy-start | bytes 6291460
  7.2 78.2 %all-gather.7.cloned.1.call-start = ((), (), s32[]{:S(2)}) async-start(), calls=%async_computation.5 | async-start | bytes 6758400 | tf_op jit(solution)/shard_map/all_gather | solution.py:232
  12.1 212.8 %all-gather.9.cloned.1.call-start = ((), (), s32[]{:S(2)}) async-start(), calls=%async_computation.6 | async-start | bytes 10813440 | tf_op jit(solution)/shard_map/all_gather | solution.py:232
  13.9 249.3 %all-gather.11.cloned.1.call-start = ((), (), s32[]{:S(2)}) async-start(), calls=%async_computation.7 | async-start | bytes 8650752 | tf_op jit(solution)/shard_map/all_gather | solution.py:232
  14.7 593.6 %reduce-scatter.6.cloned.1.call-start = ((), (), s32[]{:S(2)}) async-start(), calls=%async_computation.3 | async-start | bytes 7299072 | tf_op jit(solution)/shard_map/reduce_scatter | solution.py:238
  18.0 73.2 %copy-start.14 = (f32[1024]{0:T(1024)}, f32[1024]{0:T(1024)S(1)}, u32[]{:S(2)}) copy-start(f32[1024]{0:T(1024)S(1)} %fusion.24) | copy-start | bytes 12292
  18.4 108.5 %copy-start.10 = (f32[1024,16]{0,1:T(8,128)}, f32[1024,16]{0,1:T(8,128)S(1)}, u32[]{:S(2)}) copy-start(f32[1024,16]{0,1:T(8,128)S(1)} %get-tuple-element.89) | copy-start | bytes 196612
  18.4 108.5 %copy-start.12 = (f32[1024,16]{0,1:T(8,128)}, f32[1024,16]{0,1:T(8,128)S(1)}, u32[]{:S(2)}) copy-start(f32[1024,16]{0,1:T(8,128)S(1)} %get-tuple-element.90) | copy-start | bytes 196612
  224.9 15.1 %copy-start.3 = (bf16[1,1024,1024]{2,1,0:T(8,128)(2,1)S(1)}, bf16[1,1024,1024]{2,1,0:T(8,128)(2,1)}, u32[]{:S(2)}) copy-start(bf16[1,1024,1024]{2,1,0:T(8,128)(2,1)} %param.21) | copy-start | bytes 6291460
  289.5 17.5 %copy-start.9 = (bf16[1024,130]{1,0:T(8,128)(2,1)S(1)}, bf16[1024,130]{1,0:T(8,128)(2,1)}, u32[]{:S(2)}) copy-start(bf16[1024,130]{1,0:T(8,128)(2,1)} %copy.113) | copy-start | bytes 798724
  431.8 1.6 copy-start.7
  431.8 1.6 copy-start.11
  436.9 1.6 copy-start.6
  437.3 2.0 copy-start.5
  439.2 10.4 %slice-start = ((s8[6553600]{0:T(1024)(128)(4,1)}), s8[2359296]{0:T(1024)(128)(4,1)S(1)}, s32[]{:S(2)}) async-start(s8[6553600]{0:T(1024)(128)(4,1)} %bitcast.131), calls=%async_computation.9 | async-start | bytes 4718592
  439.9 9.8 %slice-start.1 = ((s8[6553600]{0:T(1024)(128)(4,1)}), s8[4194304]{0:T(1024)(128)(4,1)S(1)}, s32[]{:S(2)}) async-start(s8[6553600]{0:T(1024)(128)(4,1)} %bitcast.131), calls=%async_computation.10 | async-start | bytes 8388608
  458.4 14.9 %copy-start.15 = (f32[1024]{0:T(1024)S(1)}, f32[1024]{0:T(1024)}, u32[]{:S(2)}) copy-start(f32[1024]{0:T(1024)} %copy-done.14) | copy-start | bytes 12292
  473.2 2.0 copy-start.1
  473.3 4.8 copy-start.8
  489.3 259.9 %reduce-scatter.8.cloned.1.call-start = ((), (), s32[]{:S(2)}) async-start(), calls=%async_computation.4 | async-start | bytes 9732096 | tf_op jit(solution)/shard_map/reduce_scatter | solution.py:238
  489.8 400.2 %reduce-scatter.10.cloned.1.call-start = ((), (), s32[]{:S(2)}) async-start(), calls=%async_computation.8 | async-start | bytes 9732096 | tf_op jit(solution)/shard_map/reduce_scatter | solution.py:238
  503.0 4.9 copy-start.2
  503.0 4.9 copy-start.4
  507.9 2.8 copy-start.16
  (1 other events, 1.6 us)
Sparse Core Ops, SparseCore 0:
  12.2 73.0 all-gather.6
  88.8 84.6 all-gather.8
  176.5 75.6 all-gather.10
  489.4 118.8 reduce-scatter.5
  614.0 135.1 reduce-scatter.7
  754.9 135.1 reduce-scatter.9

commit v11 on v9

--- a/solution.py
+++ b/solution.py
@@ -272,8 +272,9 @@
     shift_full = shift_full.reshape(-1)
     inner_full = inner_full.reshape(-1)
     outer_full = outer_full.reshape(-1)
-    expand_full, project_full = gather_columns([expand_weight, project_weight])
-    (contract_full,) = gather_columns([contract_weight])
+    expand_full, project_full, contract_raw = gather_columns(
+        [expand_weight, project_weight, contract_weight.reshape(rows_dev, -1)]
+    )
     rows = tokens.reshape(positions, width).astype(jnp.float32)
     normed, norm_pull = jax.vjp(
         layer_norm, rows, gain_full.astype(jnp.float32), shift_full.astype(jnp.float32)
@@ -304,6 +305,17 @@
     ) + inner_full.astype(jnp.float32)
     active, gelu_pull = jax.vjp(gelu_tanh, hidden)
     active_low = active.astype(jnp.bfloat16)
+    upstream = cotangent.reshape(positions, width)
+    contract_grad = jnp.einsum(
+        "tf,td->fd", active_low, upstream, preferred_element_type=jnp.float32
+    )
+    rows_all = normed_low.shape[1]
+    first = [contract_grad.astype(jnp.bfloat16)]
+    first_packed = pad_columns(first)
+    first_packed, upstream_back, contract_raw = lax.optimization_barrier(
+        (first_packed, upstream, contract_raw)
+    )
+    contract_full = contract_raw.reshape(-1, width)
     result = rows + jnp.dot(mixed_low, project_full, preferred_element_type=jnp.float32)
     result = (
         result
@@ -311,14 +323,6 @@
         + outer_full.astype(jnp.float32)
     )
     output = result.astype(jnp.bfloat16).reshape(tokens.shape)
-    upstream = cotangent.reshape(positions, width)
-    contract_grad = jnp.einsum(
-        "tf,td->fd", active_low, upstream, preferred_element_type=jnp.float32
-    )
-    rows_all = normed_low.shape[1]
-    first = [contract_grad.astype(jnp.bfloat16)]
-    first_packed = pad_columns(first)
-    first_packed, upstream_back = lax.optimization_barrier((first_packed, upstream))
     (contract_part,) = scatter_columns(first_packed, [block.shape[1] for block in first])
     contract_part = contract_part.reshape(-1, width)
     outer_grad = jnp.sum(upstream_back, axis=0, dtype=jnp.float32)

time: 899 us -> 929 us (1.033)
  local copies, waits for them, and re-layouts: 119 us -> 142 us
    reshape x0 -> x2, local copies, waits for them, and re-layouts: none -> 15.1 us  [the longest x1 13.9 us: body(): contract_full = contract_raw.reshape(-1, width)]
    all_gather x3 -> x2, waiting for transfers between devices: 66.9 us -> 76.5 us  [gather_columns(): full = lax.all_gather(packed[None], ALL, axis=0, tiled=True)]
  transfers between devices with their start and end apart: 6 -> 5, of which waited for: 4 -> 5; matrix products, arithmetic and copies ran while one was open for 17% -> 11% of each run, Pallas kernels for 6% -> 6%
where the time goes in v11:
time: 929 us; the launch traced here: 924 us
  waiting for transfers between devices  448 us (48%)
  matrix products  155 us (17%)
  local copies, waits for them, and re-layouts  142 us (15%)
  Pallas kernels  133 us (14%)
  other arithmetic  31.1 us (3%)
  between operations  15.2 us (2%)
    reduce_scatter x3, waiting for transfers between devices, scatter_columns(): summed = lax.psum_scatter(packed, ALL, scatter_dimension=0, tiled=True)  371 us
    pallas_call x1, Pallas kernels, attention_backward(): pl.pallas_call(attention_backward_kernel, out_shape=(jax.ShapeDtypeStruct...  78.7 us
    all_gather x2, waiting for transfers between devices, gather_columns(): full = lax.all_gather(packed[None], ALL, axis=0, tiled=True)  76.5 us
    pallas_call x1, Pallas kernels, attention_forward(): pl.pallas_call(attention_forward_kernel, out_shape=(jax.ShapeDtypeStruct(...  54.1 us
    concatenate x4, local copies, waits for them, and re-layouts, pad_columns(): return jnp.concatenate(blocks, axis=1)  36.4 us
    dot_general x1, matrix products, body(): jnp.einsum('td,fd->tf', upstream_back, contract_full, preferred_element_t...  25.9 us
    dot_general x1, matrix products, body(): jnp.einsum('tf,td->fd', active_low, upstream, preferred_element_type=jnp....  18.6 us
  transfers between devices with their start and end apart: 5, of which 5 were waited for; matrix products, arithmetic and copies ran while one was open for 11% of the time, Pallas kernels for 6%

profile of v11, /device:TPU:0, one launch (start us, length us, event | category | flops | bytes accessed | tf_op | source)
XLA Modules:
  0.0 924.0 jit_solution(7736398981196515339)
XLA Ops:
  17.3 68.0 %all-gather.5.cloned.1.call-done = bf16[1024,3200]{1,0:T(8,128)(2,1)} async-done(((bf16[32,3200]{1,0:T(8,128)(2,1)}), bf16[1024,3200]{1,0:T(8,128)(2,1)}) %all-gather.5.cloned.1.call-update) | async-done | bytes 6553616 | tf_op jit(solution)/shard_map/all_gather | solution.py:232
  85.3 5.8 slice_bitcast_fusion
  91.2 8.9 copy.39
  102.3 13.0 %convolution_bitcast_fusion = f32[1,1024,3,16,64]{1,4,3,2,0:T(8,128)} fusion(bf16[3,16,64,1024]{3,2,1,0:T(8,128)(2,1)} %bitcast.129, bf16[1,1024,1024]{2,1,0:T(8,128)(2,1)S(1)} %copy-done, f32[1024]{0:T(1024)S(1)} %get-tuple-element.33, f32[1024]{0:T(1024)S(1)} %get-tuple-element.34, f32[1024]{0:T(1024)S(1)} %fusion.43, f32[1024]{0:T(1024)S(1)} %broadcast_multiply_fusion), kind=kOutput, calls=%fused_computation.33 | convolution fusion | flops 6448742400 | bytes 20987904 | tf_op jit(solution)/shard_map/dot_general | solution.py:283
  148.2 54.1 %shard_map.186 = (bf16[1024,1024]{1,0:T(8,128)(2,1)}, f32[16,1024,1]{2,1,0:T(8,128)}, f32[16,1024,1]{2,1,0:T(8,128)}) custom-call(s32[1]{0:T(128)S(6)} %copy.71.length_ref, bf16[1024,1024]{1,0:T(8,128)(2,1)} %copy.46.q_ref, bf16[1024,1024]{1,0:T(8,128)(2,1)} %copy.47.k_ref, bf16[1024,1024]{1,0:T(8,128)(2,1)} %copy.48.v_ref), custom_call_target="tpu_custom_call" | custom-call | flops 8589934592 | bytes 37748736 | tf_op jit(solution)/shard_map/pallas_call | solution.py:134
  202.3 8.5 all-gather.7.cloned.1.call-done
  210.8 15.1 %fusion.9 = f32[1024,4096]{1,0:T(8,128)} fusion(bf16[1024,9216]{1,0:T(8,128)(2,1)} %all-gather.7.cloned.1.call-done, bf16[1,1024,1024]{2,1,0:T(8,128)(2,1)S(1)} %copy-done, f32[1024]{0:T(1024)S(1)} %get-tuple-element.33, f32[1024]{0:T(1024)S(1)} %get-tuple-element.34, f32[1024]{0:T(1024)S(1)} %fusion.43, f32[1024]{0:T(1024)S(1)} %broadcast_multiply_fusion), kind=kOutput, calls=%fused_computation.15 | convolution fusion | flops 8596226048 | bytes 27279360 | tf_op jit(solution)/shard_map/dot_general | solution.py:303
  225.9 18.6 %convolution_convert_fusion.1 = bf16[4096,1024]{1,0:T(8,128)(2,1)} fusion(bf16[1,1024,1024]{2,1,0:T(8,128)(2,1)S(1)} %copy-done.3, f32[1024,4096]{1,0:T(8,128)} %fusion.9, f32[4096]{0:T(1024)S(1)} %reshape.479), kind=kOutput, calls=%fused_computation.12 | convolution fusion | flops 8636071936 | bytes 27279360 | tf_op jit(solution)/shard_map/tf,td->fd/dot_general | solution.py:309
  244.5 8.1 concatenate.49
  252.6 7.7 slice.140
  268.9 13.9 %reshape.459 = bf16[4096,1024]{1,0:T(8,128)(2,1)} reshape(bf16[1024,4096]{1,0:T(8,128)(2,1)} %slice.140) | data formatting | bytes 16777216 | tf_op jit(solution)/shard_map/reshape | solution.py:318
  282.8 25.9 %fusion.52 = (bf16[4096]{0:T(1024)(128)(2,1)S(1)}, bf16[1024,4096]{1,0:T(8,128)(2,1)}) fusion(f32[1024,4096]{1,0:T(8,128)} %fusion.9, f32[4096]{0:T(1024)S(1)} %reshape.479, bf16[1024,1024]{1,0:T(8,128)(2,1)} %bitcast.114, bf16[4096,1024]{1,0:T(8,128)(2,1)} %reshape.459), kind=kOutput, calls=%fused_computation.104 | convolution fusion | flops 8682205184 | bytes 35676160 | tf_op jit(solution)/shard_map/td,fd->tf/dot_general | solution.py:332
  308.8 15.4 %convolution_convert_fusion = bf16[1024,4096]{1,0:T(8,128)(2,1)} fusion(bf16[1024,4096]{1,0:T(8,128)(2,1)} %get-tuple-element.42, bf16[1,1024,1024]{2,1,0:T(8,128)(2,1)S(1)} %copy-done, f32[1024]{0:T(1024)S(1)} %get-tuple-element.33, f32[1024]{0:T(1024)S(1)} %get-tuple-element.34, f32[1024]{0:T(1024)S(1)} %fusion.43, f32[1024]{0:T(1024)S(1)} %broadcast_multiply_fusion), kind=kOutput, calls=%fused_computation.11 | convolution fusion | flops 8600420352 | bytes 18890752 | tf_op jit(solution)/shard_map/te,tf->ef/dot_general | solution.py:336
  325.0 15.6 %concatenate.50 = bf16[1024,4992]{1,0:T(8,128)(2,1)} concatenate(bf16[1024,4096]{1,0:T(8,128)(2,1)} %convolution_convert_fusion, bf16[1024,642]{1,0:T(8,128)(2,1)} %slice.142, bf16[1024,4]{1,0:T(8,128)(2,1)S(1)} %reshape.461, bf16[1024,1]{1,0:T(8,128)(2,1)S(1)} %reshape.494, bf16[1024,249]{1,0:T(8,128)(2,1)S(1)} %broadcast_in_dim.15), dimensions={1} | concatenate | bytes 20447232 | tf_op jit(solution)/shard_map/concatenate | solution.py:218
  340.6 5.9 convert_bitcast_fusion.1
  346.5 78.7 %shard_map.187 = (f32[1024,1024]{1,0:T(8,128)}, f32[1024,1024]{1,0:T(8,128)}, f32[1024,1024]{1,0:T(8,128)}) custom-call(s32[1]{0:T(128)S(6)} %copy.71.length_ref, bf16[1024,1024]{1,0:T(8,128)(2,1)} %copy.46.q_ref, bf16[1024,1024]{1,0:T(8,128)(2,1)} %copy.47.k_ref, bf16[1024,1024]{1,0:T(8,128)(2,1)} %copy.48.v_ref, bf16[1024,1024]{1,0:T(8,128)(2,1)} %bitcast.135, ...), custom_call_target="tpu_custom_call" | custom-call | flops 21474836480 | bytes 54525952 | tf_op jit(solution)/shard_map/pallas_call | solution.py:169
  458.2 9.8 %convolution_convert_fusion.2 = bf16[1024,3072]{1,0:T(8,128)(2,1)} fusion(bf16[1024,3072]{0,1:T(8,128)(2,1)S(1)} %bitcast.127, bf16[1,1024,1024]{2,1,0:T(8,128)(2,1)S(1)} %copy-done, f32[1024]{0:T(1024)S(1)} %get-tuple-element.33, f32[1024]{0:T(1024)S(1)} %get-tuple-element.34, f32[1024]{0:T(1024)S(1)} %fusion.43, f32[1024]{0:T(1024)S(1)} %broadcast_multiply_fusion), kind=kOutput, calls=%fused_computation.21 | convolution fusion | flops 6451888128 | bytes 14696448 | tf_op jit(solution)/shard_map/te,tc->ec/dot_general | solution.py:379
  468.0 8.5 fusion.11
  476.5 15.0 %fusion.51 = (bf16[1024]{0:T(1024)(128)(2,1)S(1)}, f32[1024]{0:T(1024)S(1)}, f32[1024,1024]{1,0:T(8,128)S(1)}) fusion(f32[1024]{0:T(1024)S(1)} %get-tuple-element.34, f32[1024]{0:T(1024)S(1)} %broadcast_multiply_fusion, bf16[1,1024,1024]{2,1,0:T(8,128)(2,1)S(1)} %copy-done, f32[1024,1024]{1,0:T(8,128)} %fusion.11, ...), kind=kOutput, calls=%fused_computation.103 | convolution fusion | flops 8597272576 | bytes 27277312 | tf_op jit(solution)/shard_map/tf,ef->te/dot_general | solution.py:348
  496.4 11.1 %concatenate.51 = bf16[1024,3456]{1,0:T(8,128)(2,1)} concatenate(bf16[1024,3072]{1,0:T(8,128)(2,1)} %convolution_convert_fusion.2, bf16[1024,1]{1,0:T(8,128)(2,1)S(1)} %convert_element_type.289, bf16[1024,1]{1,0:T(8,128)(2,1)S(1)} %convert_element_type.290, bf16[1024,382]{1,0:T(8,128)(2,1)S(1)} %slice-done.2), dimensions={1} | concatenate | bytes 14155776 | tf_op jit(solution)/shard_map/concatenate | solution.py:218
  516.5 18.3 %fusion.37 = bf16[1,1024,1024]{2,1,0:T(8,128)(2,1)} fusion(f32[1024,1024]{1,0:T(8,128)S(1)} %fusion.41, bf16[1,1024,1024]{2,1,0:T(8,128)(2,1)S(1)} %copy-done, f32[1024]{0:T(1024)S(1)} %copy-done.15, bf16[4096,1024]{1,0:T(8,128)(2,1)} %reshape.459, f32[1024,4096]{1,0:T(8,128)} %fusion.9, f32[4096]{0:T(1024)S(1)} %reshape.479), kind=kOutput, calls=%fused_computation.54 | convolution fusion | flops 8637120512 | bytes 33574912 | tf_op jit(solution)/shard_map/dot_general | solution.py:322
  534.8 90.8 %reduce-scatter.4.cloned.1.call-done = bf16[32,3456]{1,0:T(8,128)(2,1)} async-done(((bf16[1024,3456]{1,0:T(8,128)(2,1)}), bf16[32,3456]{1,0:T(8,128)(2,1)}) %reduce-scatter.4.cloned.1.call-update) | async-done | bytes 221200 | tf_op jit(solution)/shard_map/reduce_scatter | solution.py:238
  629.5 136.9 %reduce-scatter.8.cloned.1.call-done = bf16[128,1152]{1,0:T(8,128)(2,1)} async-done(((bf16[4096,1152]{1,0:T(8,128)(2,1)}), bf16[128,1152]{1,0:T(8,128)(2,1)}) %reduce-scatter.8.cloned.1.call-update) | async-done | bytes 294928 | tf_op jit(solution)/shard_map/reduce_scatter | solution.py:238
  768.2 142.9 %reduce-scatter.6.cloned.1.call-done = bf16[32,4992]{1,0:T(8,128)(2,1)} async-done(((bf16[1024,4992]{1,0:T(8,128)(2,1)}), bf16[32,4992]{1,0:T(8,128)(2,1)}) %reduce-scatter.6.cloned.1.call-update) | async-done | bytes 319504 | tf_op jit(solution)/shard_map/reduce_scatter | solution.py:238
  (122 shorter events, 112.3 us)
Async XLA Ops:
  7.2 8.7 copy-start
  7.2 78.1 %all-gather.5.cloned.1.call-start = ((), (), s32[]{:S(2)}) async-start(), calls=%async_computation.6 | async-start | bytes 6758400 | tf_op jit(solution)/shard_map/all_gather | solution.py:232
  12.1 198.7 %all-gather.7.cloned.1.call-start = ((), (), s32[]{:S(2)}) async-start(), calls=%async_computation.7 | async-start | bytes 19464192 | tf_op jit(solution)/shard_map/all_gather | solution.py:232
  15.2 610.4 %reduce-scatter.4.cloned.1.call-start = ((), (), s32[]{:S(2)}) async-start(), calls=%async_computation.3 | async-start | bytes 7299072 | tf_op jit(solution)/shard_map/reduce_scatter | solution.py:238
  16.9 74.2 %copy-start.13 = (f32[1024]{0:T(1024)}, f32[1024]{0:T(1024)S(1)}, u32[]{:S(2)}) copy-start(f32[1024]{0:T(1024)S(1)} %fusion.24) | copy-start | bytes 12292
  17.3 109.8 %copy-start.9 = (f32[1024,16]{0,1:T(8,128)}, f32[1024,16]{0,1:T(8,128)S(1)}, u32[]{:S(2)}) copy-start(f32[1024,16]{0,1:T(8,128)S(1)} %get-tuple-element.61) | copy-start | bytes 196612
  17.3 109.8 %copy-start.11 = (f32[1024,16]{0,1:T(8,128)}, f32[1024,16]{0,1:T(8,128)S(1)}, u32[]{:S(2)}) copy-start(f32[1024,16]{0,1:T(8,128)S(1)} %get-tuple-element.62) | copy-start | bytes 196612
  210.8 15.1 %copy-start.3 = (bf16[1,1024,1024]{2,1,0:T(8,128)(2,1)S(1)}, bf16[1,1024,1024]{2,1,0:T(8,128)(2,1)}, u32[]{:S(2)}) copy-start(bf16[1,1024,1024]{2,1,0:T(8,128)(2,1)} %param.21) | copy-start | bytes 6291460
  266.9 2.0 copy-start.8
  450.1 1.6 copy-start.7
  450.1 1.6 copy-start.10
  450.1 1.6 copy-start.12
  455.2 1.6 copy-start.6
  455.6 2.0 copy-start.5
  457.5 10.4 %slice-start = ((s8[6553600]{0:T(1024)(128)(4,1)}), s8[2359296]{0:T(1024)(128)(4,1)S(1)}, s32[]{:S(2)}) async-start(s8[6553600]{0:T(1024)(128)(4,1)} %bitcast.125), calls=%async_computation.8 | async-start | bytes 4718592
  458.2 9.8 %slice-start.1 = ((s8[6553600]{0:T(1024)(128)(4,1)}), s8[4194304]{0:T(1024)(128)(4,1)S(1)}, s32[]{:S(2)}) async-start(s8[6553600]{0:T(1024)(128)(4,1)} %bitcast.125), calls=%async_computation.9 | async-start | bytes 8388608
  476.5 15.0 %copy-start.14 = (f32[1024]{0:T(1024)S(1)}, f32[1024]{0:T(1024)}, u32[]{:S(2)}) copy-start(f32[1024]{0:T(1024)} %copy-done.13) | copy-start | bytes 12292
  491.4 2.1 copy-start.1
  491.5 4.9 slice-start.2
  507.5 258.9 %reduce-scatter.8.cloned.1.call-start = ((), (), s32[]{:S(2)}) async-start(), calls=%async_computation.5 | async-start | bytes 9732096 | tf_op jit(solution)/shard_map/reduce_scatter | solution.py:238
  508.1 403.0 %reduce-scatter.6.cloned.1.call-start = ((), (), s32[]{:S(2)}) async-start(), calls=%async_computation.4 | async-start | bytes 10543104 | tf_op jit(solution)/shard_map/reduce_scatter | solution.py:238
  508.7 4.7 copy-start.2
  508.7 4.7 copy-start.4
  513.5 3.0 copy-start.15
Sparse Core Ops, SparseCore 0:
  12.2 73.0 all-gather.4
  88.3 122.4 all-gather.6
  507.7 117.8 reduce-scatter.3
  631.3 135.1 reduce-scatter.7
  772.3 138.7 reduce-scatter.5
